TPU v7x, 32 devices: a whole 2x2x4 slice. The times are simulated.
32 devices in a mesh: groups: 2 (over x), dom: 16 (over z, y, core).
Axes of the slice: x: 2, y: 2, z: 4, core: 2. Of those that a mesh axis runs over, the one named last changes fastest.
Arguments:
- image: bfloat16 [32, 64, 128, 128], P(('groups', 'dom')), parts along dimension 0, may hold values from -16 to 16
- adjoint_data: bfloat16 [32, 64, 128, 128], P(('groups', 'dom')), parts along dimension 0, may hold values from -8 to 8
- coil_maps: bfloat16 [32, 16, 128, 128], P(('groups', 'dom')), parts along dimension 0, may hold values from -1 to 1
- spoke_counts: int32 [32, 64], P(('groups', 'dom')), parts along dimension 0, may hold values from 1 to 6, as said below
- tile_map: int32 [32, 64, 6, 5, 2], P(('groups', 'dom')), parts along dimension 0, may hold values from 0 to 127
- blocks: bfloat16 [5, 2, 128, 128], replicated, may hold values from -0.39648438 to 0.39648438
- z_kernel: bfloat16 [3, 2, 64, 64], replicated, may hold values from -0.3125 to 0.3125
- rank_cap: int32 [1], replicated, may hold values from 2 to 32
Outputs:
- image_next: bfloat16 [32, 64, 128, 128], P(('groups', 'dom')), parts along dimension 0
There are 2 independent parts, one for each index of `groups`. A program takes and returns all parts, laid end to end along the dimension named above; an argument that names none is the same for every part. Nothing has to cross between parts.
Inputs may be any that keep to these rules, and one draw needn't show every extreme that they name: `spoke_counts`: partitions less than 2 away from partition 16 // 2 take 6 - 1 or 6 spokes in every frame, all others 1 or 2; partition 16 // 2 takes 6 spokes in some frame.
All inputs are finite; a program needn't handle non-finite values.
Results may differ from a plain program's by a relative error of at most 0.0055.
Values may be sent and summed in bfloat16 or wider, within the bound.
No kernel may reach another device: no remote copies, remote signals or barrier semaphores. Data moves between devices by JAX's collectives and lax.ppermute only.
A program may use at most 128 MiB of HBM per device.

v0:
```python
import jax
import jax.numpy as jnp
from jax import lax
from jax.sharding import PartitionSpec as P
import functools
from jax.experimental import pallas as pl
from jax.experimental.pallas import tpu as pltpu

SOFT_CUT = 0.25


def padded_2(block, sides, width):
    for axis, dim in sides:
        count = lax.axis_size(axis)
        forward = [(i, i + 1) for i in range(count - 1)]
        backward = [(target, source) for source, target in forward]
        low = lax.ppermute(
            lax.slice_in_dim(block, block.shape[dim] - width, None, axis=dim), axis, forward
        )
        high = lax.ppermute(lax.slice_in_dim(block, 0, width, axis=dim), axis, backward)
        block = jnp.concatenate([low, block, high], axis=dim)
    return block


def rotate(field_values):
    half_width = field_values.shape[-1] // 2
    return jnp.concatenate(
        [-field_values[..., half_width:], field_values[..., :half_width]], axis=-1
    )


def complex_times(left_value, right_value):
    half_width = left_value.shape[-1] // 2
    left_real, left_imag = (left_value[..., :half_width], left_value[..., half_width:])
    right_real, right_imag = (right_value[..., :half_width], right_value[..., half_width:])
    return jnp.concatenate(
        [
            left_real * right_real - left_imag * right_imag,
            left_real * right_imag + left_imag * right_real,
        ],
        axis=-1,
    )


def conj_times(left_value, right_value):
    half_width = left_value.shape[-1] // 2
    left_real, left_imag = (left_value[..., :half_width], left_value[..., half_width:])
    right_real, right_imag = (right_value[..., :half_width], right_value[..., half_width:])
    return jnp.concatenate(
        [
            left_real * right_real + left_imag * right_imag,
            left_real * right_imag - left_imag * right_real,
        ],
        axis=-1,
    )


def grid_gradient(image_plane, plane_maps, counts, plane_map, blocks):
    frame_count, tile_count, lane_width = image_plane.shape
    read_tiles, link_count = (plane_map.shape[2], plane_map.shape[3])
    coil_count = plane_maps.shape[0]
    tile_ids = jnp.arange(tile_count, dtype=jnp.int32)

    def one_slot(spoke_slot, accum):
        tile_index = lax.dynamic_index_in_dim(plane_map, spoke_slot, axis=1, keepdims=False)
        flat_index = tile_index.reshape(frame_count, read_tiles * link_count)
        image_picked = jnp.take_along_axis(image_plane, flat_index[:, :, None], axis=1)
        image_picked = image_picked.reshape(frame_count, read_tiles, link_count, lane_width)
        maps_picked = jnp.take(plane_maps, flat_index.reshape(-1), axis=1)
        maps_picked = maps_picked.reshape(
            coil_count, frame_count, read_tiles, link_count, lane_width
        ).astype(jnp.float32)
        coil_tiles = complex_times(maps_picked, image_picked.astype(jnp.float32)[None]).astype(
            jnp.bfloat16
        )
        samples = jnp.einsum(
            "ctqji,qjio->ctqo", coil_tiles, blocks, preferred_element_type=jnp.float32
        )
        live_mask = (counts > spoke_slot).astype(jnp.float32)[None, :, None, None]
        samples = (samples * live_mask).astype(jnp.bfloat16)
        spread = jnp.einsum("ctqo,qjio->ctqji", samples, blocks, preferred_element_type=jnp.float32)
        back_sum = jnp.sum(conj_times(maps_picked, spread), axis=0)
        back_sum = back_sum.reshape(frame_count, read_tiles * link_count, lane_width)
        onehot = (flat_index[:, :, None] == tile_ids).astype(jnp.float32)
        return accum + jnp.einsum("tkn,tkw->tnw", onehot, back_sum, precision=lax.Precision.HIGHEST)

    most_spokes = jnp.max(counts)
    start_value = jnp.zeros((frame_count, tile_count, lane_width), jnp.float32)
    return lax.fori_loop(0, most_spokes, one_slot, start_value)


def gradient_kernel(idx_ref, cnt_ref, nsl_ref, img_ref, adj_ref, mrr_ref, mii_ref,
                    bf_ref, bt_ref, btr_ref, out_ref, x_scr, rx_scr, g_scr,
                    lhs_scr, y_scr, ry_scr, *, fb, slots, links, coils):
    b = pl.program_id(0)
    reads = links // 2
    img = img_ref[...].astype(jnp.float32)
    x_scr[...] = img
    half = img.shape[-1] // 2
    lane = lax.broadcasted_iota(jnp.int32, img.shape, 2)
    sign = jnp.where(lane < half, -1.0, 1.0).astype(jnp.float32)
    rx_scr[...] = pltpu.roll(img, half, 2) * sign
    g_scr[...] = jnp.zeros_like(g_scr)
    lhs_scr[...] = jnp.zeros_like(lhs_scr)

    def slot_body(s, carry):
        for q in range(reads):
            def gather_t(t, c):
                frame = b * fb + t
                live = cnt_ref[frame] > s
                base = (frame * slots + s) * links + q * 2
                row = pl.multiple_of(t * coils, coils)

                @pl.when(live)
                def _():
                    for j in range(2):
                        p = idx_ref[base + j]
                        xv = x_scr[t, pl.ds(p, 1), :]
                        rxv = rx_scr[t, pl.ds(p, 1), :]
                        ct = mrr_ref[p] * xv + mii_ref[p] * rxv
                        lhs_scr[pl.ds(row, coils), pl.ds(j * 128, 128)] = ct.astype(jnp.bfloat16)
                return c

            lax.fori_loop(0, fb, gather_t, 0)
            samples = jnp.dot(lhs_scr[...], bf_ref[q], preferred_element_type=jnp.float32)
            samples = samples.astype(jnp.bfloat16)
            y_scr[...] = jnp.dot(samples, bt_ref[q], preferred_element_type=jnp.float32)
            ry_scr[...] = jnp.dot(samples, btr_ref[q], preferred_element_type=jnp.float32)

            def scatter_t(t, c):
                frame = b * fb + t
                live = cnt_ref[frame] > s
                base = (frame * slots + s) * links + q * 2
                row = pl.multiple_of(t * coils, coils)

                @pl.when(live)
                def _():
                    for j in range(2):
                        p = idx_ref[base + j]
                        yv = y_scr[pl.ds(row, coils), pl.ds(j * 128, 128)]
                        ryv = ry_scr[pl.ds(row, coils), pl.ds(j * 128, 128)]
                        v = mrr_ref[p] * yv - mii_ref[p] * ryv
                        back = jnp.sum(v, axis=0, keepdims=True)
                        g_scr[t, pl.ds(p, 1), :] = g_scr[t, pl.ds(p, 1), :] + back
                return c

            lax.fori_loop(0, fb, scatter_t, 0)
        return carry

    lax.fori_loop(0, nsl_ref[b], slot_body, 0)
    out_ref[...] = (x_scr[...] - (g_scr[...] - adj_ref[...].astype(jnp.float32))).astype(out_ref.dtype)


def fresh_image_of(image_plane, adjoint_plane, plane_maps, counts, plane_map, blocks):
    frame_count, tile_count, lane_width = image_plane.shape
    slots, reads, links = plane_map.shape[1], plane_map.shape[2], plane_map.shape[3]
    coils = plane_maps.shape[0]
    fb = 16 if frame_count % 16 == 0 else frame_count
    nblocks = frame_count // fb
    half = lane_width // 2
    maps_t = jnp.swapaxes(plane_maps.astype(jnp.float32), 0, 1)
    mrr = jnp.concatenate([maps_t[..., :half], maps_t[..., :half]], axis=-1)
    mii = jnp.concatenate([maps_t[..., half:], maps_t[..., half:]], axis=-1)
    bf = blocks.reshape(reads, links * lane_width, lane_width)
    bt4 = jnp.transpose(blocks, (0, 3, 1, 2))
    bt = bt4.reshape(reads, lane_width, links * lane_width)
    btr = rotate(bt4).reshape(reads, lane_width, links * lane_width)
    idx = plane_map.reshape(-1).astype(jnp.int32)
    cnt = counts.astype(jnp.int32)
    nsl = jnp.minimum(jnp.max(cnt.reshape(nblocks, fb), axis=1), slots).astype(jnp.int32)
    kernel = functools.partial(
        gradient_kernel, fb=fb, slots=slots, links=reads * links, coils=coils
    )
    plane_spec = pl.BlockSpec((fb, tile_count, lane_width), lambda b, *_: (b, 0, 0))
    whole3 = lambda shape: pl.BlockSpec(shape, lambda b, *_: (0, 0, 0))
    flops = 2 * frame_count * slots * reads * coils * (links * lane_width) * lane_width * 3
    return pl.pallas_call(
        kernel,
        out_shape=jax.ShapeDtypeStruct(image_plane.shape, jnp.bfloat16),
        grid_spec=pltpu.PrefetchScalarGridSpec(
            num_scalar_prefetch=3,
            grid=(nblocks,),
            in_specs=[
                plane_spec,
                plane_spec,
                whole3(mrr.shape),
                whole3(mii.shape),
                whole3(bf.shape),
                whole3(bt.shape),
                whole3(btr.shape),
            ],
            out_specs=plane_spec,
            scratch_shapes=[
                pltpu.VMEM((fb, tile_count, lane_width), jnp.float32),
                pltpu.VMEM((fb, tile_count, lane_width), jnp.float32),
                pltpu.VMEM((fb, tile_count, lane_width), jnp.float32),
                pltpu.VMEM((fb * coils, links * lane_width), jnp.bfloat16),
                pltpu.VMEM((fb * coils, links * lane_width), jnp.float32),
                pltpu.VMEM((fb * coils, links * lane_width), jnp.float32),
            ],
        ),
        compiler_params=pltpu.CompilerParams(dimension_semantics=("arbitrary",)),
        cost_estimate=pl.CostEstimate(
            flops=flops, transcendentals=0, bytes_accessed=image_plane.size * 6 + mrr.size * 8
        ),
    )(idx, cnt, nsl, image_plane, adjoint_plane, mrr, mii, bf, bt, btr)


def post_kernel(x_ref, xb_ref, xa_ref, wl_ref, wz_ref, out_ref, *, cut):
    frames, width = x_ref.shape
    lane = lax.broadcasted_iota(jnp.int32, (frames, width), 1) % 128
    low_lane = lane < 64

    def turn(v):
        return jnp.where(low_lane, -pltpu.roll(v, width - 64, 1), pltpu.roll(v, 64, 1))

    def pair(v):
        return jnp.where(low_lane, pltpu.roll(v, width - 64, 1), pltpu.roll(v, 64, 1))

    def low_of(plane):
        mixed = jnp.dot(wl_ref[...], plane, preferred_element_type=jnp.float32)
        return mixed[:frames] + turn(mixed[frames:])

    def remainder_of(plane):
        return (plane.astype(jnp.float32) - low_of(plane)).astype(jnp.bfloat16)

    x = x_ref[...]
    low = low_of(x)
    rem = (x.astype(jnp.float32) - low).astype(jnp.bfloat16)
    planes = jnp.concatenate([remainder_of(xb_ref[...]), rem, remainder_of(xa_ref[...])], axis=0)
    mixed = jnp.dot(wz_ref[...], planes, preferred_element_type=jnp.float32)
    filtered = mixed[:frames] + turn(mixed[frames:])
    square = filtered * filtered
    magnitude = jnp.sqrt(square + pair(square))
    scale = jnp.maximum(magnitude - cut, 0.0) / jnp.maximum(magnitude, cut)
    out_ref[...] = (low + filtered * scale).astype(out_ref.dtype)


def post_of(plane, before, after, low_t, filter_t):
    frames, width = plane.shape
    nb = 2048 if width % 2048 == 0 else width
    lane_spec = pl.BlockSpec((frames, nb), lambda i: (0, i))
    whole2 = lambda shape: pl.BlockSpec(shape, lambda i: (0, 0))
    return pl.pallas_call(
        functools.partial(post_kernel, cut=SOFT_CUT),
        out_shape=jax.ShapeDtypeStruct(plane.shape, jnp.bfloat16),
        grid=(width // nb,),
        in_specs=[lane_spec, lane_spec, lane_spec, whole2(low_t.shape), whole2(filter_t.shape)],
        out_specs=lane_spec,
        compiler_params=pltpu.CompilerParams(dimension_semantics=("arbitrary",)),
        cost_estimate=pl.CostEstimate(
            flops=2 * width * frames * (2 * frames) * 6, transcendentals=width * frames,
            bytes_accessed=plane.size * 8,
        ),
    )(plane, before, after, low_t, filter_t)


def apply_frames(mix_real, mix_imag, field_values):
    direct = jnp.einsum("fg,zftw->zgtw", mix_real, field_values, preferred_element_type=jnp.float32)
    turned = jnp.einsum(
        "fg,zftw->zgtw", mix_imag, rotate(field_values), preferred_element_type=jnp.float32
    )
    return direct + turned


def soft_shrink(filtered):
    half_width = filtered.shape[-1] // 2
    real_part, imag_part = (filtered[..., :half_width], filtered[..., half_width:])
    magnitude = jnp.sqrt(real_part * real_part + imag_part * imag_part)
    scale_values = jnp.maximum(magnitude - SOFT_CUT, 0.0) / jnp.maximum(magnitude, SOFT_CUT)
    return filtered * jnp.concatenate([scale_values, scale_values], axis=-1)


def tree_sum(value, axis):
    count = lax.axis_size(axis)
    if count & (count - 1):
        return lax.psum(value, axis)
    step = 1
    while step < count:
        pairs = [(i, i ^ step) for i in range(count)]
        value = value + lax.ppermute(value, axis, pairs)
        step *= 2
    return value


def mix_frames(weights, field_values):
    half = weights.shape[1] // 2
    mixed = jnp.einsum("kh,ktw->htw", weights, field_values, preferred_element_type=jnp.float32)
    return mixed[:half] + rotate(mixed[half:])


def local(image, adjoint_data, coil_maps, spoke_counts, tile_map, blocks, z_kernel, rank_cap):
    frame_count = image.shape[1]
    fresh = fresh_image_of(
        image[0], adjoint_data[0], coil_maps[0], spoke_counts[0], tile_map[0], blocks
    )
    count = lax.axis_size("dom")
    forward = [(i, i + 1) for i in range(count - 1)]
    backward = [(target, source) for source, target in forward]
    flat = fresh.reshape(frame_count, -1)
    fresh_before = lax.ppermute(flat, "dom", forward)
    fresh_after = lax.ppermute(flat, "dom", backward)
    rows_real = flat
    rows_turned = rotate(fresh).reshape(frame_count, -1)
    gram_real = jnp.einsum("fn,gn->fg", rows_real, rows_real, preferred_element_type=jnp.float32)
    gram_imag = jnp.einsum("fn,gn->fg", rows_turned, rows_real, preferred_element_type=jnp.float32)
    gram_real, gram_imag = tree_sum(jnp.stack([gram_real, gram_imag]), "dom")
    stacked = jnp.block([[gram_real, -gram_imag], [gram_imag, gram_real]])
    threshold_sq = jnp.trace(gram_real) / rank_cap[0].astype(jnp.float32)
    unit_matrix = jnp.eye(2 * frame_count, dtype=jnp.float32)
    chol_factor = jnp.linalg.cholesky(stacked + threshold_sq * unit_matrix)
    shrink = jax.scipy.linalg.cho_solve((chol_factor, True), stacked)
    shrink_real = shrink[:frame_count, :frame_count].astype(jnp.bfloat16)
    shrink_imag = shrink[frame_count:, :frame_count].astype(jnp.bfloat16)
    low_t = jnp.concatenate([shrink_real, shrink_imag], axis=1).T
    taps = z_kernel.shape[0]
    filter_weights = jnp.concatenate([z_kernel[:, 0], z_kernel[:, 1]], axis=-1)
    filter_t = filter_weights.reshape(taps * frame_count, 2 * frame_count).T
    out = post_of(flat, fresh_before, fresh_after, low_t, filter_t)
    return out.reshape(image.shape)


def solution(mesh):
    return jax.shard_map(
        local,
        mesh=mesh,
        in_specs=(
            P(("groups", "dom"), None, None, None),
            P(("groups", "dom"), None, None, None),
            P(("groups", "dom"), None, None, None),
            P(("groups", "dom"), None),
            P(("groups", "dom"), None, None, None, None),
            P(),
            P(),
            P(),
        ),
        out_specs=P(("groups", "dom"), None, None, None),
        check_vma=False,
    )
```

profile of v0, /device:TPU:0, one launch (start us, length us, event | category | flops | bytes accessed | tf_op | source)
XLA Modules:
  0.0 243.3 jit_solution(2340326692472705016)
XLA Ops:
  0.0 1.4 convert_bitcast_fusion
  1.4 1.3 fusion.21
  2.8 0.9 copy.34.btr_ref
  3.7 0.8 copy.20
  4.4 0.9 reshape_squeeze.6.idx_ref
  5.4 0.9 copy.33.bt_ref
  6.8 0.6 reduce.9
  8.1 3.5 %pad_maximum_fusion.1 = (f32[128,16,128]{2,1,0:T(8,128)}, f32[128,16,128]{2,1,0:T(8,128)}) fusion(f32[128,16,64]{2,1,0:T(8,128)} %get-tuple-element.8, f32[128,16,64]{2,1,0:T(8,128)S(1)} %get-tuple-element.7), kind=kLoop, calls=%fused_computation.11 | loop fusion | flops 524288 | bytes 3145728 | tf_op jit(solution)/shard_map/concatenate | solution.py:162
  11.6 46.1 %shard_map.82 = bf16[64,128,128]{2,1,0:T(8,128)(2,1)} custom-call(s32[3840]{0:T(1024)} %reshape_squeeze.6.idx_ref, s32[64]{0:T(128)} %bitcast.66, s32[4]{0:T(128)} %broadcast_minimum_fusion.nsl_ref, bf16[64,128,128]{2,1,0:T(8,128)(2,1)} %bitcast.64, bf16[64,128,128]{2,1,0:T(8,128)(2,1)} %bitcast.65, f32[128,16,128]{2,1,0:T(8,128)} %get-tuple-element.19.mrr_ref, ...), custom_call_target="tpu_custom_call" | custom-call | flops 6039797760 | bytes 8388608 | tf_op jit(solution)/shard_map/pallas_call | solution.py:177
  57.7 3.2 %slice_negate_fusion = (bf16[64,128,64]{2,1,0:T(8,128)(2,1)S(1)}, bf16[64,128,64]{2,1,0:T(8,128)(2,1)S(1)}) fusion(bf16[64,128,128]{2,1,0:T(8,128)(2,1)} %shard_map.82), kind=kLoop, calls=%fused_computation.1 | loop fusion | flops 524288 | bytes 4194304 | tf_op jit(solution)/shard_map/neg | solution.py:28
  61.0 2.4 fusion.5
  63.4 1.2 pad_maximum_fusion
  64.6 2.4 fusion.8
  67.1 1.5 collective-permute-start.2
  68.5 0.9 collective-permute-done.2
  69.4 3.4 %collective-permute-start.3 = (f32[2,64,64]{2,1,0:T(8,128)S(1)}, f32[2,64,64]{2,1,0:T(8,128)S(1)}, u32[]{:S(2)}, u32[]{:S(2)}) collective-permute-start(f32[2,64,64]{2,1,0:T(8,128)S(1)} %fusion.20), channel_id=1, source_target_pairs={{0,2},{1,3},{2,0},{3,1},{4,6},{5,7},{6,4},{7,5},{8,10},{9,11},{10,... | collective-permute-start | bytes 98312 | tf_op jit(solution)/shard_map/ppermute | solution.py:281
  72.8 1.4 copy.51
  74.2 3.1 %collective-permute-start = (bf16[64,16384]{1,0:T(8,128)(2,1)S(1)}, bf16[64,16384]{1,0:T(8,128)(2,1)}, u32[]{:S(2)}, u32[]{:S(2)}) collective-permute-start(bf16[64,16384]{1,0:T(8,128)(2,1)S(1)} %bitcast.54), channel_id=1, source_target_pairs={{0,1},{1,2},{2,3},{3,4},{4,5},{5,6},{6,7},{7,8},{8,9},{9,10},{10,1... | collective-permute-start | bytes 6291464 | tf_op jit(solution)/shard_map/ppermute | solution.py:301
  77.3 1.5 collective-permute-start.1
  78.8 91.8 %collective-permute-start.4 = (f32[2,64,64]{2,1,0:T(8,128)S(1)}, f32[2,64,64]{2,1,0:T(8,128)S(1)}, u32[]{:S(2)}, u32[]{:S(2)}) collective-permute-start(f32[2,64,64]{2,1,0:T(8,128)S(1)} %fusion.25), channel_id=1, source_target_pairs={{0,4},{1,5},{2,6},{3,7},{4,0},{5,1},{6,2},{7,3},{8,12},{9,13},{10,... | collective-permute-start | bytes 98312 | tf_op jit(solution)/shard_map/ppermute | solution.py:281
  170.9 24.9 %collective-permute-done.4 = f32[2,64,64]{2,1,0:T(8,128)S(1)} collective-permute-done((f32[2,64,64]{2,1,0:T(8,128)S(1)}, f32[2,64,64]{2,1,0:T(8,128)S(1)}, u32[]{:S(2)}, u32[]{:S(2)}) %collective-permute-start.4) | collective-permute-done | bytes 32800 | tf_op jit(solution)/shard_map/ppermute | solution.py:281
  195.7 1.1 collective-permute-start.5
  196.9 0.6 maximum_bitcast_fusion.wz_ref
  198.2 2.8 %collective-permute-done.5 = f32[2,64,64]{2,1,0:T(8,128)S(1)} collective-permute-done((f32[2,64,64]{2,1,0:T(8,128)S(1)}, f32[2,64,64]{2,1,0:T(8,128)S(1)}, u32[]{:S(2)}, u32[]{:S(2)}) %collective-permute-start.5) | collective-permute-done | bytes 32800 | tf_op jit(solution)/shard_map/ppermute | solution.py:281
  201.0 0.6 fusion.19
  202.5 11.7 %cholesky.16 = f32[128,128]{1,0:T(8,128)S(1)} custom-call(f32[128,128]{1,0:T(8,128)S(1)} %fusion.17), custom_call_target="Cholesky" | custom-call | tf_op jit(solution)/shard_map/jit(cholesky)/cholesky | solution.py:311
  214.3 0.7 compare_reduce_fusion
  215.0 0.6 fusion.13
  215.6 9.8 %custom-call.10 = f32[1,128,128]{1,2,0:T(8,128)S(1)} custom-call(f32[1,128,128]{2,1,0:T(8,128)S(1)} %fusion.13), custom_call_target="InvertDiagBlocksLowerTriangular" | custom-call | tf_op jit(solution)/shard_map/jit(_cho_solve)/triangular_solve | solution.py:312
  226.1 0.6 maximum_bitcast_fusion.1.wl_ref
  226.7 13.0 %shard_map.83 = bf16[64,16384]{1,0:T(8,128)(2,1)} custom-call(bf16[64,16384]{1,0:T(8,128)(2,1)} %bitcast.56, bf16[64,16384]{1,0:T(8,128)(2,1)} %collective-permute-done.xb_ref, bf16[64,16384]{1,0:T(8,128)(2,1)} %collective-permute-done.1.xa_ref, bf16[128,64]{1,0:T(8,128)(2,1)} %maximum_bitcast_fusion.1.wl_ref, bf16[128,192]{1,0:T(8,128)(2,1)} %maximum_bitcast_fusion.wz_ref), custom_call_target="tpu_custom_call" | custom-call | flops 1610612736 | bytes 8388608 | tf_op jit(solution)/shard_map/pallas_call | solution.py:244
  239.8 3.5 %copy.36 = bf16[8,8,128,128]{3,2,1,0:T(8,128)(2,1)} copy(bf16[8,8,128,128]{3,1,2,0:T(8,128)(2,1)} %bitcast.57) | data formatting | bytes 4194304
  (37 shorter events, 2.6 us)
Async XLA Ops:
  1.4 1.3 copy-start.2
  1.4 2.3 copy-start.4
  2.7 4.0 %copy-start.5 = (s32[1,64]{1,0:T(1,128)S(1)}, s32[1,64]{1,0:T(1,128)}, u32[]{:S(2)}) copy-start(s32[1,64]{1,0:T(1,128)} %param.11) | copy-start | bytes 772
  57.7 3.2 %copy-start = (bf16[64,128,128]{2,1,0:T(8,128)(2,1)S(1)}, bf16[64,128,128]{2,1,0:T(8,128)(2,1)}, u32[]{:S(2)}) copy-start(bf16[64,128,128]{2,1,0:T(8,128)(2,1)} %shard_map.82) | copy-start | bytes 6291460
  67.1 2.4 collective-permute-start.2
  69.4 9.4 %collective-permute-start.3 = (f32[2,64,64]{2,1,0:T(8,128)S(1)}, f32[2,64,64]{2,1,0:T(8,128)S(1)}, u32[]{:S(2)}, u32[]{:S(2)}) collective-permute-start(f32[2,64,64]{2,1,0:T(8,128)S(1)} %fusion.20), channel_id=1, source_target_pairs={{0,2},{1,3},{2,0},{3,1},{4,6},{5,7},{6,4},{7,5},{8,10},{9,11},{10,... | collective-permute-start | bytes 98312 | tf_op jit(solution)/shard_map/ppermute | solution.py:281
  72.8 97.9 %copy-start.3 = (bf16[3,2,64,64]{3,2,1,0:T(8,128)(2,1)S(1)}, bf16[3,2,64,64]{3,2,1,0:T(8,128)(2,1)}, u32[]{:S(2)}) copy-start(bf16[3,2,64,64]{3,2,1,0:T(8,128)(2,1)} %param.14) | copy-start | bytes 147460
  74.2 152.6 %copy-start.1 = (bf16[8,8,128,128]{3,1,2,0:T(8,128)(2,1)}, bf16[8,8,128,128]{3,1,2,0:T(8,128)(2,1)S(1)}, u32[]{:S(2)}) copy-start(bf16[8,8,128,128]{3,1,2,0:T(8,128)(2,1)S(1)} %copy.51) | copy-start | bytes 6291460
  74.2 152.6 %collective-permute-start = (bf16[64,16384]{1,0:T(8,128)(2,1)S(1)}, bf16[64,16384]{1,0:T(8,128)(2,1)}, u32[]{:S(2)}, u32[]{:S(2)}) collective-permute-start(bf16[64,16384]{1,0:T(8,128)(2,1)S(1)} %bitcast.54), channel_id=1, source_target_pairs={{0,1},{1,2},{2,3},{3,4},{4,5},{5,6},{6,7},{7,8},{8,9},{9,10},{10,1... | collective-permute-start | bytes 6291464 | tf_op jit(solution)/shard_map/ppermute | solution.py:301
  77.3 149.4 %collective-permute-start.1 = (bf16[64,16384]{1,0:T(8,128)(2,1)S(1)}, bf16[64,16384]{1,0:T(8,128)(2,1)}, u32[]{:S(2)}, u32[]{:S(2)}) collective-permute-start(bf16[64,16384]{1,0:T(8,128)(2,1)S(1)} %bitcast.55), channel_id=1, source_target_pairs={{1,0},{2,1},{3,2},{4,3},{5,4},{6,5},{7,6},{8,7},{9,8},{10,9},{11,1... | collective-permute-start | bytes 6291464 | tf_op jit(solution)/shard_map/ppermute | solution.py:302
  78.8 116.9 %collective-permute-start.4 = (f32[2,64,64]{2,1,0:T(8,128)S(1)}, f32[2,64,64]{2,1,0:T(8,128)S(1)}, u32[]{:S(2)}, u32[]{:S(2)}) collective-permute-start(f32[2,64,64]{2,1,0:T(8,128)S(1)} %fusion.25), channel_id=1, source_target_pairs={{0,4},{1,5},{2,6},{3,7},{4,0},{5,1},{6,2},{7,3},{8,12},{9,13},{10,... | collective-permute-start | bytes 98312 | tf_op jit(solution)/shard_map/ppermute | solution.py:281
  195.7 5.2 %collective-permute-start.5 = (f32[2,64,64]{2,1,0:T(8,128)S(1)}, f32[2,64,64]{2,1,0:T(8,128)S(1)}, u32[]{:S(2)}, u32[]{:S(2)}) collective-permute-start(f32[2,64,64]{2,1,0:T(8,128)S(1)} %add.32), channel_id=1, source_target_pairs={{0,8},{1,9},{2,10},{3,11},{4,12},{5,13},{6,14},{7,15},{8,0},{9,1},... | collective-permute-start | bytes 98312 | tf_op jit(solution)/shard_map/ppermute | solution.py:281
where the time goes:
time: 244 us; the launch traced here: 243 us
  starting transfers between devices  102 us (42%)
  Pallas kernels  59.2 us (24%)
  other arithmetic  35.6 us (15%)
  waiting for transfers between devices  28.6 us (12%)
  local copies, waits for them, and re-layouts  10.6 us (4%)
  matrix products  5.45 us (2%)
    ppermute x4, starting transfers between devices, tree_sum(): value = value + lax.ppermute(value, axis, pairs)  97.8 us
    pallas_call x1, Pallas kernels, fresh_image_of(): pl.pallas_call(kernel, out_shape=jax.ShapeDtypeStruct(image_plane.shape,...  46.1 us
    ppermute x4, waiting for transfers between devices, tree_sum(): value = value + lax.ppermute(value, axis, pairs)  28.6 us
    pallas_call x1, Pallas kernels, post_of(): pl.pallas_call(functools.partial(post_kernel, cut=SOFT_CUT), out_shape=ja...  13 us
    another operation x3, other arithmetic, local(): chol_factor = jnp.linalg.cholesky(stacked + threshold_sq * unit_matrix)  12.4 us
    another operation x2, other arithmetic, local(): shrink = jax.scipy.linalg.cho_solve((chol_factor, True), stacked)  10.4 us
    unnamed x16, local copies, waits for them, and re-layouts  6.15 us
  transfers between devices with their start and end apart: 6, of which 3 were waited for; matrix products, arithmetic and copies ran while one was open for 11% of the time, Pallas kernels for 0%

commit v1 on v0

--- a/solution.py
+++ b/solution.py
@@ -107,21 +107,17 @@
         for q in range(reads):
             def gather_t(t, c):
                 frame = b * fb + t
-                live = cnt_ref[frame] > s
                 base = (frame * slots + s) * links + q * 2
                 row = pl.multiple_of(t * coils, coils)
-
-                @pl.when(live)
-                def _():
-                    for j in range(2):
-                        p = idx_ref[base + j]
-                        xv = x_scr[t, pl.ds(p, 1), :]
-                        rxv = rx_scr[t, pl.ds(p, 1), :]
-                        ct = mrr_ref[p] * xv + mii_ref[p] * rxv
-                        lhs_scr[pl.ds(row, coils), pl.ds(j * 128, 128)] = ct.astype(jnp.bfloat16)
+                for j in range(2):
+                    p = idx_ref[base + j]
+                    xv = x_scr[t, pl.ds(p, 1), :]
+                    rxv = rx_scr[t, pl.ds(p, 1), :]
+                    ct = mrr_ref[p] * xv + mii_ref[p] * rxv
+                    lhs_scr[pl.ds(row, coils), pl.ds(j * 128, 128)] = ct.astype(jnp.bfloat16)
                 return c
 
-            lax.fori_loop(0, fb, gather_t, 0)
+            lax.fori_loop(0, fb, gather_t, 0, unroll=True)
             samples = jnp.dot(lhs_scr[...], bf_ref[q], preferred_element_type=jnp.float32)
             samples = samples.astype(jnp.bfloat16)
             y_scr[...] = jnp.dot(samples, bt_ref[q], preferred_element_type=jnp.float32)
@@ -133,18 +129,17 @@
                 base = (frame * slots + s) * links + q * 2
                 row = pl.multiple_of(t * coils, coils)
 
-                @pl.when(live)
-                def _():
-                    for j in range(2):
-                        p = idx_ref[base + j]
-                        yv = y_scr[pl.ds(row, coils), pl.ds(j * 128, 128)]
-                        ryv = ry_scr[pl.ds(row, coils), pl.ds(j * 128, 128)]
-                        v = mrr_ref[p] * yv - mii_ref[p] * ryv
-                        back = jnp.sum(v, axis=0, keepdims=True)
-                        g_scr[t, pl.ds(p, 1), :] = g_scr[t, pl.ds(p, 1), :] + back
+                keep = live.astype(jnp.float32)
+                for j in range(2):
+                    p = idx_ref[base + j]
+                    yv = y_scr[pl.ds(row, coils), pl.ds(j * 128, 128)]
+                    ryv = ry_scr[pl.ds(row, coils), pl.ds(j * 128, 128)]
+                    v = mrr_ref[p] * yv - mii_ref[p] * ryv
+                    back = jnp.sum(v, axis=0, keepdims=True) * keep
+                    g_scr[t, pl.ds(p, 1), :] = g_scr[t, pl.ds(p, 1), :] + back
                 return c
 
-            lax.fori_loop(0, fb, scatter_t, 0)
+            lax.fori_loop(0, fb, scatter_t, 0, unroll=True)
         return carry
 
     lax.fori_loop(0, nsl_ref[b], slot_body, 0)
@@ -298,13 +293,14 @@
     forward = [(i, i + 1) for i in range(count - 1)]
     backward = [(target, source) for source, target in forward]
     flat = fresh.reshape(frame_count, -1)
-    fresh_before = lax.ppermute(flat, "dom", forward)
-    fresh_after = lax.ppermute(flat, "dom", backward)
     rows_real = flat
     rows_turned = rotate(fresh).reshape(frame_count, -1)
     gram_real = jnp.einsum("fn,gn->fg", rows_real, rows_real, preferred_element_type=jnp.float32)
     gram_imag = jnp.einsum("fn,gn->fg", rows_turned, rows_real, preferred_element_type=jnp.float32)
     gram_real, gram_imag = tree_sum(jnp.stack([gram_real, gram_imag]), "dom")
+    flat, gram_real, gram_imag = lax.optimization_barrier((flat, gram_real, gram_imag))
+    fresh_before = lax.ppermute(flat, "dom", forward)
+    fresh_after = lax.ppermute(flat, "dom", backward)
     stacked = jnp.block([[gram_real, -gram_imag], [gram_imag, gram_real]])
     threshold_sq = jnp.trace(gram_real) / rank_cap[0].astype(jnp.float32)
     unit_matrix = jnp.eye(2 * frame_count, dtype=jnp.float32)

time: 244 us -> 143 us (0.59)
  the two profiles are of different devices: /device:TPU:0 before, /device:TPU:19 now
where the time goes in v1:
time: 143 us; the launch traced here: 142 us
  Pallas kernels  51.8 us (36%)
  other arithmetic  35.7 us (25%)
  waiting for transfers between devices  28.4 us (20%)
  local copies, waits for them, and re-layouts  10.6 us (7%)
  starting transfers between devices  8.79 us (6%)
  matrix products  5.45 us (4%)
  between operations  1.52 us (1%)
    pallas_call x1, Pallas kernels, fresh_image_of(): pl.pallas_call(kernel, out_shape=jax.ShapeDtypeStruct(image_plane.shape,...  38.8 us
    ppermute x1, waiting for transfers between devices, local(): fresh_before = lax.ppermute(flat, 'dom', forward)  15.7 us
    pallas_call x1, Pallas kernels, post_of(): pl.pallas_call(functools.partial(post_kernel, cut=SOFT_CUT), out_shape=ja...  13 us
    another operation x3, other arithmetic, local(): chol_factor = jnp.linalg.cholesky(stacked + threshold_sq * unit_matrix)  12.5 us
    another operation x2, other arithmetic, local(): shrink = jax.scipy.linalg.cho_solve((chol_factor, True), stacked)  10.5 us
    ppermute x4, waiting for transfers between devices, tree_sum(): value = value + lax.ppermute(value, axis, pairs)  9.71 us
    unnamed x16, local copies, waits for them, and re-layouts  6.16 us
    ppermute x1, starting transfers between devices, local(): fresh_before = lax.ppermute(flat, 'dom', forward)  5.49 us
  transfers between devices with their start and end apart: 6, of which 6 were waited for; matrix products, arithmetic and copies ran while one was open for 19% of the time, Pallas kernels for 0%

profile of v1, /device:TPU:19, one launch (start us, length us, event | category | flops | bytes accessed | tf_op | source)
XLA Modules:
  0.0 142.3 jit_solution(15018528659229253334)
XLA Ops:
  0.0 1.4 convert_bitcast_fusion
  1.4 1.3 fusion.20
  2.8 0.9 copy.34.btr_ref
  3.7 0.8 copy.20
  4.4 0.9 reshape_squeeze.6.idx_ref
  5.4 0.9 copy.33.bt_ref
  6.8 0.6 reduce.9
  8.1 3.5 %pad_maximum_fusion.1 = (f32[128,16,128]{2,1,0:T(8,128)}, f32[128,16,128]{2,1,0:T(8,128)}) fusion(f32[128,16,64]{2,1,0:T(8,128)} %get-tuple-element.14, f32[128,16,64]{2,1,0:T(8,128)S(1)} %get-tuple-element.13), kind=kLoop, calls=%fused_computation.11 | loop fusion | flops 524288 | bytes 3145728 | tf_op jit(solution)/shard_map/concatenate | solution.py:157
  11.6 38.8 %shard_map.82 = bf16[64,128,128]{2,1,0:T(8,128)(2,1)} custom-call(s32[3840]{0:T(1024)} %reshape_squeeze.6.idx_ref, s32[64]{0:T(128)} %bitcast.62, s32[4]{0:T(128)} %broadcast_minimum_fusion.nsl_ref, bf16[64,128,128]{2,1,0:T(8,128)(2,1)} %bitcast.60, bf16[64,128,128]{2,1,0:T(8,128)(2,1)} %bitcast.61, f32[128,16,128]{2,1,0:T(8,128)} %get-tuple-element.23.mrr_ref, ...), custom_call_target="tpu_custom_call" | custom-call | flops 6039797760 | bytes 8388608 | tf_op jit(solution)/shard_map/pallas_call | solution.py:172
  50.4 3.2 %slice_negate_fusion = (bf16[64,128,64]{2,1,0:T(8,128)(2,1)S(1)}, bf16[64,128,64]{2,1,0:T(8,128)(2,1)S(1)}) fusion(bf16[64,128,128]{2,1,0:T(8,128)(2,1)} %shard_map.82), kind=kLoop, calls=%fused_computation.1 | loop fusion | flops 524288 | bytes 4194304 | tf_op jit(solution)/shard_map/neg | solution.py:28
  53.6 2.4 %fusion.5 = f32[1,64,64]{2,1,0:T(8,128)S(1)} fusion(bf16[64,128,128]{2,1,0:T(8,128)(2,1)S(1)} %copy-done), kind=kOutput, calls=%fused_computation.9 | convolution fusion | flops 134217728 | bytes 2113536 | tf_op jit(solution)/shard_map/fn,gn->fg/dot_general | solution.py:298
  56.1 1.2 pad_maximum_fusion
  57.3 2.4 %fusion.8 = f32[1,64,64]{2,1,0:T(8,128)S(1)} fusion(bf16[64,128,128]{2,1,0:T(8,128)(2,1)S(1)} %copy-done, bf16[64,128,128]{2,1,0:T(8,128)(2,1)S(1)} %pad_maximum_fusion), kind=kOutput, calls=%fused_computation.10 | convolution fusion | flops 134217728 | bytes 4210688 | tf_op jit(solution)/shard_map/fn,gn->fg/dot_general | solution.py:299
  59.7 0.7 collective-permute-start
  60.4 0.9 collective-permute-done
  61.4 3.1 %collective-permute-done.1 = f32[2,64,64]{2,1,0:T(8,128)S(1)} collective-permute-done((f32[2,64,64]{2,1,0:T(8,128)S(1)}, f32[2,64,64]{2,1,0:T(8,128)S(1)}, u32[]{:S(2)}, u32[]{:S(2)}) %collective-permute-start.1) | collective-permute-done | bytes 32800 | tf_op jit(solution)/shard_map/ppermute | solution.py:276
  64.6 3.1 %collective-permute-done.2 = f32[2,64,64]{2,1,0:T(8,128)S(1)} collective-permute-done((f32[2,64,64]{2,1,0:T(8,128)S(1)}, f32[2,64,64]{2,1,0:T(8,128)S(1)}, u32[]{:S(2)}, u32[]{:S(2)}) %collective-permute-start.2) | collective-permute-done | bytes 32800 | tf_op jit(solution)/shard_map/ppermute | solution.py:276
  67.8 1.4 copy.51
  69.2 2.6 %collective-permute-done.3 = f32[2,64,64]{2,1,0:T(8,128)S(1)} collective-permute-done((f32[2,64,64]{2,1,0:T(8,128)S(1)}, f32[2,64,64]{2,1,0:T(8,128)S(1)}, u32[]{:S(2)}, u32[]{:S(2)}) %collective-permute-start.3) | collective-permute-done | bytes 32800 | tf_op jit(solution)/shard_map/ppermute | solution.py:276
  71.8 5.5 %collective-permute-start.4 = (bf16[64,16384]{1,0:T(8,128)(2,1)S(1)}, bf16[64,16384]{1,0:T(8,128)(2,1)}, u32[]{:S(2)}, u32[]{:S(2)}) collective-permute-start(bf16[64,16384]{1,0:T(8,128)(2,1)S(1)} %bitcast.50), channel_id=1, source_target_pairs={{0,1},{1,2},{2,3},{3,4},{4,5},{5,6},{6,7},{7,8},{8,9},{9,10},{10,1... | collective-permute-start | bytes 6291464 | tf_op jit(solution)/shard_map/ppermute | solution.py:302
  77.3 2.4 %collective-permute-start.5 = (bf16[64,16384]{1,0:T(8,128)(2,1)S(1)}, bf16[64,16384]{1,0:T(8,128)(2,1)}, u32[]{:S(2)}, u32[]{:S(2)}) collective-permute-start(bf16[64,16384]{1,0:T(8,128)(2,1)S(1)} %bitcast.51), channel_id=1, source_target_pairs={{1,0},{2,1},{3,2},{4,3},{5,4},{6,5},{7,6},{8,7},{9,8},{10,9},{11,1... | collective-permute-start | bytes 6291464 | tf_op jit(solution)/shard_map/ppermute | solution.py:303
  80.6 0.6 maximum_bitcast_fusion.wz_ref
  81.2 0.6 select_reduce_fusion.1
  82.8 11.7 %cholesky.16 = f32[128,128]{1,0:T(8,128)S(1)} custom-call(f32[128,128]{1,0:T(8,128)S(1)} %fusion.17), custom_call_target="Cholesky" | custom-call | tf_op jit(solution)/shard_map/jit(cholesky)/cholesky | solution.py:307
  94.5 0.7 compare_reduce_fusion
  95.2 0.7 fusion.13
  95.9 9.8 %custom-call.10 = f32[1,128,128]{1,2,0:T(8,128)S(1)} custom-call(f32[1,128,128]{2,1,0:T(8,128)S(1)} %fusion.13), custom_call_target="InvertDiagBlocksLowerTriangular" | custom-call | tf_op jit(solution)/shard_map/jit(_cho_solve)/triangular_solve | solution.py:308
  106.4 0.6 maximum_bitcast_fusion.1.wl_ref
  107.1 15.7 %collective-permute-done.4.xb_ref = bf16[64,16384]{1,0:T(8,128)(2,1)} collective-permute-done((bf16[64,16384]{1,0:T(8,128)(2,1)S(1)}, bf16[64,16384]{1,0:T(8,128)(2,1)}, u32[]{:S(2)}, u32[]{:S(2)}) %collective-permute-start.4) | collective-permute-done | bytes 2097184 | tf_op jit(solution)/shard_map/ppermute | solution.py:302
  122.8 3.0 %collective-permute-done.5.xa_ref = bf16[64,16384]{1,0:T(8,128)(2,1)} collective-permute-done((bf16[64,16384]{1,0:T(8,128)(2,1)S(1)}, bf16[64,16384]{1,0:T(8,128)(2,1)}, u32[]{:S(2)}, u32[]{:S(2)}) %collective-permute-start.5) | collective-permute-done | bytes 2097184 | tf_op jit(solution)/shard_map/ppermute | solution.py:303
  125.8 13.0 %shard_map.83 = bf16[64,16384]{1,0:T(8,128)(2,1)} custom-call(bf16[64,16384]{1,0:T(8,128)(2,1)} %bitcast.52, bf16[64,16384]{1,0:T(8,128)(2,1)} %collective-permute-done.4.xb_ref, bf16[64,16384]{1,0:T(8,128)(2,1)} %collective-permute-done.5.xa_ref, bf16[128,64]{1,0:T(8,128)(2,1)} %maximum_bitcast_fusion.1.wl_ref, bf16[128,192]{1,0:T(8,128)(2,1)} %maximum_bitcast_fusion.wz_ref), custom_call_target="tpu_custom_call" | custom-call | flops 1610612736 | bytes 8388608 | tf_op jit(solution)/shard_map/pallas_call | solution.py:239
  138.8 3.5 %copy.36 = bf16[8,8,128,128]{3,2,1,0:T(8,128)(2,1)} copy(bf16[8,8,128,128]{3,1,2,0:T(8,128)(2,1)} %bitcast.53) | data formatting | bytes 4194304
  (38 shorter events, 2.8 us)
Async XLA Ops:
  1.4 1.3 copy-start.2
  1.4 2.3 %copy-start.4 = (s32[1,64,6,5,2]{1,4,3,2,0:T(2,128)S(1)}, s32[1,64,6,5,2]{1,4,3,2,0:T(2,128)}, u32[]{:S(2)}) copy-start(s32[1,64,6,5,2]{1,4,3,2,0:T(2,128)} %param.12) | copy-start | bytes 46084
  2.7 4.0 %copy-start.5 = (s32[1,64]{1,0:T(1,128)S(1)}, s32[1,64]{1,0:T(1,128)}, u32[]{:S(2)}) copy-start(s32[1,64]{1,0:T(1,128)} %param.11) | copy-start | bytes 772
  50.4 3.2 %copy-start = (bf16[64,128,128]{2,1,0:T(8,128)(2,1)S(1)}, bf16[64,128,128]{2,1,0:T(8,128)(2,1)}, u32[]{:S(2)}) copy-start(bf16[64,128,128]{2,1,0:T(8,128)(2,1)} %shard_map.82) | copy-start | bytes 6291460
  59.7 1.6 %collective-permute-start = (f32[2,64,64]{2,1,0:T(8,128)S(1)}, f32[2,64,64]{2,1,0:T(8,128)S(1)}, u32[]{:S(2)}, u32[]{:S(2)}) collective-permute-start(f32[2,64,64]{2,1,0:T(8,128)S(1)} %pad_maximum_fusion.4), channel_id=1, source_target_pairs={{0,1},{1,0},{2,3},{3,2},{4,5},{5,4},{6,7},{7,6},{8,9},{9,8},{10,11... | collective-permute-start | bytes 98312 | tf_op jit(solution)/shard_map/ppermute | solution.py:276
  61.3 3.2 %collective-permute-start.1 = (f32[2,64,64]{2,1,0:T(8,128)S(1)}, f32[2,64,64]{2,1,0:T(8,128)S(1)}, u32[]{:S(2)}, u32[]{:S(2)}) collective-permute-start(f32[2,64,64]{2,1,0:T(8,128)S(1)} %fusion.19), channel_id=1, source_target_pairs={{0,2},{1,3},{2,0},{3,1},{4,6},{5,7},{6,4},{7,5},{8,10},{9,11},{10,... | collective-permute-start | bytes 98312 | tf_op jit(solution)/shard_map/ppermute | solution.py:276
  64.5 3.2 %collective-permute-start.2 = (f32[2,64,64]{2,1,0:T(8,128)S(1)}, f32[2,64,64]{2,1,0:T(8,128)S(1)}, u32[]{:S(2)}, u32[]{:S(2)}) collective-permute-start(f32[2,64,64]{2,1,0:T(8,128)S(1)} %fusion.24), channel_id=1, source_target_pairs={{0,4},{1,5},{2,6},{3,7},{4,0},{5,1},{6,2},{7,3},{8,12},{9,13},{10,... | collective-permute-start | bytes 98312 | tf_op jit(solution)/shard_map/ppermute | solution.py:276
  67.7 4.1 %collective-permute-start.3 = (f32[2,64,64]{2,1,0:T(8,128)S(1)}, f32[2,64,64]{2,1,0:T(8,128)S(1)}, u32[]{:S(2)}, u32[]{:S(2)}) collective-permute-start(f32[2,64,64]{2,1,0:T(8,128)S(1)} %add.32), channel_id=1, source_target_pairs={{0,8},{1,9},{2,10},{3,11},{4,12},{5,13},{6,14},{7,15},{8,0},{9,1},... | collective-permute-start | bytes 98312 | tf_op jit(solution)/shard_map/ppermute | solution.py:276
  67.8 12.5 %copy-start.3 = (bf16[3,2,64,64]{3,2,1,0:T(8,128)(2,1)S(1)}, bf16[3,2,64,64]{3,2,1,0:T(8,128)(2,1)}, u32[]{:S(2)}) copy-start(bf16[3,2,64,64]{3,2,1,0:T(8,128)(2,1)} %param.14) | copy-start | bytes 147460
  69.2 56.6 %copy-start.1 = (bf16[8,8,128,128]{3,1,2,0:T(8,128)(2,1)}, bf16[8,8,128,128]{3,1,2,0:T(8,128)(2,1)S(1)}, u32[]{:S(2)}) copy-start(bf16[8,8,128,128]{3,1,2,0:T(8,128)(2,1)S(1)} %copy.51) | copy-start | bytes 6291460
  71.8 50.9 %collective-permute-start.4 = (bf16[64,16384]{1,0:T(8,128)(2,1)S(1)}, bf16[64,16384]{1,0:T(8,128)(2,1)}, u32[]{:S(2)}, u32[]{:S(2)}) collective-permute-start(bf16[64,16384]{1,0:T(8,128)(2,1)S(1)} %bitcast.50), channel_id=1, source_target_pairs={{0,1},{1,2},{2,3},{3,4},{4,5},{5,6},{6,7},{7,8},{8,9},{9,10},{10,1... | collective-permute-start | bytes 6291464 | tf_op jit(solution)/shard_map/ppermute | solution.py:302
  77.3 48.4 %collective-permute-start.5 = (bf16[64,16384]{1,0:T(8,128)(2,1)S(1)}, bf16[64,16384]{1,0:T(8,128)(2,1)}, u32[]{:S(2)}, u32[]{:S(2)}) collective-permute-start(bf16[64,16384]{1,0:T(8,128)(2,1)S(1)} %bitcast.51), channel_id=1, source_target_pairs={{1,0},{2,1},{3,2},{4,3},{5,4},{6,5},{7,6},{8,7},{9,8},{10,9},{11,1... | collective-permute-start | bytes 6291464 | tf_op jit(solution)/shard_map/ppermute | solution.py:303

commit v2 on v1

--- a/solution.py
+++ b/solution.py
@@ -89,9 +89,9 @@
     return lax.fori_loop(0, most_spokes, one_slot, start_value)
 
 
-def gradient_kernel(idx_ref, cnt_ref, nsl_ref, img_ref, adj_ref, mrr_ref, mii_ref,
+def gradient_kernel(idx_ref, cnt_ref, nsl_ref, img_ref, adj_ref, maps_ref,
                     bf_ref, bt_ref, btr_ref, out_ref, x_scr, rx_scr, g_scr,
-                    lhs_scr, y_scr, ry_scr, *, fb, slots, links, coils):
+                    lhs_scr, y_scr, ry_scr, mrr_ref, mii_ref, *, fb, slots, links, coils):
     b = pl.program_id(0)
     reads = links // 2
     img = img_ref[...].astype(jnp.float32)
@@ -100,6 +100,14 @@
     lane = lax.broadcasted_iota(jnp.int32, img.shape, 2)
     sign = jnp.where(lane < half, -1.0, 1.0).astype(jnp.float32)
     rx_scr[...] = pltpu.roll(img, half, 2) * sign
+
+    @pl.when(b == 0)
+    def _():
+        maps = maps_ref[...].astype(jnp.float32)
+        map_lane = lax.broadcasted_iota(jnp.int32, maps.shape, 2) < half
+        swapped = pltpu.roll(maps, half, 2)
+        mrr_ref[...] = jnp.where(map_lane, maps, swapped)
+        mii_ref[...] = jnp.where(map_lane, swapped, maps)
     g_scr[...] = jnp.zeros_like(g_scr)
     lhs_scr[...] = jnp.zeros_like(lhs_scr)
 
@@ -153,9 +161,7 @@
     fb = 16 if frame_count % 16 == 0 else frame_count
     nblocks = frame_count // fb
     half = lane_width // 2
-    maps_t = jnp.swapaxes(plane_maps.astype(jnp.float32), 0, 1)
-    mrr = jnp.concatenate([maps_t[..., :half], maps_t[..., :half]], axis=-1)
-    mii = jnp.concatenate([maps_t[..., half:], maps_t[..., half:]], axis=-1)
+    maps_t = jnp.swapaxes(plane_maps, 0, 1)
     bf = blocks.reshape(reads, links * lane_width, lane_width)
     bt4 = jnp.transpose(blocks, (0, 3, 1, 2))
     bt = bt4.reshape(reads, lane_width, links * lane_width)
@@ -178,8 +184,7 @@
             in_specs=[
                 plane_spec,
                 plane_spec,
-                whole3(mrr.shape),
-                whole3(mii.shape),
+                whole3(maps_t.shape),
                 whole3(bf.shape),
                 whole3(bt.shape),
                 whole3(btr.shape),
@@ -192,13 +197,15 @@
                 pltpu.VMEM((fb * coils, links * lane_width), jnp.bfloat16),
                 pltpu.VMEM((fb * coils, links * lane_width), jnp.float32),
                 pltpu.VMEM((fb * coils, links * lane_width), jnp.float32),
+                pltpu.VMEM(maps_t.shape, jnp.float32),
+                pltpu.VMEM(maps_t.shape, jnp.float32),
             ],
         ),
         compiler_params=pltpu.CompilerParams(dimension_semantics=("arbitrary",)),
         cost_estimate=pl.CostEstimate(
-            flops=flops, transcendentals=0, bytes_accessed=image_plane.size * 6 + mrr.size * 8
+            flops=flops, transcendentals=0, bytes_accessed=image_plane.size * 6 + maps_t.size * 2
         ),
-    )(idx, cnt, nsl, image_plane, adjoint_plane, mrr, mii, bf, bt, btr)
+    )(idx, cnt, nsl, image_plane, adjoint_plane, maps_t, bf, bt, btr)
 
 
 def post_kernel(x_ref, xb_ref, xa_ref, wl_ref, wz_ref, out_ref, *, cut):
@@ -250,6 +257,38 @@
     )(plane, before, after, low_t, filter_t)
 
 
+def solve_kernel(a_ref, x0_ref, s_ref, out_ref, *, steps):
+    size = a_ref.shape[0]
+    rows = lax.broadcasted_iota(jnp.int32, (size, size), 0)
+    cols = lax.broadcasted_iota(jnp.int32, (size, size), 1)
+    twice = jnp.where(rows == cols, 2.0, 0.0).astype(jnp.float32)
+    a = a_ref[...]
+    high = lax.Precision.HIGHEST
+
+    def step(i, x):
+        t = jnp.dot(a, x, precision=high, preferred_element_type=jnp.float32)
+        return jnp.dot(x, twice - t, precision=high, preferred_element_type=jnp.float32)
+
+    x = x0_ref[...]
+    for i in range(steps):
+        x = step(i, x)
+    out_ref[...] = jnp.dot(x, s_ref[...], precision=high, preferred_element_type=jnp.float32)
+
+
+def shrink_of(stacked, threshold_sq, rank_value):
+    size = stacked.shape[0]
+    unit_matrix = jnp.eye(size, dtype=jnp.float32)
+    system = stacked + threshold_sq * unit_matrix
+    start = unit_matrix * (2.0 / (threshold_sq * (2.0 + rank_value)))
+    whole = pl.BlockSpec(memory_space=pltpu.VMEM)
+    return pl.pallas_call(
+        functools.partial(solve_kernel, steps=12),
+        out_shape=jax.ShapeDtypeStruct((size, size), jnp.float32),
+        in_specs=[whole, whole, whole],
+        out_specs=whole,
+    )(system, start, stacked)
+
+
 def apply_frames(mix_real, mix_imag, field_values):
     direct = jnp.einsum("fg,zftw->zgtw", mix_real, field_values, preferred_element_type=jnp.float32)
     turned = jnp.einsum(
@@ -302,10 +341,9 @@
     fresh_before = lax.ppermute(flat, "dom", forward)
     fresh_after = lax.ppermute(flat, "dom", backward)
     stacked = jnp.block([[gram_real, -gram_imag], [gram_imag, gram_real]])
-    threshold_sq = jnp.trace(gram_real) / rank_cap[0].astype(jnp.float32)
-    unit_matrix = jnp.eye(2 * frame_count, dtype=jnp.float32)
-    chol_factor = jnp.linalg.cholesky(stacked + threshold_sq * unit_matrix)
-    shrink = jax.scipy.linalg.cho_solve((chol_factor, True), stacked)
+    rank_value = rank_cap[0].astype(jnp.float32)
+    threshold_sq = jnp.trace(gram_real) / rank_value
+    shrink = shrink_of(stacked, threshold_sq, rank_value)
     shrink_real = shrink[:frame_count, :frame_count].astype(jnp.bfloat16)
     shrink_imag = shrink[frame_count:, :frame_count].astype(jnp.bfloat16)
     low_t = jnp.concatenate([shrink_real, shrink_imag], axis=1).T

time: 143 us -> 139 us (0.972)
  other arithmetic: 35.7 us -> 10.1 us
  waiting for transfers between devices: 28.4 us -> 43 us
  Pallas kernels: 51.8 us -> 58.4 us
  local copies, waits for them, and re-layouts: 10.6 us -> 12.1 us
    another operation x5 -> x0, other arithmetic: 23 us -> none  [the longest x3 12.5 us: local(): chol_factor = jnp.linalg.cholesky(stacked + threshold_sq * unit_matrix)]
    ppermute x1, waiting for transfers between devices: 15.7 us -> 30.2 us  [local(): fresh_before = lax.ppermute(flat, 'dom', forward)]
    pallas_call x0 -> x1, Pallas kernels: none -> 6.94 us  [shrink_of(): pl.pallas_call(functools.partial(solve_kernel, steps=12), out_shape=jax.S...]
    concatenate x1 -> x0, other arithmetic: 3.49 us -> none  [fresh_image_of(): mrr = jnp.concatenate([maps_t[..., :half], maps_t[..., :half]], axis=-1)]
    unnamed x16 -> x17, local copies, waits for them, and re-layouts: 6.16 us -> 8.08 us
  transfers between devices with their start and end apart: 6 -> 6, of which waited for: 6 -> 6; matrix products, arithmetic and copies ran while one was open for 19% -> 4% of each run, Pallas kernels for 0% -> 5%
where the time goes in v2:
time: 139 us
  Pallas kernels  58.4 us (42%)
  waiting for transfers between devices  43 us (31%)
  local copies, waits for them, and re-layouts  12.1 us (9%)
  other arithmetic  10.1 us (7%)
  starting transfers between devices  8.78 us (6%)
  matrix products  4.84 us (3%)
  between operations  1.58 us (1%)
    pallas_call x1, Pallas kernels, fresh_image_of(): pl.pallas_call(kernel, out_shape=jax.ShapeDtypeStruct(image_plane.shape,...  38.4 us
    ppermute x1, waiting for transfers between devices, local(): fresh_before = lax.ppermute(flat, 'dom', forward)  30.2 us
    pallas_call x1, Pallas kernels, post_of(): pl.pallas_call(functools.partial(post_kernel, cut=SOFT_CUT), out_shape=ja...  13 us
    ppermute x4, waiting for transfers between devices, tree_sum(): value = value + lax.ppermute(value, axis, pairs)  9.71 us
    unnamed x17, local copies, waits for them, and re-layouts  8.08 us
    pallas_call x1, Pallas kernels, shrink_of(): pl.pallas_call(functools.partial(solve_kernel, steps=12), out_shape=jax.S...  6.94 us
    ppermute x1, starting transfers between devices, local(): fresh_before = lax.ppermute(flat, 'dom', forward)  5.49 us
    neg x2, other arithmetic, rotate(): -field_values[..., half_width:]  4.27 us
  transfers between devices with their start and end apart: 6, of which 6 were waited for; matrix products, arithmetic and copies ran while one was open for 4% of the time, Pallas kernels for 5%

profile of v2, /device:TPU:19, one launch (start us, length us, event | category | flops | bytes accessed | tf_op | source)
XLA Modules:
  0.0 138.9 jit_solution(15283703923338719802)
XLA Ops:
  0.0 1.0 slice_negate_fusion.1
  1.1 0.9 copy.31.btr_ref
  2.0 1.5 %copy.19 = s32[1,64,6,5,2]{4,3,2,1,0:T(8,128)S(1)} copy(s32[1,64,6,5,2]{1,4,3,2,0:T(2,128)} %param.12) | data formatting | bytes 30720 | tf_op args[4]
  3.6 0.9 reshape_squeeze.6.idx_ref
  4.5 1.1 copy.49
  5.6 0.9 copy.30.bt_ref
  7.1 0.7 reduce.3
  7.9 0.5 broadcast_minimum_fusion.nsl_ref
  8.5 38.4 %shard_map.82 = bf16[64,128,128]{2,1,0:T(8,128)(2,1)} custom-call(s32[3840]{0:T(1024)} %reshape_squeeze.6.idx_ref, s32[64]{0:T(128)} %bitcast.51, s32[4]{0:T(128)} %broadcast_minimum_fusion.nsl_ref, bf16[64,128,128]{2,1,0:T(8,128)(2,1)} %bitcast.49, bf16[64,128,128]{2,1,0:T(8,128)(2,1)} %bitcast.50, bf16[128,16,128]{2,1,0:T(8,128)(2,1)} %bitcast.46, ...), custom_call_target="tpu_custom_call" | custom-call | flops 6039797760 | bytes 6815744 | tf_op jit(solution)/shard_map/pallas_call | solution.py:178
  46.9 3.2 %slice_negate_fusion = (bf16[64,128,64]{2,1,0:T(8,128)(2,1)S(1)}, bf16[64,128,64]{2,1,0:T(8,128)(2,1)S(1)}) fusion(bf16[64,128,128]{2,1,0:T(8,128)(2,1)} %shard_map.82), kind=kLoop, calls=%fused_computation.1 | loop fusion | flops 524288 | bytes 4194304 | tf_op jit(solution)/shard_map/neg | solution.py:28
  50.2 2.4 %fusion.5 = f32[1,64,64]{2,1,0:T(8,128)S(1)} fusion(bf16[64,128,128]{2,1,0:T(8,128)(2,1)S(1)} %copy-done), kind=kOutput, calls=%fused_computation.8 | convolution fusion | flops 134217728 | bytes 2113536 | tf_op jit(solution)/shard_map/fn,gn->fg/dot_general | solution.py:337
  52.6 1.2 pad_maximum_fusion
  53.8 2.4 %fusion.8 = f32[1,64,64]{2,1,0:T(8,128)S(1)} fusion(bf16[64,128,128]{2,1,0:T(8,128)(2,1)S(1)} %copy-done, bf16[64,128,128]{2,1,0:T(8,128)(2,1)S(1)} %pad_maximum_fusion), kind=kOutput, calls=%fused_computation.9 | convolution fusion | flops 134217728 | bytes 4210688 | tf_op jit(solution)/shard_map/fn,gn->fg/dot_general | solution.py:338
  56.3 0.7 collective-permute-start
  57.0 0.9 collective-permute-done
  58.0 3.1 %collective-permute-done.1 = f32[2,64,64]{2,1,0:T(8,128)S(1)} collective-permute-done((f32[2,64,64]{2,1,0:T(8,128)S(1)}, f32[2,64,64]{2,1,0:T(8,128)S(1)}, u32[]{:S(2)}, u32[]{:S(2)}) %collective-permute-start.1) | collective-permute-done | bytes 32800 | tf_op jit(solution)/shard_map/ppermute | solution.py:315
  61.2 3.1 %collective-permute-done.2 = f32[2,64,64]{2,1,0:T(8,128)S(1)} collective-permute-done((f32[2,64,64]{2,1,0:T(8,128)S(1)}, f32[2,64,64]{2,1,0:T(8,128)S(1)}, u32[]{:S(2)}, u32[]{:S(2)}) %collective-permute-start.2) | collective-permute-done | bytes 32800 | tf_op jit(solution)/shard_map/ppermute | solution.py:315
  64.4 1.4 copy.48
  65.8 2.6 %collective-permute-done.3 = f32[2,64,64]{2,1,0:T(8,128)S(1)} collective-permute-done((f32[2,64,64]{2,1,0:T(8,128)S(1)}, f32[2,64,64]{2,1,0:T(8,128)S(1)}, u32[]{:S(2)}, u32[]{:S(2)}) %collective-permute-start.3) | collective-permute-done | bytes 32800 | tf_op jit(solution)/shard_map/ppermute | solution.py:315
  68.4 5.5 %collective-permute-start.4 = (bf16[64,16384]{1,0:T(8,128)(2,1)S(1)}, bf16[64,16384]{1,0:T(8,128)(2,1)}, u32[]{:S(2)}, u32[]{:S(2)}) collective-permute-start(bf16[64,16384]{1,0:T(8,128)(2,1)S(1)} %bitcast.38), channel_id=1, source_target_pairs={{0,1},{1,2},{2,3},{3,4},{4,5},{5,6},{6,7},{7,8},{8,9},{9,10},{10,1... | collective-permute-start | bytes 6291464 | tf_op jit(solution)/shard_map/ppermute | solution.py:341
  73.9 2.3 %collective-permute-start.5 = (bf16[64,16384]{1,0:T(8,128)(2,1)S(1)}, bf16[64,16384]{1,0:T(8,128)(2,1)}, u32[]{:S(2)}, u32[]{:S(2)}) collective-permute-start(bf16[64,16384]{1,0:T(8,128)(2,1)S(1)} %bitcast.39), channel_id=1, source_target_pairs={{1,0},{2,1},{3,2},{4,3},{5,4},{6,5},{7,6},{8,7},{9,8},{10,9},{11,1... | collective-permute-start | bytes 6291464 | tf_op jit(solution)/shard_map/ppermute | solution.py:342
  77.1 0.6 maximum_bitcast_fusion.wz_ref
  77.8 0.7 select_reduce_fusion
  79.2 0.6 fusion.13.x0_ref
  79.8 0.7 select_add_fusion
  80.5 6.9 %shard_map.83 = f32[128,128]{1,0:T(8,128)} custom-call(f32[128,128]{1,0:T(8,128)} %get-tuple-element.11.a_ref, f32[128,128]{1,0:T(8,128)} %fusion.13.x0_ref, f32[128,128]{1,0:T(8,128)} %get-tuple-element.12.s_ref), custom_call_target="tpu_custom_call" | custom-call | tf_op jit(solution)/shard_map/pallas_call | solution.py:284
  87.5 0.9 copy.27
  88.5 0.6 maximum_bitcast_fusion.1.wl_ref
  89.1 30.2 %collective-permute-done.4.xb_ref = bf16[64,16384]{1,0:T(8,128)(2,1)} collective-permute-done((bf16[64,16384]{1,0:T(8,128)(2,1)S(1)}, bf16[64,16384]{1,0:T(8,128)(2,1)}, u32[]{:S(2)}, u32[]{:S(2)}) %collective-permute-start.4) | collective-permute-done | bytes 2097184 | tf_op jit(solution)/shard_map/ppermute | solution.py:341
  119.3 3.0 %collective-permute-done.5.xa_ref = bf16[64,16384]{1,0:T(8,128)(2,1)} collective-permute-done((bf16[64,16384]{1,0:T(8,128)(2,1)S(1)}, bf16[64,16384]{1,0:T(8,128)(2,1)}, u32[]{:S(2)}, u32[]{:S(2)}) %collective-permute-start.5) | collective-permute-done | bytes 2097184 | tf_op jit(solution)/shard_map/ppermute | solution.py:342
  122.4 13.0 %shard_map.84 = bf16[64,16384]{1,0:T(8,128)(2,1)} custom-call(bf16[64,16384]{1,0:T(8,128)(2,1)} %bitcast.40, bf16[64,16384]{1,0:T(8,128)(2,1)} %collective-permute-done.4.xb_ref, bf16[64,16384]{1,0:T(8,128)(2,1)} %collective-permute-done.5.xa_ref, bf16[128,64]{1,0:T(8,128)(2,1)} %maximum_bitcast_fusion.1.wl_ref, bf16[128,192]{1,0:T(8,128)(2,1)} %maximum_bitcast_fusion.wz_ref), custom_call_target="tpu_custom_call" | custom-call | flops 1610612736 | bytes 8388608 | tf_op jit(solution)/shard_map/pallas_call | solution.py:246
  135.4 3.5 %copy.33 = bf16[8,8,128,128]{3,2,1,0:T(8,128)(2,1)} copy(bf16[8,8,128,128]{3,1,2,0:T(8,128)(2,1)} %bitcast.41) | data formatting | bytes 4194304
  (30 shorter events, 1.3 us)
Async XLA Ops:
  1.0 3.5 %copy-start.3 = (bf16[1,16,128,128]{3,2,1,0:T(8,128)(2,1)S(1)}, bf16[1,16,128,128]{3,2,1,0:T(8,128)(2,1)}, u32[]{:S(2)}) copy-start(bf16[1,16,128,128]{3,2,1,0:T(8,128)(2,1)} %param.10) | copy-start | bytes 1572868
  2.0 3.6 %copy-start.2 = (bf16[5,2,128,128]{3,2,1,0:T(8,128)(2,1)S(1)}, bf16[5,2,128,128]{3,2,1,0:T(8,128)(2,1)}, u32[]{:S(2)}) copy-start(bf16[5,2,128,128]{3,2,1,0:T(8,128)(2,1)} %param.13) | copy-start | bytes 983044
  2.0 5.1 %copy-start.5 = (s32[1,64]{1,0:T(1,128)S(1)}, s32[1,64]{1,0:T(1,128)}, u32[]{:S(2)}) copy-start(s32[1,64]{1,0:T(1,128)} %param.11) | copy-start | bytes 772
  46.9 3.2 %copy-start = (bf16[64,128,128]{2,1,0:T(8,128)(2,1)S(1)}, bf16[64,128,128]{2,1,0:T(8,128)(2,1)}, u32[]{:S(2)}) copy-start(bf16[64,128,128]{2,1,0:T(8,128)(2,1)} %shard_map.82) | copy-start | bytes 6291460
  56.3 1.6 %collective-permute-start = (f32[2,64,64]{2,1,0:T(8,128)S(1)}, f32[2,64,64]{2,1,0:T(8,128)S(1)}, u32[]{:S(2)}, u32[]{:S(2)}) collective-permute-start(f32[2,64,64]{2,1,0:T(8,128)S(1)} %pad_maximum_fusion.2), channel_id=1, source_target_pairs={{0,1},{1,0},{2,3},{3,2},{4,5},{5,4},{6,7},{7,6},{8,9},{9,8},{10,11... | collective-permute-start | bytes 98312 | tf_op jit(solution)/shard_map/ppermute | solution.py:315
  57.9 3.2 %collective-permute-start.1 = (f32[2,64,64]{2,1,0:T(8,128)S(1)}, f32[2,64,64]{2,1,0:T(8,128)S(1)}, u32[]{:S(2)}, u32[]{:S(2)}) collective-permute-start(f32[2,64,64]{2,1,0:T(8,128)S(1)} %fusion.14), channel_id=1, source_target_pairs={{0,2},{1,3},{2,0},{3,1},{4,6},{5,7},{6,4},{7,5},{8,10},{9,11},{10,... | collective-permute-start | bytes 98312 | tf_op jit(solution)/shard_map/ppermute | solution.py:315
  61.1 3.2 %collective-permute-start.2 = (f32[2,64,64]{2,1,0:T(8,128)S(1)}, f32[2,64,64]{2,1,0:T(8,128)S(1)}, u32[]{:S(2)}, u32[]{:S(2)}) collective-permute-start(f32[2,64,64]{2,1,0:T(8,128)S(1)} %fusion.17), channel_id=1, source_target_pairs={{0,4},{1,5},{2,6},{3,7},{4,0},{5,1},{6,2},{7,3},{8,12},{9,13},{10,... | collective-permute-start | bytes 98312 | tf_op jit(solution)/shard_map/ppermute | solution.py:315
  64.3 4.1 %collective-permute-start.3 = (f32[2,64,64]{2,1,0:T(8,128)S(1)}, f32[2,64,64]{2,1,0:T(8,128)S(1)}, u32[]{:S(2)}, u32[]{:S(2)}) collective-permute-start(f32[2,64,64]{2,1,0:T(8,128)S(1)} %add.20), channel_id=1, source_target_pairs={{0,8},{1,9},{2,10},{3,11},{4,12},{5,13},{6,14},{7,15},{8,0},{9,1},... | collective-permute-start | bytes 98312 | tf_op jit(solution)/shard_map/ppermute | solution.py:315
  64.4 12.5 %copy-start.4 = (bf16[3,2,64,64]{3,2,1,0:T(8,128)(2,1)S(1)}, bf16[3,2,64,64]{3,2,1,0:T(8,128)(2,1)}, u32[]{:S(2)}) copy-start(bf16[3,2,64,64]{3,2,1,0:T(8,128)(2,1)} %param.14) | copy-start | bytes 147460
  65.8 56.6 %copy-start.1 = (bf16[8,8,128,128]{3,1,2,0:T(8,128)(2,1)}, bf16[8,8,128,128]{3,1,2,0:T(8,128)(2,1)S(1)}, u32[]{:S(2)}) copy-start(bf16[8,8,128,128]{3,1,2,0:T(8,128)(2,1)S(1)} %copy.48) | copy-start | bytes 6291460
  68.4 50.9 %collective-permute-start.4 = (bf16[64,16384]{1,0:T(8,128)(2,1)S(1)}, bf16[64,16384]{1,0:T(8,128)(2,1)}, u32[]{:S(2)}, u32[]{:S(2)}) collective-permute-start(bf16[64,16384]{1,0:T(8,128)(2,1)S(1)} %bitcast.38), channel_id=1, source_target_pairs={{0,1},{1,2},{2,3},{3,4},{4,5},{5,6},{6,7},{7,8},{8,9},{9,10},{10,1... | collective-permute-start | bytes 6291464 | tf_op jit(solution)/shard_map/ppermute | solution.py:341
  73.9 48.4 %collective-permute-start.5 = (bf16[64,16384]{1,0:T(8,128)(2,1)S(1)}, bf16[64,16384]{1,0:T(8,128)(2,1)}, u32[]{:S(2)}, u32[]{:S(2)}) collective-permute-start(bf16[64,16384]{1,0:T(8,128)(2,1)S(1)} %bitcast.39), channel_id=1, source_target_pairs={{1,0},{2,1},{3,2},{4,3},{5,4},{6,5},{7,6},{8,7},{9,8},{10,9},{11,1... | collective-permute-start | bytes 6291464 | tf_op jit(solution)/shard_map/ppermute | solution.py:342

commit v3 on v2

v3 whole, which is shorter than its diff:
```python
import jax
import jax.numpy as jnp
from jax import lax
from jax.sharding import PartitionSpec as P
import functools
from jax.experimental import pallas as pl
from jax.experimental.pallas import tpu as pltpu

SOFT_CUT = 0.25


def rotate(field_values):
    half_width = field_values.shape[-1] // 2
    return jnp.concatenate(
        [-field_values[..., half_width:], field_values[..., :half_width]], axis=-1
    )


def gradient_kernel(idx_ref, cnt_ref, nsl_ref, img_ref, adj_ref, maps_ref,
                    bf_ref, bt_ref, btr_ref, out_ref, x_scr, rx_scr, g_scr,
                    lhs_scr, y_scr, ry_scr, mrr_ref, mii_ref, *, fb, block, slots, links, coils):
    b = block
    reads = links // 2
    img = img_ref[...].astype(jnp.float32)
    x_scr[...] = img
    half = img.shape[-1] // 2
    lane = lax.broadcasted_iota(jnp.int32, img.shape, 2)
    sign = jnp.where(lane < half, -1.0, 1.0).astype(jnp.float32)
    rx_scr[...] = pltpu.roll(img, half, 2) * sign

    maps = maps_ref[...].astype(jnp.float32)
    map_lane = lax.broadcasted_iota(jnp.int32, maps.shape, 2) < half
    swapped = pltpu.roll(maps, half, 2)
    mrr_ref[...] = jnp.where(map_lane, maps, swapped)
    mii_ref[...] = jnp.where(map_lane, swapped, maps)
    g_scr[...] = jnp.zeros_like(g_scr)
    lhs_scr[...] = jnp.zeros_like(lhs_scr)

    def slot_body(s, carry):
        for q in range(reads):
            def gather_t(t, c):
                frame = b * fb + t
                base = (frame * slots + s) * links + q * 2
                row = pl.multiple_of(t * coils, coils)
                for j in range(2):
                    p = idx_ref[base + j]
                    xv = x_scr[t, pl.ds(p, 1), :]
                    rxv = rx_scr[t, pl.ds(p, 1), :]
                    ct = mrr_ref[p] * xv + mii_ref[p] * rxv
                    lhs_scr[pl.ds(row, coils), pl.ds(j * 128, 128)] = ct.astype(jnp.bfloat16)
                return c

            lax.fori_loop(0, fb, gather_t, 0, unroll=True)
            samples = jnp.dot(lhs_scr[...], bf_ref[q], preferred_element_type=jnp.float32)
            samples = samples.astype(jnp.bfloat16)
            y_scr[...] = jnp.dot(samples, bt_ref[q], preferred_element_type=jnp.float32)
            ry_scr[...] = jnp.dot(samples, btr_ref[q], preferred_element_type=jnp.float32)

            def scatter_t(t, c):
                frame = b * fb + t
                live = cnt_ref[frame] > s
                base = (frame * slots + s) * links + q * 2
                row = pl.multiple_of(t * coils, coils)

                keep = live.astype(jnp.float32)
                for j in range(2):
                    p = idx_ref[base + j]
                    yv = y_scr[pl.ds(row, coils), pl.ds(j * 128, 128)]
                    ryv = ry_scr[pl.ds(row, coils), pl.ds(j * 128, 128)]
                    v = mrr_ref[p] * yv - mii_ref[p] * ryv
                    back = jnp.sum(v, axis=0, keepdims=True) * keep
                    g_scr[t, pl.ds(p, 1), :] = g_scr[t, pl.ds(p, 1), :] + back
                return c

            lax.fori_loop(0, fb, scatter_t, 0, unroll=True)
        return carry

    lax.fori_loop(0, nsl_ref[b], slot_body, 0)
    out_ref[...] = (x_scr[...] - (g_scr[...] - adj_ref[...].astype(jnp.float32))).astype(out_ref.dtype)


def fresh_blocks_of(image_plane, adjoint_plane, plane_maps, counts, plane_map, blocks):
    frame_count, tile_count, lane_width = image_plane.shape
    slots, reads, links = plane_map.shape[1], plane_map.shape[2], plane_map.shape[3]
    coils = plane_maps.shape[0]
    fb = 16 if frame_count % 16 == 0 else frame_count
    nblocks = frame_count // fb
    maps_t = jnp.swapaxes(plane_maps, 0, 1)
    bf = blocks.reshape(reads, links * lane_width, lane_width)
    bt4 = jnp.transpose(blocks, (0, 3, 1, 2))
    bt = bt4.reshape(reads, lane_width, links * lane_width)
    btr = rotate(bt4).reshape(reads, lane_width, links * lane_width)
    idx = plane_map.reshape(-1).astype(jnp.int32)
    cnt = counts.astype(jnp.int32)
    nsl = jnp.minimum(jnp.max(cnt.reshape(nblocks, fb), axis=1), slots).astype(jnp.int32)
    whole3 = lambda shape: pl.BlockSpec(shape, lambda i, *_: (0, 0, 0))
    flops = 2 * fb * slots * reads * coils * (links * lane_width) * lane_width * 3
    outs = []
    for block in range(nblocks):
        kernel = functools.partial(
            gradient_kernel, fb=fb, block=block, slots=slots, links=reads * links, coils=coils
        )
        plane_spec = pl.BlockSpec(
            (fb, tile_count, lane_width), functools.partial(lambda k, i, *_: (k, 0, 0), block)
        )
        out_spec = pl.BlockSpec((fb, tile_count, lane_width), lambda i, *_: (0, 0, 0))
        outs.append(grad_call(kernel, fb, tile_count, lane_width, plane_spec, out_spec,
                              whole3, maps_t, bf, bt, btr, coils, links, flops,
                              idx, cnt, nsl, image_plane, adjoint_plane))
    return outs


def grad_call(kernel, fb, tile_count, lane_width, plane_spec, out_spec, whole3, maps_t, bf, bt,
              btr, coils, links, flops, idx, cnt, nsl, image_plane, adjoint_plane):
    return (pl.pallas_call(
            kernel,
            out_shape=jax.ShapeDtypeStruct((fb, tile_count, lane_width), jnp.bfloat16),
            grid_spec=pltpu.PrefetchScalarGridSpec(
                num_scalar_prefetch=3,
                grid=(1,),
                in_specs=[
                    plane_spec,
                    plane_spec,
                    whole3(maps_t.shape),
                    whole3(bf.shape),
                    whole3(bt.shape),
                    whole3(btr.shape),
                ],
                out_specs=out_spec,
                scratch_shapes=[
                    pltpu.VMEM((fb, tile_count, lane_width), jnp.float32),
                    pltpu.VMEM((fb, tile_count, lane_width), jnp.float32),
                    pltpu.VMEM((fb, tile_count, lane_width), jnp.float32),
                    pltpu.VMEM((fb * coils, links * lane_width), jnp.bfloat16),
                    pltpu.VMEM((fb * coils, links * lane_width), jnp.float32),
                    pltpu.VMEM((fb * coils, links * lane_width), jnp.float32),
                    pltpu.VMEM(maps_t.shape, jnp.float32),
                    pltpu.VMEM(maps_t.shape, jnp.float32),
                ],
            ),
            compiler_params=pltpu.CompilerParams(dimension_semantics=("arbitrary",)),
            cost_estimate=pl.CostEstimate(
                flops=flops, transcendentals=0,
                bytes_accessed=fb * tile_count * lane_width * 6 + maps_t.size * 2,
            ),
        )(idx, cnt, nsl, image_plane, adjoint_plane, maps_t, bf, bt, btr))


def post_kernel(*refs, pieces, cut):
    x_ref = refs[0]
    before = refs[1:1 + pieces]
    after = refs[1 + pieces:1 + 2 * pieces]
    wl_ref, wz_ref, out_ref = refs[1 + 2 * pieces:]
    frames, width = x_ref.shape
    lane = lax.broadcasted_iota(jnp.int32, (frames, width), 1) % 128
    low_lane = lane < 64

    def turn(v):
        return jnp.where(low_lane, -pltpu.roll(v, width - 64, 1), pltpu.roll(v, 64, 1))

    def pair(v):
        return jnp.where(low_lane, pltpu.roll(v, width - 64, 1), pltpu.roll(v, 64, 1))

    def low_of(plane):
        mixed = jnp.dot(wl_ref[...], plane, preferred_element_type=jnp.float32)
        return mixed[:frames] + turn(mixed[frames:])

    def remainder_of(plane):
        return (plane.astype(jnp.float32) - low_of(plane)).astype(jnp.bfloat16)

    x = x_ref[...]
    low = low_of(x)
    rem = (x.astype(jnp.float32) - low).astype(jnp.bfloat16)
    plane_before = jnp.concatenate([r[...] for r in before], axis=0)
    plane_after = jnp.concatenate([r[...] for r in after], axis=0)
    planes = jnp.concatenate([remainder_of(plane_before), rem, remainder_of(plane_after)], axis=0)
    mixed = jnp.dot(wz_ref[...], planes, preferred_element_type=jnp.float32)
    filtered = mixed[:frames] + turn(mixed[frames:])
    square = filtered * filtered
    magnitude = jnp.sqrt(square + pair(square))
    scale = jnp.maximum(magnitude - cut, 0.0) / jnp.maximum(magnitude, cut)
    out_ref[...] = (low + filtered * scale).astype(out_ref.dtype)


def post_of(plane, before, after, low_t, filter_t):
    frames, width = plane.shape
    pieces = len(before)
    piece = before[0].shape[0]
    nb = 2048 if width % 2048 == 0 else width
    lane_spec = pl.BlockSpec((frames, nb), lambda i: (0, i))
    piece_spec = pl.BlockSpec((piece, nb), lambda i: (0, i))
    whole2 = lambda shape: pl.BlockSpec(shape, lambda i: (0, 0))
    return pl.pallas_call(
        functools.partial(post_kernel, pieces=pieces, cut=SOFT_CUT),
        out_shape=jax.ShapeDtypeStruct(plane.shape, jnp.bfloat16),
        grid=(width // nb,),
        in_specs=[lane_spec] + [piece_spec] * (2 * pieces) + [whole2(low_t.shape), whole2(filter_t.shape)],
        out_specs=lane_spec,
        compiler_params=pltpu.CompilerParams(dimension_semantics=("arbitrary",)),
        cost_estimate=pl.CostEstimate(
            flops=2 * width * frames * (2 * frames) * 6, transcendentals=width * frames,
            bytes_accessed=plane.size * 8,
        ),
    )(plane, *before, *after, low_t, filter_t)


def solve_kernel(a_ref, x0_ref, s_ref, out_ref, *, steps):
    size = a_ref.shape[0]
    rows = lax.broadcasted_iota(jnp.int32, (size, size), 0)
    cols = lax.broadcasted_iota(jnp.int32, (size, size), 1)
    twice = jnp.where(rows == cols, 2.0, 0.0).astype(jnp.float32)
    a = a_ref[...]
    high = lax.Precision.HIGHEST

    def step(x):
        t = jnp.dot(a, x, precision=high, preferred_element_type=jnp.float32)
        return jnp.dot(x, twice - t, precision=high, preferred_element_type=jnp.float32)

    x = x0_ref[...]
    for _ in range(steps):
        x = step(x)
    out_ref[...] = jnp.dot(x, s_ref[...], precision=high, preferred_element_type=jnp.float32)


def shrink_of(stacked, threshold_sq, rank_value):
    size = stacked.shape[0]
    unit_matrix = jnp.eye(size, dtype=jnp.float32)
    system = stacked + threshold_sq * unit_matrix
    start = unit_matrix * (2.0 / (threshold_sq * (2.0 + rank_value)))
    whole = pl.BlockSpec(memory_space=pltpu.VMEM)
    return pl.pallas_call(
        functools.partial(solve_kernel, steps=12),
        out_shape=jax.ShapeDtypeStruct((size, size), jnp.float32),
        in_specs=[whole, whole, whole],
        out_specs=whole,
    )(system, start, stacked)


def tree_sum(value, axis):
    count = lax.axis_size(axis)
    if count & (count - 1):
        return lax.psum(value, axis)
    step = 1
    while step < count:
        pairs = [(i, i ^ step) for i in range(count)]
        value = value + lax.ppermute(value, axis, pairs)
        step *= 2
    return value


def local(image, adjoint_data, coil_maps, spoke_counts, tile_map, blocks, z_kernel, rank_cap):
    frame_count = image.shape[1]
    pieces = fresh_blocks_of(
        image[0], adjoint_data[0], coil_maps[0], spoke_counts[0], tile_map[0], blocks
    )
    count = lax.axis_size("dom")
    forward = [(i, i + 1) for i in range(count - 1)]
    backward = [(target, source) for source, target in forward]
    flat_pieces = [piece.reshape(piece.shape[0], -1) for piece in pieces]
    before, after = [], []
    for piece in flat_pieces[:-1]:
        before.append(lax.ppermute(piece, "dom", forward))
        after.append(lax.ppermute(piece, "dom", backward))
    fresh = jnp.concatenate(pieces, axis=0)
    flat = jnp.concatenate(flat_pieces, axis=0)
    rows_real = flat
    rows_turned = rotate(fresh).reshape(frame_count, -1)
    gram_real = jnp.einsum("fn,gn->fg", rows_real, rows_real, preferred_element_type=jnp.float32)
    gram_imag = jnp.einsum("fn,gn->fg", rows_turned, rows_real, preferred_element_type=jnp.float32)
    gram_real, gram_imag = tree_sum(jnp.stack([gram_real, gram_imag]), "dom")
    last, gram_real, gram_imag = lax.optimization_barrier((flat_pieces[-1], gram_real, gram_imag))
    before.append(lax.ppermute(last, "dom", forward))
    after.append(lax.ppermute(last, "dom", backward))
    stacked = jnp.block([[gram_real, -gram_imag], [gram_imag, gram_real]])
    rank_value = rank_cap[0].astype(jnp.float32)
    threshold_sq = jnp.trace(gram_real) / rank_value
    shrink = shrink_of(stacked, threshold_sq, rank_value)
    shrink_real = shrink[:frame_count, :frame_count].astype(jnp.bfloat16)
    shrink_imag = shrink[frame_count:, :frame_count].astype(jnp.bfloat16)
    low_t = jnp.concatenate([shrink_real, shrink_imag], axis=1).T
    taps = z_kernel.shape[0]
    filter_weights = jnp.concatenate([z_kernel[:, 0], z_kernel[:, 1]], axis=-1)
    filter_t = filter_weights.reshape(taps * frame_count, 2 * frame_count).T
    out = post_of(flat, before, after, low_t, filter_t)
    return out.reshape(image.shape)


def solution(mesh):
    return jax.shard_map(
        local,
        mesh=mesh,
        in_specs=(
            P(("groups", "dom"), None, None, None),
            P(("groups", "dom"), None, None, None),
            P(("groups", "dom"), None, None, None),
            P(("groups", "dom"), None),
            P(("groups", "dom"), None, None, None, None),
            P(),
            P(),
            P(),
        ),
        out_specs=P(("groups", "dom"), None, None, None),
        check_vma=False,
    )
```

time: 139 us -> 142 us (1.022)
  waiting for transfers between devices: 43 us -> 11.1 us
  starting transfers between devices: 8.78 us -> 30.4 us
  Pallas kernels: 58.4 us -> 69.1 us
  local copies, waits for them, and re-layouts: 12.1 us -> 16.8 us
  matrix products: 4.84 us -> 2.6 us
    ppermute x2 -> x8, waiting for transfers between devices: 33.3 us -> 7.11 us  [the longest x1 5.5 us: local(): after.append(lax.ppermute(last, 'dom', backward))]
    ppermute x2 -> x8, starting transfers between devices: 7.81 us -> 28.6 us  [the longest x3 11.8 us: local(): before.append(lax.ppermute(piece, 'dom', forward))]
    pallas_call x2 -> x5, Pallas kernels: 51.5 us -> 62.2 us  [the longest x4 49 us: grad_call(): pl.pallas_call(kernel, out_shape=jax.ShapeDtypeStruct((fb, tile_count, la...]
    ppermute x4, waiting for transfers between devices: 9.71 us -> 4 us  [tree_sum(): value = value + lax.ppermute(value, axis, pairs)]
    unnamed x17 -> x41, local copies, waits for them, and re-layouts: 8.08 us -> 12.4 us
    neg x2, other arithmetic: 4.27 us -> 1.9 us  [rotate(): -field_values[..., half_width:]]
    dot_general x1, matrix products: 2.42 us -> 0.69 us  [local(): jnp.einsum('fn,gn->fg', rows_real, rows_real, preferred_element_type=jnp....]
  transfers between devices with their start and end apart: 6 -> 12, of which waited for: 6 -> 5; matrix products, arithmetic and copies ran while one was open for 4% -> 7% of each run, Pallas kernels for 5% -> 5%
where the time goes in v3:
time: 142 us; the launch traced here: 141 us
  Pallas kernels  69.1 us (49%)
  starting transfers between devices  30.4 us (21%)
  local copies, waits for them, and re-layouts  16.8 us (12%)
  waiting for transfers between devices  11.1 us (8%)
  other arithmetic  9.2 us (6%)
  matrix products  2.6 us (2%)
  between operations  1.78 us (1%)
    pallas_call x4, Pallas kernels, grad_call(): pl.pallas_call(kernel, out_shape=jax.ShapeDtypeStruct((fb, tile_count, la...  49 us
    pallas_call x1, Pallas kernels, post_of(): pl.pallas_call(functools.partial(post_kernel, pieces=pieces, cut=SOFT_CUT...  13.2 us
    unnamed x41, local copies, waits for them, and re-layouts  12.4 us
    ppermute x3, starting transfers between devices, local(): before.append(lax.ppermute(piece, 'dom', forward))  11.8 us
    ppermute x3, starting transfers between devices, local(): after.append(lax.ppermute(piece, 'dom', backward))  10.2 us
    pallas_call x1, Pallas kernels, shrink_of(): pl.pallas_call(functools.partial(solve_kernel, steps=12), out_shape=jax.S...  6.96 us
    ppermute x1, waiting for transfers between devices, local(): after.append(lax.ppermute(last, 'dom', backward))  5.5 us
    ppermute x1, starting transfers between devices, local(): after.append(lax.ppermute(last, 'dom', backward))  4.54 us
  transfers between devices with their start and end apart: 12, of which 5 were waited for; matrix products, arithmetic and copies ran while one was open for 7% of the time, Pallas kernels for 5%

profile of v3, /device:TPU:19, one launch (start us, length us, event | category | flops | bytes accessed | tf_op | source)
XLA Modules:
  0.0 141.0 jit_solution(11544356464643368443)
XLA Ops:
  0.0 1.0 slice_negate_fusion.1
  1.1 0.9 copy.23.btr_ref
  2.0 1.5 %copy.15 = s32[1,64,6,5,2]{4,3,2,1,0:T(8,128)S(1)} copy(s32[1,64,6,5,2]{1,4,3,2,0:T(2,128)} %param.12) | data formatting | bytes 30720 | tf_op args[4]
  3.6 0.9 reshape_squeeze.6.idx_ref
  4.5 1.1 copy.53
  5.6 0.9 copy.22.bt_ref
  8.5 12.2 %shard_map.83 = bf16[16,128,128]{2,1,0:T(8,128)(2,1)} custom-call(s32[3840]{0:T(1024)} %reshape_squeeze.6.idx_ref, s32[64]{0:T(128)} %bitcast.99, s32[4]{0:T(128)} %broadcast_minimum_fusion.nsl_ref, bf16[64,128,128]{2,1,0:T(8,128)(2,1)} %bitcast.64, bf16[64,128,128]{2,1,0:T(8,128)(2,1)} %bitcast.68, bf16[128,16,128]{2,1,0:T(8,128)(2,1)} %bitcast.72, ...), custom_call_target="tpu_custom_call" | custom-call | flops 1509949440 | bytes 2097152 | tf_op jit(solution)/shard_map/pallas_call | solution.py:115
  20.7 12.2 %shard_map.84 = bf16[16,128,128]{2,1,0:T(8,128)(2,1)} custom-call(s32[3840]{0:T(1024)} %reshape_squeeze.6.idx_ref, s32[64]{0:T(128)} %bitcast.100, s32[4]{0:T(128)} %broadcast_minimum_fusion.nsl_ref, bf16[64,128,128]{2,1,0:T(8,128)(2,1)} %bitcast.65, bf16[64,128,128]{2,1,0:T(8,128)(2,1)} %bitcast.69, bf16[128,16,128]{2,1,0:T(8,128)(2,1)} %bitcast.73, ...), custom_call_target="tpu_custom_call" | custom-call | flops 1509949440 | bytes 2097152 | tf_op jit(solution)/shard_map/pallas_call | solution.py:115
  32.8 12.2 %shard_map.85 = bf16[16,128,128]{2,1,0:T(8,128)(2,1)} custom-call(s32[3840]{0:T(1024)} %reshape_squeeze.6.idx_ref, s32[64]{0:T(128)} %bitcast.101, s32[4]{0:T(128)} %broadcast_minimum_fusion.nsl_ref, bf16[64,128,128]{2,1,0:T(8,128)(2,1)} %bitcast.66, bf16[64,128,128]{2,1,0:T(8,128)(2,1)} %bitcast.70, bf16[128,16,128]{2,1,0:T(8,128)(2,1)} %bitcast.74, ...), custom_call_target="tpu_custom_call" | custom-call | flops 1509949440 | bytes 2097152 | tf_op jit(solution)/shard_map/pallas_call | solution.py:115
  45.0 12.5 %shard_map.82 = bf16[16,128,128]{2,1,0:T(8,128)(2,1)} custom-call(s32[3840]{0:T(1024)} %reshape_squeeze.6.idx_ref, s32[64]{0:T(128)} %bitcast.102, s32[4]{0:T(128)} %broadcast_minimum_fusion.nsl_ref, bf16[64,128,128]{2,1,0:T(8,128)(2,1)} %bitcast.67, bf16[64,128,128]{2,1,0:T(8,128)(2,1)} %bitcast.71, bf16[128,16,128]{2,1,0:T(8,128)(2,1)} %bitcast.75, ...), custom_call_target="tpu_custom_call" | custom-call | flops 1509949440 | bytes 2097152 | tf_op jit(solution)/shard_map/pallas_call | solution.py:115
  57.5 1.3 pad_maximum_fusion
  61.8 1.2 pad_maximum_fusion.1
  63.0 1.9 %fusion.3 = f32[1,64,64]{2,1,0:T(8,128)S(1)} fusion(bf16[64,16384]{1,0:T(8,128)(2,1)S(1)} %constant_dynamic-update-slice_fusion.refs_0_, bf16[8,8,128,128]{3,2,1,0:T(8,128)(2,1)S(1)} %bitcast.91), kind=kOutput, calls=%fused_computation.6 | convolution fusion | flops 134217728 | bytes 4210688 | tf_op jit(solution)/shard_map/fn,gn->fg/dot_general | solution.py:269
  66.7 1.1 copy.50
  67.9 2.2 %collective-permute-start.10 = (bf16[16,16384]{1,0:T(8,128)(2,1)}, bf16[16,16384]{1,0:T(8,128)(2,1)S(1)}, u32[]{:S(2)}, u32[]{:S(2)}) collective-permute-start(bf16[16,16384]{1,0:T(8,128)(2,1)} %bitcast.60), channel_id=1, source_target_pairs={{1,0},{2,1},{3,2},{4,3},{5,4},{6,5},{7,6},{8,7},{9,8},{10,9},{11,1... | collective-permute-start | bytes 1572872 | tf_op jit(solution)/shard_map/ppermute | solution.py:263
  70.1 3.5 %collective-permute-start.2 = (bf16[16,16384]{1,0:T(8,128)(2,1)}, bf16[16,16384]{1,0:T(8,128)(2,1)S(1)}, u32[]{:S(2)}, u32[]{:S(2)}) collective-permute-start(bf16[16,16384]{1,0:T(8,128)(2,1)} %bitcast.60), channel_id=1, source_target_pairs={{0,1},{1,2},{2,3},{3,4},{4,5},{5,6},{6,7},{7,8},{8,9},{9,10},{10,1... | collective-permute-start | bytes 1572872 | tf_op jit(solution)/shard_map/ppermute | solution.py:262
  73.7 1.1 copy.51
  74.8 2.4 %collective-permute-start.1 = (bf16[16,16384]{1,0:T(8,128)(2,1)}, bf16[16,16384]{1,0:T(8,128)(2,1)S(1)}, u32[]{:S(2)}, u32[]{:S(2)}) collective-permute-start(bf16[16,16384]{1,0:T(8,128)(2,1)} %bitcast.61), channel_id=1, source_target_pairs={{0,1},{1,2},{2,3},{3,4},{4,5},{5,6},{6,7},{7,8},{8,9},{9,10},{10,1... | collective-permute-start | bytes 1572872 | tf_op jit(solution)/shard_map/ppermute | solution.py:262
  77.2 1.9 %collective-permute-start.9 = (bf16[16,16384]{1,0:T(8,128)(2,1)}, bf16[16,16384]{1,0:T(8,128)(2,1)S(1)}, u32[]{:S(2)}, u32[]{:S(2)}) collective-permute-start(bf16[16,16384]{1,0:T(8,128)(2,1)} %bitcast.61), channel_id=1, source_target_pairs={{1,0},{2,1},{3,2},{4,3},{5,4},{6,5},{7,6},{8,7},{9,8},{10,9},{11,1... | collective-permute-start | bytes 1572872 | tf_op jit(solution)/shard_map/ppermute | solution.py:263
  80.0 2.6 %collective-permute-done.5 = f32[2,64,64]{2,1,0:T(8,128)S(1)} collective-permute-done((f32[2,64,64]{2,1,0:T(8,128)S(1)}, f32[2,64,64]{2,1,0:T(8,128)S(1)}, u32[]{:S(2)}, u32[]{:S(2)}) %collective-permute-start.5) | collective-permute-done | bytes 32800 | tf_op jit(solution)/shard_map/ppermute | solution.py:246
  83.6 1.1 copy.49
  84.8 1.2 copy.52
  87.0 5.8 %collective-permute-start = (bf16[16,16384]{1,0:T(8,128)(2,1)}, bf16[16,16384]{1,0:T(8,128)(2,1)S(1)}, u32[]{:S(2)}, u32[]{:S(2)}) collective-permute-start(bf16[16,16384]{1,0:T(8,128)(2,1)} %bitcast.95), channel_id=1, source_target_pairs={{0,1},{1,2},{2,3},{3,4},{4,5},{5,6},{6,7},{7,8},{8,9},{9,10},{10,1... | collective-permute-start | bytes 1572872 | tf_op jit(solution)/shard_map/ppermute | solution.py:262
  94.4 1.6 %collective-permute-done.1.refs_2_ = bf16[16,16384]{1,0:T(8,128)(2,1)S(1)} collective-permute-done((bf16[16,16384]{1,0:T(8,128)(2,1)}, bf16[16,16384]{1,0:T(8,128)(2,1)S(1)}, u32[]{:S(2)}, u32[]{:S(2)}) %collective-permute-start.1) | collective-permute-done | bytes 524320 | tf_op jit(solution)/shard_map/ppermute | solution.py:262
  96.0 6.0 %collective-permute-start.8 = (bf16[16,16384]{1,0:T(8,128)(2,1)}, bf16[16,16384]{1,0:T(8,128)(2,1)S(1)}, u32[]{:S(2)}, u32[]{:S(2)}) collective-permute-start(bf16[16,16384]{1,0:T(8,128)(2,1)} %bitcast.96), channel_id=1, source_target_pairs={{1,0},{2,1},{3,2},{4,3},{5,4},{6,5},{7,6},{8,7},{9,8},{10,9},{11,1... | collective-permute-start | bytes 1572872 | tf_op jit(solution)/shard_map/ppermute | solution.py:263
  102.0 4.5 %collective-permute-start.11 = (bf16[16,16384]{1,0:T(8,128)(2,1)}, bf16[16,16384]{1,0:T(8,128)(2,1)}, u32[]{:S(2)}, u32[]{:S(2)}) collective-permute-start(bf16[16,16384]{1,0:T(8,128)(2,1)} %bitcast.93), channel_id=1, source_target_pairs={{1,0},{2,1},{3,2},{4,3},{5,4},{6,5},{7,6},{8,7},{9,8},{10,9},{11,1... | collective-permute-start | bytes 1572872 | tf_op jit(solution)/shard_map/ppermute | solution.py:273
  106.6 2.1 %collective-permute-start.7 = (bf16[16,16384]{1,0:T(8,128)(2,1)}, bf16[16,16384]{1,0:T(8,128)(2,1)}, u32[]{:S(2)}, u32[]{:S(2)}) collective-permute-start(bf16[16,16384]{1,0:T(8,128)(2,1)} %bitcast.94), channel_id=1, source_target_pairs={{0,1},{1,2},{2,3},{3,4},{4,5},{5,6},{6,7},{7,8},{8,9},{9,10},{10,1... | collective-permute-start | bytes 1572872 | tf_op jit(solution)/shard_map/ppermute | solution.py:272
  110.1 7.0 %shard_map.86 = f32[128,128]{1,0:T(8,128)} custom-call(f32[128,128]{1,0:T(8,128)} %get-tuple-element.11.a_ref, f32[128,128]{1,0:T(8,128)} %fusion.6.x0_ref, f32[128,128]{1,0:T(8,128)} %get-tuple-element.12.s_ref), custom_call_target="tpu_custom_call" | custom-call | tf_op jit(solution)/shard_map/pallas_call | solution.py:231
  117.1 0.9 copy.19
  118.8 5.5 %collective-permute-done.11.refs_8_ = bf16[16,16384]{1,0:T(8,128)(2,1)} collective-permute-done((bf16[16,16384]{1,0:T(8,128)(2,1)}, bf16[16,16384]{1,0:T(8,128)(2,1)}, u32[]{:S(2)}, u32[]{:S(2)}) %collective-permute-start.11) | collective-permute-done | bytes 524320 | tf_op jit(solution)/shard_map/ppermute | solution.py:273
  124.3 13.2 %shard_map.87 = bf16[64,16384]{1,0:T(8,128)(2,1)} custom-call(bf16[64,16384]{1,0:T(8,128)(2,1)} %copy-done, bf16[16,16384]{1,0:T(8,128)(2,1)} %copy-done.10, bf16[16,16384]{1,0:T(8,128)(2,1)} %copy-done.8, bf16[16,16384]{1,0:T(8,128)(2,1)} %copy-done.7, bf16[16,16384]{1,0:T(8,128)(2,1)} %collective-permute-done.7.refs_4_, bf16[16,16384]{1,0:T(8,128)(2,1)} %copy-done.11, ...), custom_call_target="tpu_custom_call" | custom-call | flops 1610612736 | bytes 8388608 | tf_op jit(solution)/shard_map/pallas_call | solution.py:193
  137.5 3.5 %copy.29 = bf16[8,8,128,128]{3,2,1,0:T(8,128)(2,1)} copy(bf16[8,8,128,128]{3,1,2,0:T(8,128)(2,1)} %bitcast.82) | data formatting | bytes 4194304
  (71 shorter events, 11.8 us)
Async XLA Ops:
  1.0 3.5 %copy-start.12 = (bf16[1,16,128,128]{3,2,1,0:T(8,128)(2,1)S(1)}, bf16[1,16,128,128]{3,2,1,0:T(8,128)(2,1)}, u32[]{:S(2)}) copy-start(bf16[1,16,128,128]{3,2,1,0:T(8,128)(2,1)} %param.10) | copy-start | bytes 1572868
  2.0 3.6 %copy-start.1 = (bf16[5,2,128,128]{3,2,1,0:T(8,128)(2,1)S(1)}, bf16[5,2,128,128]{3,2,1,0:T(8,128)(2,1)}, u32[]{:S(2)}) copy-start(bf16[5,2,128,128]{3,2,1,0:T(8,128)(2,1)} %param.13) | copy-start | bytes 983044
  2.0 5.1 %copy-start.14 = (s32[1,64]{1,0:T(1,128)S(1)}, s32[1,64]{1,0:T(1,128)}, u32[]{:S(2)}) copy-start(s32[1,64]{1,0:T(1,128)} %param.11) | copy-start | bytes 772
  45.0 12.5 %copy-start.3 = (bf16[16,128,128]{2,1,0:T(8,128)(2,1)S(1)}, bf16[16,128,128]{2,1,0:T(8,128)(2,1)}, u32[]{:S(2)}) copy-start(bf16[16,128,128]{2,1,0:T(8,128)(2,1)} %shard_map.85) | copy-start | bytes 1572868
  45.0 12.5 %copy-start.4 = (bf16[16,128,128]{2,1,0:T(8,128)(2,1)S(1)}, bf16[16,128,128]{2,1,0:T(8,128)(2,1)}, u32[]{:S(2)}) copy-start(bf16[16,128,128]{2,1,0:T(8,128)(2,1)} %shard_map.83) | copy-start | bytes 1572868
  45.0 12.5 %copy-start.5 = (bf16[16,128,128]{2,1,0:T(8,128)(2,1)S(1)}, bf16[16,128,128]{2,1,0:T(8,128)(2,1)}, u32[]{:S(2)}) copy-start(bf16[16,128,128]{2,1,0:T(8,128)(2,1)} %shard_map.84) | copy-start | bytes 1572868
  58.8 1.0 copy-start.2
  61.1 1.9 %copy-start = (bf16[64,16384]{1,0:T(8,128)(2,1)}, bf16[64,16384]{1,0:T(8,128)(2,1)S(1)}, u32[]{:S(2)}) copy-start(bf16[64,16384]{1,0:T(8,128)(2,1)S(1)} %constant_dynamic-update-slice_fusion.refs_0_) | copy-start | bytes 6291460
  65.0 14.8 %copy-start.13 = (bf16[3,2,64,64]{3,2,1,0:T(8,128)(2,1)S(1)}, bf16[3,2,64,64]{3,2,1,0:T(8,128)(2,1)}, u32[]{:S(2)}) copy-start(bf16[3,2,64,64]{3,2,1,0:T(8,128)(2,1)} %param.14) | copy-start | bytes 147460
  65.0 1.6 %collective-permute-start.3 = (f32[2,64,64]{2,1,0:T(8,128)S(1)}, f32[2,64,64]{2,1,0:T(8,128)S(1)}, u32[]{:S(2)}, u32[]{:S(2)}) collective-permute-start(f32[2,64,64]{2,1,0:T(8,128)S(1)} %pad_maximum_fusion.3), channel_id=1, source_target_pairs={{0,1},{1,0},{2,3},{3,2},{4,5},{5,4},{6,7},{7,6},{8,9},{9,8},{10,11... | collective-permute-start | bytes 98312 | tf_op jit(solution)/shard_map/ppermute | solution.py:246
  66.6 12.5 %collective-permute-start.4 = (f32[2,64,64]{2,1,0:T(8,128)S(1)}, f32[2,64,64]{2,1,0:T(8,128)S(1)}, u32[]{:S(2)}, u32[]{:S(2)}) collective-permute-start(f32[2,64,64]{2,1,0:T(8,128)S(1)} %fusion.7), channel_id=1, source_target_pairs={{0,2},{1,3},{2,0},{3,1},{4,6},{5,7},{6,4},{7,5},{8,10},{9,11},{10,... | collective-permute-start | bytes 98312 | tf_op jit(solution)/shard_map/ppermute | solution.py:246
  67.9 34.1 %collective-permute-start.10 = (bf16[16,16384]{1,0:T(8,128)(2,1)}, bf16[16,16384]{1,0:T(8,128)(2,1)S(1)}, u32[]{:S(2)}, u32[]{:S(2)}) collective-permute-start(bf16[16,16384]{1,0:T(8,128)(2,1)} %bitcast.60), channel_id=1, source_target_pairs={{1,0},{2,1},{3,2},{4,3},{5,4},{6,5},{7,6},{8,7},{9,8},{10,9},{11,1... | collective-permute-start | bytes 1572872 | tf_op jit(solution)/shard_map/ppermute | solution.py:263
  70.1 36.4 %collective-permute-start.2 = (bf16[16,16384]{1,0:T(8,128)(2,1)}, bf16[16,16384]{1,0:T(8,128)(2,1)S(1)}, u32[]{:S(2)}, u32[]{:S(2)}) collective-permute-start(bf16[16,16384]{1,0:T(8,128)(2,1)} %bitcast.60), channel_id=1, source_target_pairs={{0,1},{1,2},{2,3},{3,4},{4,5},{5,6},{6,7},{7,8},{8,9},{9,10},{10,1... | collective-permute-start | bytes 1572872 | tf_op jit(solution)/shard_map/ppermute | solution.py:262
  74.8 21.2 %collective-permute-start.1 = (bf16[16,16384]{1,0:T(8,128)(2,1)}, bf16[16,16384]{1,0:T(8,128)(2,1)S(1)}, u32[]{:S(2)}, u32[]{:S(2)}) collective-permute-start(bf16[16,16384]{1,0:T(8,128)(2,1)} %bitcast.61), channel_id=1, source_target_pairs={{0,1},{1,2},{2,3},{3,4},{4,5},{5,6},{6,7},{7,8},{8,9},{9,10},{10,1... | collective-permute-start | bytes 1572872 | tf_op jit(solution)/shard_map/ppermute | solution.py:262
  77.2 41.5 %collective-permute-start.9 = (bf16[16,16384]{1,0:T(8,128)(2,1)}, bf16[16,16384]{1,0:T(8,128)(2,1)S(1)}, u32[]{:S(2)}, u32[]{:S(2)}) collective-permute-start(bf16[16,16384]{1,0:T(8,128)(2,1)} %bitcast.61), channel_id=1, source_target_pairs={{1,0},{2,1},{3,2},{4,3},{5,4},{6,5},{7,6},{8,7},{9,8},{10,9},{11,1... | collective-permute-start | bytes 1572872 | tf_op jit(solution)/shard_map/ppermute | solution.py:263
  79.2 3.5 %collective-permute-start.5 = (f32[2,64,64]{2,1,0:T(8,128)S(1)}, f32[2,64,64]{2,1,0:T(8,128)S(1)}, u32[]{:S(2)}, u32[]{:S(2)}) collective-permute-start(f32[2,64,64]{2,1,0:T(8,128)S(1)} %fusion.13), channel_id=1, source_target_pairs={{0,4},{1,5},{2,6},{3,7},{4,0},{5,1},{6,2},{7,3},{8,12},{9,13},{10,... | collective-permute-start | bytes 98312 | tf_op jit(solution)/shard_map/ppermute | solution.py:246
  82.7 4.4 %collective-permute-start.6 = (f32[2,64,64]{2,1,0:T(8,128)S(1)}, f32[2,64,64]{2,1,0:T(8,128)S(1)}, u32[]{:S(2)}, u32[]{:S(2)}) collective-permute-start(f32[2,64,64]{2,1,0:T(8,128)S(1)} %add.20), channel_id=1, source_target_pairs={{0,8},{1,9},{2,10},{3,11},{4,12},{5,13},{6,14},{7,15},{8,0},{9,1},... | collective-permute-start | bytes 98312 | tf_op jit(solution)/shard_map/ppermute | solution.py:246
  87.0 31.7 %collective-permute-start = (bf16[16,16384]{1,0:T(8,128)(2,1)}, bf16[16,16384]{1,0:T(8,128)(2,1)S(1)}, u32[]{:S(2)}, u32[]{:S(2)}) collective-permute-start(bf16[16,16384]{1,0:T(8,128)(2,1)} %bitcast.95), channel_id=1, source_target_pairs={{0,1},{1,2},{2,3},{3,4},{4,5},{5,6},{6,7},{7,8},{8,9},{9,10},{10,1... | collective-permute-start | bytes 1572872 | tf_op jit(solution)/shard_map/ppermute | solution.py:262
  96.0 28.3 %copy-start.8 = (bf16[16,16384]{1,0:T(8,128)(2,1)}, bf16[16,16384]{1,0:T(8,128)(2,1)S(1)}, u32[]{:S(2)}) copy-start(bf16[16,16384]{1,0:T(8,128)(2,1)S(1)} %collective-permute-done.1.refs_2_) | copy-start | bytes 1572868
  96.0 22.8 %collective-permute-start.8 = (bf16[16,16384]{1,0:T(8,128)(2,1)}, bf16[16,16384]{1,0:T(8,128)(2,1)S(1)}, u32[]{:S(2)}, u32[]{:S(2)}) collective-permute-start(bf16[16,16384]{1,0:T(8,128)(2,1)} %bitcast.96), channel_id=1, source_target_pairs={{1,0},{2,1},{3,2},{4,3},{5,4},{6,5},{7,6},{8,7},{9,8},{10,9},{11,1... | collective-permute-start | bytes 1572872 | tf_op jit(solution)/shard_map/ppermute | solution.py:263
  102.0 22.3 %copy-start.6 = (bf16[16,16384]{1,0:T(8,128)(2,1)}, bf16[16,16384]{1,0:T(8,128)(2,1)S(1)}, u32[]{:S(2)}) copy-start(bf16[16,16384]{1,0:T(8,128)(2,1)S(1)} %collective-permute-done.10.refs_7_) | copy-start | bytes 1572868
  102.0 22.3 %collective-permute-start.11 = (bf16[16,16384]{1,0:T(8,128)(2,1)}, bf16[16,16384]{1,0:T(8,128)(2,1)}, u32[]{:S(2)}, u32[]{:S(2)}) collective-permute-start(bf16[16,16384]{1,0:T(8,128)(2,1)} %bitcast.93), channel_id=1, source_target_pairs={{1,0},{2,1},{3,2},{4,3},{5,4},{6,5},{7,6},{8,7},{9,8},{10,9},{11,1... | collective-permute-start | bytes 1572872 | tf_op jit(solution)/shard_map/ppermute | solution.py:273
  106.6 17.7 %copy-start.7 = (bf16[16,16384]{1,0:T(8,128)(2,1)}, bf16[16,16384]{1,0:T(8,128)(2,1)S(1)}, u32[]{:S(2)}) copy-start(bf16[16,16384]{1,0:T(8,128)(2,1)S(1)} %collective-permute-done.2.refs_3_) | copy-start | bytes 1572868
  106.6 17.7 %collective-permute-start.7 = (bf16[16,16384]{1,0:T(8,128)(2,1)}, bf16[16,16384]{1,0:T(8,128)(2,1)}, u32[]{:S(2)}, u32[]{:S(2)}) collective-permute-start(bf16[16,16384]{1,0:T(8,128)(2,1)} %bitcast.94), channel_id=1, source_target_pairs={{0,1},{1,2},{2,3},{3,4},{4,5},{5,6},{6,7},{7,8},{8,9},{9,10},{10,1... | collective-permute-start | bytes 1572872 | tf_op jit(solution)/shard_map/ppermute | solution.py:272
  118.7 5.6 %copy-start.9 = (bf16[16,16384]{1,0:T(8,128)(2,1)}, bf16[16,16384]{1,0:T(8,128)(2,1)S(1)}, u32[]{:S(2)}) copy-start(bf16[16,16384]{1,0:T(8,128)(2,1)S(1)} %collective-permute-done.9.refs_6_) | copy-start | bytes 1572868
  118.7 5.6 %copy-start.10 = (bf16[16,16384]{1,0:T(8,128)(2,1)}, bf16[16,16384]{1,0:T(8,128)(2,1)S(1)}, u32[]{:S(2)}) copy-start(bf16[16,16384]{1,0:T(8,128)(2,1)S(1)} %collective-permute-done.refs_1_) | copy-start | bytes 1572868
  118.8 5.6 %copy-start.11 = (bf16[16,16384]{1,0:T(8,128)(2,1)}, bf16[16,16384]{1,0:T(8,128)(2,1)S(1)}, u32[]{:S(2)}) copy-start(bf16[16,16384]{1,0:T(8,128)(2,1)S(1)} %collective-permute-done.8.refs_5_) | copy-start | bytes 1572868

commit v4 on v2

--- a/solution.py
+++ b/solution.py
@@ -309,12 +309,61 @@
     count = lax.axis_size(axis)
     if count & (count - 1):
         return lax.psum(value, axis)
+    me = lax.axis_index(axis)
     step = 1
     while step < count:
-        pairs = [(i, i ^ step) for i in range(count)]
-        value = value + lax.ppermute(value, axis, pairs)
-        step *= 2
+        if step * 4 <= count:
+            got = [value] + [
+                lax.ppermute(value, axis, [(i, i ^ (k * step)) for i in range(count)])
+                for k in range(1, 4)
+            ]
+            digit = (me // step) % 4
+            ordered = []
+            for j in range(4):
+                picked = got[0]
+                for k in range(1, 4):
+                    picked = jnp.where((digit ^ j) == k, got[k], picked)
+                ordered.append(picked)
+            value = (ordered[0] + ordered[1]) + (ordered[2] + ordered[3])
+            step *= 4
+        else:
+            value = value + lax.ppermute(value, axis, [(i, i ^ step) for i in range(count)])
+            step *= 2
     return value
+
+
+def gram_kernel(x_ref, out_ref):
+    frames, width = x_ref.shape
+    step = pl.program_id(0)
+
+    @pl.when(step == 0)
+    def _():
+        out_ref[...] = jnp.zeros_like(out_ref)
+
+    x = x_ref[...]
+    wide = x.astype(jnp.float32)
+    low_lane = lax.broadcasted_iota(jnp.int32, (frames, width), 1) % 128 < 64
+    turned = jnp.where(low_lane, -pltpu.roll(wide, width - 64, 1), pltpu.roll(wide, 64, 1))
+    turned = turned.astype(jnp.bfloat16)
+    pairs = (((1,), (1,)), ((), ()))
+    out_ref[0] += lax.dot_general(x, x, pairs, preferred_element_type=jnp.float32)
+    out_ref[1] += lax.dot_general(turned, x, pairs, preferred_element_type=jnp.float32)
+
+
+def gram_of(flat):
+    frames, width = flat.shape
+    nb = 2048 if width % 2048 == 0 else width
+    return pl.pallas_call(
+        gram_kernel,
+        out_shape=jax.ShapeDtypeStruct((2, frames, frames), jnp.float32),
+        grid=(width // nb,),
+        in_specs=[pl.BlockSpec((frames, nb), lambda i: (0, i))],
+        out_specs=pl.BlockSpec((2, frames, frames), lambda i: (0, 0, 0)),
+        compiler_params=pltpu.CompilerParams(dimension_semantics=("arbitrary",)),
+        cost_estimate=pl.CostEstimate(
+            flops=4 * frames * frames * width, transcendentals=0, bytes_accessed=flat.size * 2
+        ),
+    )(flat)
 
 
 def mix_frames(weights, field_values):
@@ -332,11 +381,7 @@
     forward = [(i, i + 1) for i in range(count - 1)]
     backward = [(target, source) for source, target in forward]
     flat = fresh.reshape(frame_count, -1)
-    rows_real = flat
-    rows_turned = rotate(fresh).reshape(frame_count, -1)
-    gram_real = jnp.einsum("fn,gn->fg", rows_real, rows_real, preferred_element_type=jnp.float32)
-    gram_imag = jnp.einsum("fn,gn->fg", rows_turned, rows_real, preferred_element_type=jnp.float32)
-    gram_real, gram_imag = tree_sum(jnp.stack([gram_real, gram_imag]), "dom")
+    gram_real, gram_imag = tree_sum(gram_of(flat), "dom")
     flat, gram_real, gram_imag = lax.optimization_barrier((flat, gram_real, gram_imag))
     fresh_before = lax.ppermute(flat, "dom", forward)
     fresh_after = lax.ppermute(flat, "dom", backward)

time: 139 us -> 142 us (1.022)
  Pallas kernels: 58.4 us -> 64.7 us
  matrix products: 4.84 us -> 0 us
  local copies, waits for them, and re-layouts: 12.1 us -> 15.2 us
  other arithmetic: 10.1 us -> 7.26 us
  starting transfers between devices: 8.78 us -> 10.5 us
    ppermute x1, waiting for transfers between devices: 30.2 us -> 0.01 us  [local(): fresh_before = lax.ppermute(flat, 'dom', forward)]
    ppermute x1, waiting for transfers between devices: 3.01 us -> 31.5 us  [local(): fresh_after = lax.ppermute(flat, 'dom', backward)]
    pallas_call x0 -> x1, Pallas kernels: none -> 6.22 us  [gram_of(): pl.pallas_call(gram_kernel, out_shape=jax.ShapeDtypeStruct((2, frames, fr...]
    dot_general x2 -> x0, matrix products: 4.84 us -> none  [the longest x1 2.42 us: local(): jnp.einsum('fn,gn->fg', rows_turned, rows_real, preferred_element_type=jn...]
    ppermute x4 -> x6, starting transfers between devices: 0.96 us -> 4.97 us  [tree_sum(): lax.ppermute(value, axis, [(i, i ^ k * step) for i in range(count)])]
    neg x2 -> x1, other arithmetic: 4.27 us -> 1.03 us  [rotate(): -field_values[..., half_width:]]
    ppermute x1, starting transfers between devices: 5.49 us -> 2.76 us  [local(): fresh_before = lax.ppermute(flat, 'dom', forward)]
    unnamed x17 -> x13, local copies, waits for them, and re-layouts: 8.08 us -> 10.2 us
  transfers between devices with their start and end apart: 6 -> 8, of which waited for: 6 -> 6; matrix products, arithmetic and copies ran while one was open for 4% -> 3% of each run, Pallas kernels for 5% -> 5%
where the time goes in v4:
time: 142 us; the launch traced here: 141 us
  Pallas kernels  64.7 us (46%)
  waiting for transfers between devices  41.6 us (29%)
  local copies, waits for them, and re-layouts  15.2 us (11%)
  starting transfers between devices  10.5 us (7%)
  other arithmetic  7.26 us (5%)
  between operations  1.49 us (1%)
    pallas_call x1, Pallas kernels, fresh_image_of(): pl.pallas_call(kernel, out_shape=jax.ShapeDtypeStruct(image_plane.shape,...  38.5 us
    ppermute x1, waiting for transfers between devices, local(): fresh_after = lax.ppermute(flat, 'dom', backward)  31.5 us
    pallas_call x1, Pallas kernels, post_of(): pl.pallas_call(functools.partial(post_kernel, cut=SOFT_CUT), out_shape=ja...  13.1 us
    unnamed x13, local copies, waits for them, and re-layouts  10.2 us
    ppermute x6, waiting for transfers between devices, tree_sum(): lax.ppermute(value, axis, [(i, i ^ k * step) for i in range(count)])  10 us
    pallas_call x1, Pallas kernels, shrink_of(): pl.pallas_call(functools.partial(solve_kernel, steps=12), out_shape=jax.S...  6.94 us
    pallas_call x1, Pallas kernels, gram_of(): pl.pallas_call(gram_kernel, out_shape=jax.ShapeDtypeStruct((2, frames, fr...  6.22 us
    ppermute x6, starting transfers between devices, tree_sum(): lax.ppermute(value, axis, [(i, i ^ k * step) for i in range(count)])  4.97 us
  transfers between devices with their start and end apart: 8, of which 6 were waited for; matrix products, arithmetic and copies ran while one was open for 3% of the time, Pallas kernels for 5%

profile of v4, /device:TPU:19, one launch (start us, length us, event | category | flops | bytes accessed | tf_op | source)
XLA Modules:
  0.0 140.8 jit_solution(369753282230011318)
XLA Ops:
  0.5 1.3 reduce.3
  2.6 1.9 %copy.22.bt_ref = bf16[5,128,256]{2,1,0:T(8,128)(2,1)} copy(bf16[5,128,256]{1,2,0:T(8,128)(2,1)} %bitcast.37) | data formatting | bytes 655360 | tf_op jit(solution)/shard_map/reshape | solution.py:167
  4.5 1.0 slice_negate_fusion
  5.6 0.9 copy.23.btr_ref
  6.5 1.1 copy.29
  7.6 0.8 copy.15
  8.4 0.9 reshape_squeeze.6.idx_ref
  9.3 38.5 %shard_map.82 = bf16[64,128,128]{2,1,0:T(8,128)(2,1)} custom-call(s32[3840]{0:T(1024)} %reshape_squeeze.6.idx_ref, s32[64]{0:T(128)} %bitcast.46, s32[4]{0:T(128)} %broadcast_minimum_fusion.nsl_ref, bf16[64,128,128]{2,1,0:T(8,128)(2,1)} %bitcast.44, bf16[64,128,128]{2,1,0:T(8,128)(2,1)} %bitcast.45, bf16[128,16,128]{2,1,0:T(8,128)(2,1)} %bitcast.41, ...), custom_call_target="tpu_custom_call" | custom-call | flops 6039797760 | bytes 6815744 | tf_op jit(solution)/shard_map/pallas_call | solution.py:178
  47.8 4.3 %copy.28 = bf16[8,8,128,128]{3,1,2,0:T(8,128)(2,1)} copy(bf16[8,8,128,128]{3,2,1,0:T(8,128)(2,1)} %bitcast.36) | data formatting | bytes 4194304
  52.1 6.2 %shard_map.83 = f32[2,64,64]{2,1,0:T(8,128)} custom-call(bf16[64,16384]{1,0:T(8,128)(2,1)} %bitcast.31), custom_call_target="tpu_custom_call" | custom-call | flops 268435456 | bytes 2097152 | tf_op jit(solution)/shard_map/pallas_call | solution.py:356
  58.3 0.6 collective-permute-start.2
  59.0 1.6 %collective-permute-start = (f32[2,64,64]{2,1,0:T(8,128)}, f32[2,64,64]{2,1,0:T(8,128)S(1)}, u32[]{:S(2)}, u32[]{:S(2)}) collective-permute-start(f32[2,64,64]{2,1,0:T(8,128)} %shard_map.83), channel_id=1, source_target_pairs={{0,3},{1,2},{2,1},{3,0},{4,7},{5,6},{6,5},{7,4},{8,11},{9,10},{10,... | collective-permute-start | bytes 98312 | tf_op jit(solution)/shard_map/ppermute | solution.py:317
  60.6 2.2 %collective-permute-done.1 = f32[2,64,64]{2,1,0:T(8,128)S(1)} collective-permute-done((f32[2,64,64]{2,1,0:T(8,128)}, f32[2,64,64]{2,1,0:T(8,128)S(1)}, u32[]{:S(2)}, u32[]{:S(2)}) %collective-permute-start.1) | collective-permute-done | bytes 32800 | tf_op jit(solution)/shard_map/ppermute | solution.py:317
  62.8 1.6 %collective-permute-done = f32[2,64,64]{2,1,0:T(8,128)S(1)} collective-permute-done((f32[2,64,64]{2,1,0:T(8,128)}, f32[2,64,64]{2,1,0:T(8,128)S(1)}, u32[]{:S(2)}, u32[]{:S(2)}) %collective-permute-start) | collective-permute-done | bytes 32800 | tf_op jit(solution)/shard_map/ppermute | solution.py:317
  64.4 0.9 add_add_fusion.1
  65.3 1.3 collective-permute-start.4
  66.6 1.4 collective-permute-start.3
  68.0 0.8 collective-permute-done.5
  68.8 1.7 %collective-permute-done.4 = f32[2,64,64]{2,1,0:T(8,128)S(1)} collective-permute-done((f32[2,64,64]{2,1,0:T(8,128)S(1)}, f32[2,64,64]{2,1,0:T(8,128)S(1)}, u32[]{:S(2)}, u32[]{:S(2)}) %collective-permute-start.4) | collective-permute-done | bytes 32800 | tf_op jit(solution)/shard_map/ppermute | solution.py:317
  70.4 3.8 %collective-permute-done.3 = f32[2,64,64]{2,1,0:T(8,128)S(1)} collective-permute-done((f32[2,64,64]{2,1,0:T(8,128)S(1)}, f32[2,64,64]{2,1,0:T(8,128)S(1)}, u32[]{:S(2)}, u32[]{:S(2)}) %collective-permute-start.3) | collective-permute-done | bytes 32800 | tf_op jit(solution)/shard_map/ppermute | solution.py:317
  74.3 2.8 %collective-permute-start.7 = (bf16[64,16384]{1,0:T(8,128)(2,1)S(1)}, bf16[64,16384]{1,0:T(8,128)(2,1)}, u32[]{:S(2)}, u32[]{:S(2)}) collective-permute-start(bf16[64,16384]{1,0:T(8,128)(2,1)S(1)} %bitcast.33), channel_id=1, source_target_pairs={{1,0},{2,1},{3,2},{4,3},{5,4},{6,5},{7,6},{8,7},{9,8},{10,9},{11,1... | collective-permute-start | bytes 6291464 | tf_op jit(solution)/shard_map/ppermute | solution.py:387
  77.1 2.8 %collective-permute-start.6 = (bf16[64,16384]{1,0:T(8,128)(2,1)S(1)}, bf16[64,16384]{1,0:T(8,128)(2,1)}, u32[]{:S(2)}, u32[]{:S(2)}) collective-permute-start(bf16[64,16384]{1,0:T(8,128)(2,1)S(1)} %bitcast.34), channel_id=1, source_target_pairs={{0,1},{1,2},{2,3},{3,4},{4,5},{5,6},{6,7},{7,8},{8,9},{9,10},{10,1... | collective-permute-start | bytes 6291464 | tf_op jit(solution)/shard_map/ppermute | solution.py:386
  80.8 0.6 maximum_bitcast_fusion.wz_ref
  81.4 0.6 select_reduce_fusion
  82.7 0.6 fusion.x0_ref
  83.4 0.7 select_add_fusion
  84.1 6.9 %shard_map.84 = f32[128,128]{1,0:T(8,128)} custom-call(f32[128,128]{1,0:T(8,128)} %get-tuple-element.11.a_ref, f32[128,128]{1,0:T(8,128)} %fusion.x0_ref, f32[128,128]{1,0:T(8,128)} %get-tuple-element.12.s_ref), custom_call_target="tpu_custom_call" | custom-call | tf_op jit(solution)/shard_map/pallas_call | solution.py:284
  91.0 0.9 copy.19
  92.1 0.6 maximum_bitcast_fusion.1.wl_ref
  92.7 31.5 %collective-permute-done.7.xa_ref = bf16[64,16384]{1,0:T(8,128)(2,1)} collective-permute-done((bf16[64,16384]{1,0:T(8,128)(2,1)S(1)}, bf16[64,16384]{1,0:T(8,128)(2,1)}, u32[]{:S(2)}, u32[]{:S(2)}) %collective-permute-start.7) | collective-permute-done | bytes 2097184 | tf_op jit(solution)/shard_map/ppermute | solution.py:387
  124.2 13.1 %shard_map.85 = bf16[64,16384]{1,0:T(8,128)(2,1)} custom-call(bf16[64,16384]{1,0:T(8,128)(2,1)} %bitcast.32, bf16[64,16384]{1,0:T(8,128)(2,1)} %collective-permute-done.6.xb_ref, bf16[64,16384]{1,0:T(8,128)(2,1)} %collective-permute-done.7.xa_ref, bf16[128,64]{1,0:T(8,128)(2,1)} %maximum_bitcast_fusion.1.wl_ref, bf16[128,192]{1,0:T(8,128)(2,1)} %maximum_bitcast_fusion.wz_ref), custom_call_target="tpu_custom_call" | custom-call | flops 1610612736 | bytes 8388608 | tf_op jit(solution)/shard_map/pallas_call | solution.py:246
  137.3 3.5 %copy.25 = bf16[8,8,128,128]{3,2,1,0:T(8,128)(2,1)} copy(bf16[8,8,128,128]{3,1,2,0:T(8,128)(2,1)} %bitcast.35) | data formatting | bytes 4194304
  (24 shorter events, 1.7 us)
Async XLA Ops:
  0.0 6.5 %copy-start.1 = (bf16[1,16,128,128]{3,2,1,0:T(8,128)(2,1)S(1)}, bf16[1,16,128,128]{3,2,1,0:T(8,128)(2,1)}, u32[]{:S(2)}) copy-start(bf16[1,16,128,128]{3,2,1,0:T(8,128)(2,1)} %param.10) | copy-start | bytes 1572868
  0.0 7.6 %copy-start.3 = (s32[1,64,6,5,2]{1,4,3,2,0:T(2,128)S(1)}, s32[1,64,6,5,2]{1,4,3,2,0:T(2,128)}, u32[]{:S(2)}) copy-start(s32[1,64,6,5,2]{1,4,3,2,0:T(2,128)} %param.12) | copy-start | bytes 46084
  52.1 22.2 %copy-start = (bf16[8,8,128,128]{3,1,2,0:T(8,128)(2,1)S(1)}, bf16[8,8,128,128]{3,1,2,0:T(8,128)(2,1)}, u32[]{:S(2)}) copy-start(bf16[8,8,128,128]{3,1,2,0:T(8,128)(2,1)} %copy.28) | copy-start | bytes 6291460
  52.1 28.4 %copy-start.2 = (bf16[3,2,64,64]{3,2,1,0:T(8,128)(2,1)S(1)}, bf16[3,2,64,64]{3,2,1,0:T(8,128)(2,1)}, u32[]{:S(2)}) copy-start(bf16[3,2,64,64]{3,2,1,0:T(8,128)(2,1)} %param.14) | copy-start | bytes 147460
  58.3 2.3 %collective-permute-start.2 = (f32[2,64,64]{2,1,0:T(8,128)}, f32[2,64,64]{2,1,0:T(8,128)S(1)}, u32[]{:S(2)}, u32[]{:S(2)}) collective-permute-start(f32[2,64,64]{2,1,0:T(8,128)} %shard_map.83), channel_id=1, source_target_pairs={{0,1},{1,0},{2,3},{3,2},{4,5},{5,4},{6,7},{7,6},{8,9},{9,8},{10,11... | collective-permute-start | bytes 98312 | tf_op jit(solution)/shard_map/ppermute | solution.py:317
  59.0 3.9 %collective-permute-start.1 = (f32[2,64,64]{2,1,0:T(8,128)}, f32[2,64,64]{2,1,0:T(8,128)S(1)}, u32[]{:S(2)}, u32[]{:S(2)}) collective-permute-start(f32[2,64,64]{2,1,0:T(8,128)} %shard_map.83), channel_id=1, source_target_pairs={{0,2},{1,3},{2,0},{3,1},{4,6},{5,7},{6,4},{7,5},{8,10},{9,11},{10,... | collective-permute-start | bytes 98312 | tf_op jit(solution)/shard_map/ppermute | solution.py:317
  59.0 5.4 %collective-permute-start = (f32[2,64,64]{2,1,0:T(8,128)}, f32[2,64,64]{2,1,0:T(8,128)S(1)}, u32[]{:S(2)}, u32[]{:S(2)}) collective-permute-start(f32[2,64,64]{2,1,0:T(8,128)} %shard_map.83), channel_id=1, source_target_pairs={{0,3},{1,2},{2,1},{3,0},{4,7},{5,6},{6,5},{7,4},{8,11},{9,10},{10,... | collective-permute-start | bytes 98312 | tf_op jit(solution)/shard_map/ppermute | solution.py:317
  65.3 3.5 %collective-permute-start.5 = (f32[2,64,64]{2,1,0:T(8,128)S(1)}, f32[2,64,64]{2,1,0:T(8,128)S(1)}, u32[]{:S(2)}, u32[]{:S(2)}) collective-permute-start(f32[2,64,64]{2,1,0:T(8,128)S(1)} %add_add_fusion.1), channel_id=1, source_target_pairs={{0,4},{1,5},{2,6},{3,7},{4,0},{5,1},{6,2},{7,3},{8,12},{9,13},{10,... | collective-permute-start | bytes 98312 | tf_op jit(solution)/shard_map/ppermute | solution.py:317
  65.3 5.1 %collective-permute-start.4 = (f32[2,64,64]{2,1,0:T(8,128)S(1)}, f32[2,64,64]{2,1,0:T(8,128)S(1)}, u32[]{:S(2)}, u32[]{:S(2)}) collective-permute-start(f32[2,64,64]{2,1,0:T(8,128)S(1)} %add_add_fusion.1), channel_id=1, source_target_pairs={{0,8},{1,9},{2,10},{3,11},{4,12},{5,13},{6,14},{7,15},{8,0},{9,1},... | collective-permute-start | bytes 98312 | tf_op jit(solution)/shard_map/ppermute | solution.py:317
  66.6 7.6 %collective-permute-start.3 = (f32[2,64,64]{2,1,0:T(8,128)S(1)}, f32[2,64,64]{2,1,0:T(8,128)S(1)}, u32[]{:S(2)}, u32[]{:S(2)}) collective-permute-start(f32[2,64,64]{2,1,0:T(8,128)S(1)} %add_add_fusion.1), channel_id=1, source_target_pairs={{0,12},{1,13},{2,14},{3,15},{4,8},{5,9},{6,10},{7,11},{8,4},{9,5},... | collective-permute-start | bytes 98312 | tf_op jit(solution)/shard_map/ppermute | solution.py:317
  74.3 49.9 %collective-permute-start.7 = (bf16[64,16384]{1,0:T(8,128)(2,1)S(1)}, bf16[64,16384]{1,0:T(8,128)(2,1)}, u32[]{:S(2)}, u32[]{:S(2)}) collective-permute-start(bf16[64,16384]{1,0:T(8,128)(2,1)S(1)} %bitcast.33), channel_id=1, source_target_pairs={{1,0},{2,1},{3,2},{4,3},{5,4},{6,5},{7,6},{8,7},{9,8},{10,9},{11,1... | collective-permute-start | bytes 6291464 | tf_op jit(solution)/shard_map/ppermute | solution.py:387
  77.1 47.1 %collective-permute-start.6 = (bf16[64,16384]{1,0:T(8,128)(2,1)S(1)}, bf16[64,16384]{1,0:T(8,128)(2,1)}, u32[]{:S(2)}, u32[]{:S(2)}) collective-permute-start(bf16[64,16384]{1,0:T(8,128)(2,1)S(1)} %bitcast.34), channel_id=1, source_target_pairs={{0,1},{1,2},{2,3},{3,4},{4,5},{5,6},{6,7},{7,8},{8,9},{9,10},{10,1... | collective-permute-start | bytes 6291464 | tf_op jit(solution)/shard_map/ppermute | solution.py:386

commit v5 on v2

--- a/solution.py
+++ b/solution.py
@@ -90,8 +90,9 @@
 
 
 def gradient_kernel(idx_ref, cnt_ref, nsl_ref, img_ref, adj_ref, maps_ref,
-                    bf_ref, bt_ref, btr_ref, out_ref, x_scr, rx_scr, g_scr,
-                    lhs_scr, y_scr, ry_scr, mrr_ref, mii_ref, *, fb, slots, links, coils):
+                    bf_ref, bt_ref, btr_ref, out_ref, x_scr, rx_scr, g_scr, g2_scr,
+                    lhs_a, y_a, ry_a, lhs_b, y_b, ry_b, mrr_ref, mii_ref, *, fb, slots, links,
+                    coils):
     b = pl.program_id(0)
     reads = links // 2
     img = img_ref[...].astype(jnp.float32)
@@ -109,10 +110,15 @@
         mrr_ref[...] = jnp.where(map_lane, maps, swapped)
         mii_ref[...] = jnp.where(map_lane, swapped, maps)
     g_scr[...] = jnp.zeros_like(g_scr)
-    lhs_scr[...] = jnp.zeros_like(lhs_scr)
+    g2_scr[...] = jnp.zeros_like(g2_scr)
+    lhs_a[...] = jnp.zeros_like(lhs_a)
+    lhs_b[...] = jnp.zeros_like(lhs_b)
+    accums = (g_scr, g2_scr)
 
     def slot_body(s, carry):
         for q in range(reads):
+            lhs_scr, y_scr, ry_scr = (lhs_a, y_a, ry_a) if q % 2 == 0 else (lhs_b, y_b, ry_b)
+
             def gather_t(t, c):
                 frame = b * fb + t
                 base = (frame * slots + s) * links + q * 2
@@ -144,14 +150,16 @@
                     ryv = ry_scr[pl.ds(row, coils), pl.ds(j * 128, 128)]
                     v = mrr_ref[p] * yv - mii_ref[p] * ryv
                     back = jnp.sum(v, axis=0, keepdims=True) * keep
-                    g_scr[t, pl.ds(p, 1), :] = g_scr[t, pl.ds(p, 1), :] + back
+                    acc = accums[j]
+                    acc[t, pl.ds(p, 1), :] = acc[t, pl.ds(p, 1), :] + back
                 return c
 
             lax.fori_loop(0, fb, scatter_t, 0, unroll=True)
         return carry
 
     lax.fori_loop(0, nsl_ref[b], slot_body, 0)
-    out_ref[...] = (x_scr[...] - (g_scr[...] - adj_ref[...].astype(jnp.float32))).astype(out_ref.dtype)
+    grad = g_scr[...] + g2_scr[...]
+    out_ref[...] = (x_scr[...] - (grad - adj_ref[...].astype(jnp.float32))).astype(out_ref.dtype)
 
 
 def fresh_image_of(image_plane, adjoint_plane, plane_maps, counts, plane_map, blocks):
@@ -194,6 +202,10 @@
                 pltpu.VMEM((fb, tile_count, lane_width), jnp.float32),
                 pltpu.VMEM((fb, tile_count, lane_width), jnp.float32),
                 pltpu.VMEM((fb, tile_count, lane_width), jnp.float32),
+                pltpu.VMEM((fb, tile_count, lane_width), jnp.float32),
+                pltpu.VMEM((fb * coils, links * lane_width), jnp.bfloat16),
+                pltpu.VMEM((fb * coils, links * lane_width), jnp.float32),
+                pltpu.VMEM((fb * coils, links * lane_width), jnp.float32),
                 pltpu.VMEM((fb * coils, links * lane_width), jnp.bfloat16),
                 pltpu.VMEM((fb * coils, links * lane_width), jnp.float32),
                 pltpu.VMEM((fb * coils, links * lane_width), jnp.float32),

time: 139 us -> 139 us (level)
  no operation moved by 1% of the time
where the time goes in v5:
time: 139 us
  Pallas kernels  58.5 us (42%)
  waiting for transfers between devices  43 us (31%)
  local copies, waits for them, and re-layouts  12.1 us (9%)
  other arithmetic  10.1 us (7%)
  starting transfers between devices  8.74 us (6%)
  matrix products  4.84 us (3%)
  between operations  1.58 us (1%)
    pallas_call x1, Pallas kernels, fresh_image_of(): pl.pallas_call(kernel, out_shape=jax.ShapeDtypeStruct(image_plane.shape,...  38.5 us
    ppermute x1, waiting for transfers between devices, local(): fresh_before = lax.ppermute(flat, 'dom', forward)  30.2 us
    pallas_call x1, Pallas kernels, post_of(): pl.pallas_call(functools.partial(post_kernel, cut=SOFT_CUT), out_shape=ja...  13 us
    ppermute x4, waiting for transfers between devices, tree_sum(): value = value + lax.ppermute(value, axis, pairs)  9.71 us
    unnamed x17, local copies, waits for them, and re-layouts  8.08 us
    pallas_call x1, Pallas kernels, shrink_of(): pl.pallas_call(functools.partial(solve_kernel, steps=12), out_shape=jax.S...  6.94 us
    ppermute x1, starting transfers between devices, local(): fresh_before = lax.ppermute(flat, 'dom', forward)  5.49 us
    neg x2, other arithmetic, rotate(): -field_values[..., half_width:]  4.27 us
  transfers between devices with their start and end apart: 6, of which 6 were waited for; matrix products, arithmetic and copies ran while one was open for 4% of the time, Pallas kernels for 5%

profile of v5, /device:TPU:19, one launch (start us, length us, event | category | flops | bytes accessed | tf_op | source)
XLA Modules:
  0.0 138.9 jit_solution(15572221140074364484)
XLA Ops:
  0.0 1.0 slice_negate_fusion.1
  1.1 0.9 copy.31.btr_ref
  2.0 1.5 %copy.19 = s32[1,64,6,5,2]{4,3,2,1,0:T(8,128)S(1)} copy(s32[1,64,6,5,2]{1,4,3,2,0:T(2,128)} %param.12) | data formatting | bytes 30720 | tf_op args[4]
  3.6 0.9 reshape_squeeze.6.idx_ref
  4.5 1.1 copy.49
  5.6 0.9 copy.30.bt_ref
  7.1 0.7 reduce.3
  7.9 0.5 broadcast_minimum_fusion.nsl_ref
  8.5 38.5 %shard_map.82 = bf16[64,128,128]{2,1,0:T(8,128)(2,1)} custom-call(s32[3840]{0:T(1024)} %reshape_squeeze.6.idx_ref, s32[64]{0:T(128)} %bitcast.51, s32[4]{0:T(128)} %broadcast_minimum_fusion.nsl_ref, bf16[64,128,128]{2,1,0:T(8,128)(2,1)} %bitcast.49, bf16[64,128,128]{2,1,0:T(8,128)(2,1)} %bitcast.50, bf16[128,16,128]{2,1,0:T(8,128)(2,1)} %bitcast.46, ...), custom_call_target="tpu_custom_call" | custom-call | flops 6039797760 | bytes 6815744 | tf_op jit(solution)/shard_map/pallas_call | solution.py:186
  47.0 3.2 %slice_negate_fusion = (bf16[64,128,64]{2,1,0:T(8,128)(2,1)S(1)}, bf16[64,128,64]{2,1,0:T(8,128)(2,1)S(1)}) fusion(bf16[64,128,128]{2,1,0:T(8,128)(2,1)} %shard_map.82), kind=kLoop, calls=%fused_computation.1 | loop fusion | flops 524288 | bytes 4194304 | tf_op jit(solution)/shard_map/neg | solution.py:28
  50.2 2.4 %fusion.5 = f32[1,64,64]{2,1,0:T(8,128)S(1)} fusion(bf16[64,128,128]{2,1,0:T(8,128)(2,1)S(1)} %copy-done), kind=kOutput, calls=%fused_computation.8 | convolution fusion | flops 134217728 | bytes 2113536 | tf_op jit(solution)/shard_map/fn,gn->fg/dot_general | solution.py:349
  52.7 1.2 pad_maximum_fusion
  53.9 2.4 %fusion.8 = f32[1,64,64]{2,1,0:T(8,128)S(1)} fusion(bf16[64,128,128]{2,1,0:T(8,128)(2,1)S(1)} %copy-done, bf16[64,128,128]{2,1,0:T(8,128)(2,1)S(1)} %pad_maximum_fusion), kind=kOutput, calls=%fused_computation.9 | convolution fusion | flops 134217728 | bytes 4210688 | tf_op jit(solution)/shard_map/fn,gn->fg/dot_general | solution.py:350
  56.3 0.7 collective-permute-start
  57.0 0.9 collective-permute-done
  58.0 3.1 %collective-permute-done.1 = f32[2,64,64]{2,1,0:T(8,128)S(1)} collective-permute-done((f32[2,64,64]{2,1,0:T(8,128)S(1)}, f32[2,64,64]{2,1,0:T(8,128)S(1)}, u32[]{:S(2)}, u32[]{:S(2)}) %collective-permute-start.1) | collective-permute-done | bytes 32800 | tf_op jit(solution)/shard_map/ppermute | solution.py:327
  61.2 3.1 %collective-permute-done.2 = f32[2,64,64]{2,1,0:T(8,128)S(1)} collective-permute-done((f32[2,64,64]{2,1,0:T(8,128)S(1)}, f32[2,64,64]{2,1,0:T(8,128)S(1)}, u32[]{:S(2)}, u32[]{:S(2)}) %collective-permute-start.2) | collective-permute-done | bytes 32800 | tf_op jit(solution)/shard_map/ppermute | solution.py:327
  64.4 1.4 copy.48
  65.8 2.6 %collective-permute-done.3 = f32[2,64,64]{2,1,0:T(8,128)S(1)} collective-permute-done((f32[2,64,64]{2,1,0:T(8,128)S(1)}, f32[2,64,64]{2,1,0:T(8,128)S(1)}, u32[]{:S(2)}, u32[]{:S(2)}) %collective-permute-start.3) | collective-permute-done | bytes 32800 | tf_op jit(solution)/shard_map/ppermute | solution.py:327
  68.5 5.5 %collective-permute-start.4 = (bf16[64,16384]{1,0:T(8,128)(2,1)S(1)}, bf16[64,16384]{1,0:T(8,128)(2,1)}, u32[]{:S(2)}, u32[]{:S(2)}) collective-permute-start(bf16[64,16384]{1,0:T(8,128)(2,1)S(1)} %bitcast.38), channel_id=1, source_target_pairs={{0,1},{1,2},{2,3},{3,4},{4,5},{5,6},{6,7},{7,8},{8,9},{9,10},{10,1... | collective-permute-start | bytes 6291464 | tf_op jit(solution)/shard_map/ppermute | solution.py:353
  74.0 2.3 %collective-permute-start.5 = (bf16[64,16384]{1,0:T(8,128)(2,1)S(1)}, bf16[64,16384]{1,0:T(8,128)(2,1)}, u32[]{:S(2)}, u32[]{:S(2)}) collective-permute-start(bf16[64,16384]{1,0:T(8,128)(2,1)S(1)} %bitcast.39), channel_id=1, source_target_pairs={{1,0},{2,1},{3,2},{4,3},{5,4},{6,5},{7,6},{8,7},{9,8},{10,9},{11,1... | collective-permute-start | bytes 6291464 | tf_op jit(solution)/shard_map/ppermute | solution.py:354
  77.2 0.6 maximum_bitcast_fusion.wz_ref
  77.8 0.7 select_reduce_fusion
  79.2 0.6 fusion.13.x0_ref
  79.8 0.7 select_add_fusion
  80.5 6.9 %shard_map.83 = f32[128,128]{1,0:T(8,128)} custom-call(f32[128,128]{1,0:T(8,128)} %get-tuple-element.11.a_ref, f32[128,128]{1,0:T(8,128)} %fusion.13.x0_ref, f32[128,128]{1,0:T(8,128)} %get-tuple-element.12.s_ref), custom_call_target="tpu_custom_call" | custom-call | tf_op jit(solution)/shard_map/pallas_call | solution.py:296
  87.5 0.9 copy.27
  88.5 0.6 maximum_bitcast_fusion.1.wl_ref
  89.1 30.2 %collective-permute-done.4.xb_ref = bf16[64,16384]{1,0:T(8,128)(2,1)} collective-permute-done((bf16[64,16384]{1,0:T(8,128)(2,1)S(1)}, bf16[64,16384]{1,0:T(8,128)(2,1)}, u32[]{:S(2)}, u32[]{:S(2)}) %collective-permute-start.4) | collective-permute-done | bytes 2097184 | tf_op jit(solution)/shard_map/ppermute | solution.py:353
  119.4 3.0 %collective-permute-done.5.xa_ref = bf16[64,16384]{1,0:T(8,128)(2,1)} collective-permute-done((bf16[64,16384]{1,0:T(8,128)(2,1)S(1)}, bf16[64,16384]{1,0:T(8,128)(2,1)}, u32[]{:S(2)}, u32[]{:S(2)}) %collective-permute-start.5) | collective-permute-done | bytes 2097184 | tf_op jit(solution)/shard_map/ppermute | solution.py:354
  122.4 13.0 %shard_map.84 = bf16[64,16384]{1,0:T(8,128)(2,1)} custom-call(bf16[64,16384]{1,0:T(8,128)(2,1)} %bitcast.40, bf16[64,16384]{1,0:T(8,128)(2,1)} %collective-permute-done.4.xb_ref, bf16[64,16384]{1,0:T(8,128)(2,1)} %collective-permute-done.5.xa_ref, bf16[128,64]{1,0:T(8,128)(2,1)} %maximum_bitcast_fusion.1.wl_ref, bf16[128,192]{1,0:T(8,128)(2,1)} %maximum_bitcast_fusion.wz_ref), custom_call_target="tpu_custom_call" | custom-call | flops 1610612736 | bytes 8388608 | tf_op jit(solution)/shard_map/pallas_call | solution.py:258
  135.4 3.5 %copy.33 = bf16[8,8,128,128]{3,2,1,0:T(8,128)(2,1)} copy(bf16[8,8,128,128]{3,1,2,0:T(8,128)(2,1)} %bitcast.41) | data formatting | bytes 4194304
  (30 shorter events, 1.3 us)
Async XLA Ops:
  1.0 3.5 %copy-start.3 = (bf16[1,16,128,128]{3,2,1,0:T(8,128)(2,1)S(1)}, bf16[1,16,128,128]{3,2,1,0:T(8,128)(2,1)}, u32[]{:S(2)}) copy-start(bf16[1,16,128,128]{3,2,1,0:T(8,128)(2,1)} %param.10) | copy-start | bytes 1572868
  2.0 3.6 %copy-start.2 = (bf16[5,2,128,128]{3,2,1,0:T(8,128)(2,1)S(1)}, bf16[5,2,128,128]{3,2,1,0:T(8,128)(2,1)}, u32[]{:S(2)}) copy-start(bf16[5,2,128,128]{3,2,1,0:T(8,128)(2,1)} %param.13) | copy-start | bytes 983044
  2.0 5.1 %copy-start.5 = (s32[1,64]{1,0:T(1,128)S(1)}, s32[1,64]{1,0:T(1,128)}, u32[]{:S(2)}) copy-start(s32[1,64]{1,0:T(1,128)} %param.11) | copy-start | bytes 772
  47.0 3.2 %copy-start = (bf16[64,128,128]{2,1,0:T(8,128)(2,1)S(1)}, bf16[64,128,128]{2,1,0:T(8,128)(2,1)}, u32[]{:S(2)}) copy-start(bf16[64,128,128]{2,1,0:T(8,128)(2,1)} %shard_map.82) | copy-start | bytes 6291460
  56.3 1.6 %collective-permute-start = (f32[2,64,64]{2,1,0:T(8,128)S(1)}, f32[2,64,64]{2,1,0:T(8,128)S(1)}, u32[]{:S(2)}, u32[]{:S(2)}) collective-permute-start(f32[2,64,64]{2,1,0:T(8,128)S(1)} %pad_maximum_fusion.2), channel_id=1, source_target_pairs={{0,1},{1,0},{2,3},{3,2},{4,5},{5,4},{6,7},{7,6},{8,9},{9,8},{10,11... | collective-permute-start | bytes 98312 | tf_op jit(solution)/shard_map/ppermute | solution.py:327
  58.0 3.2 %collective-permute-start.1 = (f32[2,64,64]{2,1,0:T(8,128)S(1)}, f32[2,64,64]{2,1,0:T(8,128)S(1)}, u32[]{:S(2)}, u32[]{:S(2)}) collective-permute-start(f32[2,64,64]{2,1,0:T(8,128)S(1)} %fusion.14), channel_id=1, source_target_pairs={{0,2},{1,3},{2,0},{3,1},{4,6},{5,7},{6,4},{7,5},{8,10},{9,11},{10,... | collective-permute-start | bytes 98312 | tf_op jit(solution)/shard_map/ppermute | solution.py:327
  61.1 3.2 %collective-permute-start.2 = (f32[2,64,64]{2,1,0:T(8,128)S(1)}, f32[2,64,64]{2,1,0:T(8,128)S(1)}, u32[]{:S(2)}, u32[]{:S(2)}) collective-permute-start(f32[2,64,64]{2,1,0:T(8,128)S(1)} %fusion.17), channel_id=1, source_target_pairs={{0,4},{1,5},{2,6},{3,7},{4,0},{5,1},{6,2},{7,3},{8,12},{9,13},{10,... | collective-permute-start | bytes 98312 | tf_op jit(solution)/shard_map/ppermute | solution.py:327
  64.3 4.1 %collective-permute-start.3 = (f32[2,64,64]{2,1,0:T(8,128)S(1)}, f32[2,64,64]{2,1,0:T(8,128)S(1)}, u32[]{:S(2)}, u32[]{:S(2)}) collective-permute-start(f32[2,64,64]{2,1,0:T(8,128)S(1)} %add.20), channel_id=1, source_target_pairs={{0,8},{1,9},{2,10},{3,11},{4,12},{5,13},{6,14},{7,15},{8,0},{9,1},... | collective-permute-start | bytes 98312 | tf_op jit(solution)/shard_map/ppermute | solution.py:327
  64.4 12.5 %copy-start.4 = (bf16[3,2,64,64]{3,2,1,0:T(8,128)(2,1)S(1)}, bf16[3,2,64,64]{3,2,1,0:T(8,128)(2,1)}, u32[]{:S(2)}) copy-start(bf16[3,2,64,64]{3,2,1,0:T(8,128)(2,1)} %param.14) | copy-start | bytes 147460
  65.8 56.6 %copy-start.1 = (bf16[8,8,128,128]{3,1,2,0:T(8,128)(2,1)}, bf16[8,8,128,128]{3,1,2,0:T(8,128)(2,1)S(1)}, u32[]{:S(2)}) copy-start(bf16[8,8,128,128]{3,1,2,0:T(8,128)(2,1)S(1)} %copy.48) | copy-start | bytes 6291460
  68.5 50.9 %collective-permute-start.4 = (bf16[64,16384]{1,0:T(8,128)(2,1)S(1)}, bf16[64,16384]{1,0:T(8,128)(2,1)}, u32[]{:S(2)}, u32[]{:S(2)}) collective-permute-start(bf16[64,16384]{1,0:T(8,128)(2,1)S(1)} %bitcast.38), channel_id=1, source_target_pairs={{0,1},{1,2},{2,3},{3,4},{4,5},{5,6},{6,7},{7,8},{8,9},{9,10},{10,1... | collective-permute-start | bytes 6291464 | tf_op jit(solution)/shard_map/ppermute | solution.py:353
  74.0 48.4 %collective-permute-start.5 = (bf16[64,16384]{1,0:T(8,128)(2,1)S(1)}, bf16[64,16384]{1,0:T(8,128)(2,1)}, u32[]{:S(2)}, u32[]{:S(2)}) collective-permute-start(bf16[64,16384]{1,0:T(8,128)(2,1)S(1)} %bitcast.39), channel_id=1, source_target_pairs={{1,0},{2,1},{3,2},{4,3},{5,4},{6,5},{7,6},{8,7},{9,8},{10,9},{11,1... | collective-permute-start | bytes 6291464 | tf_op jit(solution)/shard_map/ppermute | solution.py:354

commit v6 on v5

--- a/solution.py
+++ b/solution.py
@@ -348,10 +348,9 @@
     rows_turned = rotate(fresh).reshape(frame_count, -1)
     gram_real = jnp.einsum("fn,gn->fg", rows_real, rows_real, preferred_element_type=jnp.float32)
     gram_imag = jnp.einsum("fn,gn->fg", rows_turned, rows_real, preferred_element_type=jnp.float32)
-    gram_real, gram_imag = tree_sum(jnp.stack([gram_real, gram_imag]), "dom")
-    flat, gram_real, gram_imag = lax.optimization_barrier((flat, gram_real, gram_imag))
     fresh_before = lax.ppermute(flat, "dom", forward)
     fresh_after = lax.ppermute(flat, "dom", backward)
+    gram_real, gram_imag = tree_sum(jnp.stack([gram_real, gram_imag]), "dom")
     stacked = jnp.block([[gram_real, -gram_imag], [gram_imag, gram_real]])
     rank_value = rank_cap[0].astype(jnp.float32)
     threshold_sq = jnp.trace(gram_real) / rank_value

time: 139 us -> 141 us (1.014)
  the two profiles are of different devices: /device:TPU:19 before, /device:TPU:0 now
where the time goes in v6:
time: 141 us; the launch traced here: 140 us
  starting transfers between devices  55.4 us (39%)
  Pallas kernels  36.7 us (26%)
  waiting for transfers between devices  20.9 us (15%)
  local copies, waits for them, and re-layouts  13.9 us (10%)
  other arithmetic  7.14 us (5%)
  matrix products  4.85 us (3%)
  between operations  1.52 us (1%)
    ppermute x4, starting transfers between devices, tree_sum(): value = value + lax.ppermute(value, axis, pairs)  50.2 us
    ppermute x4, waiting for transfers between devices, tree_sum(): value = value + lax.ppermute(value, axis, pairs)  20.9 us
    pallas_call x1, Pallas kernels, fresh_image_of(): pl.pallas_call(kernel, out_shape=jax.ShapeDtypeStruct(image_plane.shape,...  16.7 us
    pallas_call x1, Pallas kernels, post_of(): pl.pallas_call(functools.partial(post_kernel, cut=SOFT_CUT), out_shape=ja...  13 us
    unnamed x17, local copies, waits for them, and re-layouts  9.81 us
    pallas_call x1, Pallas kernels, shrink_of(): pl.pallas_call(functools.partial(solve_kernel, steps=12), out_shape=jax.S...  6.95 us
    ppermute x1, starting transfers between devices, local(): fresh_before = lax.ppermute(flat, 'dom', forward)  3.74 us
  transfers between devices with their start and end apart: 6, of which 4 were waited for; matrix products, arithmetic and copies ran while one was open for 8% of the time, Pallas kernels for 5%

profile of v6, /device:TPU:0, one launch (start us, length us, event | category | flops | bytes accessed | tf_op | source)
XLA Modules:
  0.0 140.4 jit_solution(6085254746724468795)
XLA Ops:
  0.0 1.0 slice_negate_fusion.1
  1.1 0.9 copy.31.btr_ref
  2.0 1.5 %copy.19 = s32[1,64,6,5,2]{4,3,2,1,0:T(8,128)S(1)} copy(s32[1,64,6,5,2]{1,4,3,2,0:T(2,128)} %param.12) | data formatting | bytes 30720 | tf_op args[4]
  3.6 0.9 reshape_squeeze.6.idx_ref
  4.5 1.1 copy.49
  5.6 0.9 copy.30.bt_ref
  7.1 0.7 reduce.3
  7.9 0.5 broadcast_minimum_fusion.nsl_ref
  8.5 16.7 %shard_map.82 = bf16[64,128,128]{2,1,0:T(8,128)(2,1)} custom-call(s32[3840]{0:T(1024)} %reshape_squeeze.6.idx_ref, s32[64]{0:T(128)} %bitcast.55, s32[4]{0:T(128)} %broadcast_minimum_fusion.nsl_ref, bf16[64,128,128]{2,1,0:T(8,128)(2,1)} %bitcast.53, bf16[64,128,128]{2,1,0:T(8,128)(2,1)} %bitcast.54, bf16[128,16,128]{2,1,0:T(8,128)(2,1)} %bitcast.50, ...), custom_call_target="tpu_custom_call" | custom-call | flops 6039797760 | bytes 6815744 | tf_op jit(solution)/shard_map/pallas_call | solution.py:186
  25.2 3.1 %copy.48 = bf16[8,8,128,128]{3,1,2,0:T(8,128)(2,1)S(1)} copy(bf16[8,8,128,128]{3,2,1,0:T(8,128)(2,1)} %bitcast.41) | data formatting | bytes 4194304
  28.3 3.7 %collective-permute-start = (bf16[64,16384]{1,0:T(8,128)(2,1)S(1)}, bf16[64,16384]{1,0:T(8,128)(2,1)}, u32[]{:S(2)}, u32[]{:S(2)}) collective-permute-start(bf16[64,16384]{1,0:T(8,128)(2,1)S(1)} %bitcast.42), channel_id=1, source_target_pairs={{0,1},{1,2},{2,3},{3,4},{4,5},{5,6},{6,7},{7,8},{8,9},{9,10},{10,1... | collective-permute-start | bytes 6291464 | tf_op jit(solution)/shard_map/ppermute | solution.py:351
  32.1 1.5 %collective-permute-start.1 = (bf16[64,16384]{1,0:T(8,128)(2,1)S(1)}, bf16[64,16384]{1,0:T(8,128)(2,1)}, u32[]{:S(2)}, u32[]{:S(2)}) collective-permute-start(bf16[64,16384]{1,0:T(8,128)(2,1)S(1)} %bitcast.43), channel_id=1, source_target_pairs={{1,0},{2,1},{3,2},{4,3},{5,4},{6,5},{7,6},{8,7},{9,8},{10,9},{11,1... | collective-permute-start | bytes 6291464 | tf_op jit(solution)/shard_map/ppermute | solution.py:352
  33.6 0.9 slice_negate_fusion
  34.4 1.2 pad_maximum_fusion
  35.6 2.4 %fusion.8 = f32[1,64,64]{2,1,0:T(8,128)S(1)} fusion(bf16[64,128,128]{2,1,0:T(8,128)(2,1)S(1)} %copy-done, bf16[64,128,128]{2,1,0:T(8,128)(2,1)S(1)} %pad_maximum_fusion), kind=kOutput, calls=%fused_computation.9 | convolution fusion | flops 134217728 | bytes 4210688 | tf_op jit(solution)/shard_map/fn,gn->fg/dot_general | solution.py:350
  38.1 2.4 %fusion.5 = f32[1,64,64]{2,1,0:T(8,128)S(1)} fusion(bf16[64,128,128]{2,1,0:T(8,128)(2,1)S(1)} %copy-done), kind=kOutput, calls=%fused_computation.8 | convolution fusion | flops 134217728 | bytes 2113536 | tf_op jit(solution)/shard_map/fn,gn->fg/dot_general | solution.py:349
  40.5 2.1 %collective-permute-start.2 = (f32[2,64,64]{2,1,0:T(8,128)S(1)}, f32[2,64,64]{2,1,0:T(8,128)S(1)}, u32[]{:S(2)}, u32[]{:S(2)}) collective-permute-start(f32[2,64,64]{2,1,0:T(8,128)S(1)} %pad_maximum_fusion.2), channel_id=1, source_target_pairs={{0,1},{1,0},{2,3},{3,2},{4,5},{5,4},{6,7},{7,6},{8,9},{9,8},{10,11... | collective-permute-start | bytes 98312 | tf_op jit(solution)/shard_map/ppermute | solution.py:327
  42.6 0.9 collective-permute-done.2
  43.5 2.0 %collective-permute-start.3 = (f32[2,64,64]{2,1,0:T(8,128)S(1)}, f32[2,64,64]{2,1,0:T(8,128)S(1)}, u32[]{:S(2)}, u32[]{:S(2)}) collective-permute-start(f32[2,64,64]{2,1,0:T(8,128)S(1)} %fusion.15), channel_id=1, source_target_pairs={{0,2},{1,3},{2,0},{3,1},{4,6},{5,7},{6,4},{7,5},{8,10},{9,11},{10,... | collective-permute-start | bytes 98312 | tf_op jit(solution)/shard_map/ppermute | solution.py:327
  45.5 16.8 %collective-permute-done.3 = f32[2,64,64]{2,1,0:T(8,128)S(1)} collective-permute-done((f32[2,64,64]{2,1,0:T(8,128)S(1)}, f32[2,64,64]{2,1,0:T(8,128)S(1)}, u32[]{:S(2)}, u32[]{:S(2)}) %collective-permute-start.3) | collective-permute-done | bytes 32800 | tf_op jit(solution)/shard_map/ppermute | solution.py:327
  62.3 23.4 %collective-permute-start.4 = (f32[2,64,64]{2,1,0:T(8,128)S(1)}, f32[2,64,64]{2,1,0:T(8,128)S(1)}, u32[]{:S(2)}, u32[]{:S(2)}) collective-permute-start(f32[2,64,64]{2,1,0:T(8,128)S(1)} %fusion.18), channel_id=1, source_target_pairs={{0,4},{1,5},{2,6},{3,7},{4,0},{5,1},{6,2},{7,3},{8,12},{9,13},{10,... | collective-permute-start | bytes 98312 | tf_op jit(solution)/shard_map/ppermute | solution.py:327
  85.9 2.1 %collective-permute-done.4 = f32[2,64,64]{2,1,0:T(8,128)S(1)} collective-permute-done((f32[2,64,64]{2,1,0:T(8,128)S(1)}, f32[2,64,64]{2,1,0:T(8,128)S(1)}, u32[]{:S(2)}, u32[]{:S(2)}) %collective-permute-start.4) | collective-permute-done | bytes 32800 | tf_op jit(solution)/shard_map/ppermute | solution.py:327
  88.0 22.7 %collective-permute-start.5 = (f32[2,64,64]{2,1,0:T(8,128)S(1)}, f32[2,64,64]{2,1,0:T(8,128)S(1)}, u32[]{:S(2)}, u32[]{:S(2)}) collective-permute-start(f32[2,64,64]{2,1,0:T(8,128)S(1)} %add.20), channel_id=1, source_target_pairs={{0,8},{1,9},{2,10},{3,11},{4,12},{5,13},{6,14},{7,15},{8,0},{9,1},... | collective-permute-start | bytes 98312 | tf_op jit(solution)/shard_map/ppermute | solution.py:327
  110.8 0.6 maximum_bitcast_fusion.wz_ref
  112.1 1.1 collective-permute-done.5
  113.2 0.6 fusion.14
  114.5 0.8 select_add_fusion
  115.3 6.9 %shard_map.83 = f32[128,128]{1,0:T(8,128)} custom-call(f32[128,128]{1,0:T(8,128)} %get-tuple-element.5.a_ref, f32[128,128]{1,0:T(8,128)} %get-tuple-element.19.x0_ref, f32[128,128]{1,0:T(8,128)} %get-tuple-element.6.s_ref), custom_call_target="tpu_custom_call" | custom-call | tf_op jit(solution)/shard_map/pallas_call | solution.py:296
  122.2 0.9 copy.27
  123.2 0.6 maximum_bitcast_fusion.1.wl_ref
  123.9 13.0 %shard_map.84 = bf16[64,16384]{1,0:T(8,128)(2,1)} custom-call(bf16[64,16384]{1,0:T(8,128)(2,1)} %bitcast.44, bf16[64,16384]{1,0:T(8,128)(2,1)} %collective-permute-done.xb_ref, bf16[64,16384]{1,0:T(8,128)(2,1)} %collective-permute-done.1.xa_ref, bf16[128,64]{1,0:T(8,128)(2,1)} %maximum_bitcast_fusion.1.wl_ref, bf16[128,192]{1,0:T(8,128)(2,1)} %maximum_bitcast_fusion.wz_ref), custom_call_target="tpu_custom_call" | custom-call | flops 1610612736 | bytes 8388608 | tf_op jit(solution)/shard_map/pallas_call | solution.py:258
  136.9 3.5 %copy.33 = bf16[8,8,128,128]{3,2,1,0:T(8,128)(2,1)} copy(bf16[8,8,128,128]{3,1,2,0:T(8,128)(2,1)} %bitcast.45) | data formatting | bytes 4194304
  (28 shorter events, 1.1 us)
Async XLA Ops:
  1.0 3.5 %copy-start.3 = (bf16[1,16,128,128]{3,2,1,0:T(8,128)(2,1)S(1)}, bf16[1,16,128,128]{3,2,1,0:T(8,128)(2,1)}, u32[]{:S(2)}) copy-start(bf16[1,16,128,128]{3,2,1,0:T(8,128)(2,1)} %param.10) | copy-start | bytes 1572868
  2.0 3.6 %copy-start.2 = (bf16[5,2,128,128]{3,2,1,0:T(8,128)(2,1)S(1)}, bf16[5,2,128,128]{3,2,1,0:T(8,128)(2,1)}, u32[]{:S(2)}) copy-start(bf16[5,2,128,128]{3,2,1,0:T(8,128)(2,1)} %param.13) | copy-start | bytes 983044
  2.0 5.1 %copy-start.5 = (s32[1,64]{1,0:T(1,128)S(1)}, s32[1,64]{1,0:T(1,128)}, u32[]{:S(2)}) copy-start(s32[1,64]{1,0:T(1,128)} %param.11) | copy-start | bytes 772
  25.2 8.3 %copy-start = (bf16[64,128,128]{2,1,0:T(8,128)(2,1)S(1)}, bf16[64,128,128]{2,1,0:T(8,128)(2,1)}, u32[]{:S(2)}) copy-start(bf16[64,128,128]{2,1,0:T(8,128)(2,1)} %shard_map.82) | copy-start | bytes 6291460
  28.3 6.1 %copy-start.1 = (bf16[8,8,128,128]{3,1,2,0:T(8,128)(2,1)}, bf16[8,8,128,128]{3,1,2,0:T(8,128)(2,1)S(1)}, u32[]{:S(2)}) copy-start(bf16[8,8,128,128]{3,1,2,0:T(8,128)(2,1)S(1)} %copy.48) | copy-start | bytes 6291460
  28.3 95.5 %collective-permute-start = (bf16[64,16384]{1,0:T(8,128)(2,1)S(1)}, bf16[64,16384]{1,0:T(8,128)(2,1)}, u32[]{:S(2)}, u32[]{:S(2)}) collective-permute-start(bf16[64,16384]{1,0:T(8,128)(2,1)S(1)} %bitcast.42), channel_id=1, source_target_pairs={{0,1},{1,2},{2,3},{3,4},{4,5},{5,6},{6,7},{7,8},{8,9},{9,10},{10,1... | collective-permute-start | bytes 6291464 | tf_op jit(solution)/shard_map/ppermute | solution.py:351
  32.1 91.8 %collective-permute-start.1 = (bf16[64,16384]{1,0:T(8,128)(2,1)S(1)}, bf16[64,16384]{1,0:T(8,128)(2,1)}, u32[]{:S(2)}, u32[]{:S(2)}) collective-permute-start(bf16[64,16384]{1,0:T(8,128)(2,1)S(1)} %bitcast.43), channel_id=1, source_target_pairs={{1,0},{2,1},{3,2},{4,3},{5,4},{6,5},{7,6},{8,7},{9,8},{10,9},{11,1... | collective-permute-start | bytes 6291464 | tf_op jit(solution)/shard_map/ppermute | solution.py:352
  38.1 47.7 %copy-start.4 = (bf16[3,2,64,64]{3,2,1,0:T(8,128)(2,1)S(1)}, bf16[3,2,64,64]{3,2,1,0:T(8,128)(2,1)}, u32[]{:S(2)}) copy-start(bf16[3,2,64,64]{3,2,1,0:T(8,128)(2,1)} %param.14) | copy-start | bytes 147460
  40.5 3.0 %collective-permute-start.2 = (f32[2,64,64]{2,1,0:T(8,128)S(1)}, f32[2,64,64]{2,1,0:T(8,128)S(1)}, u32[]{:S(2)}, u32[]{:S(2)}) collective-permute-start(f32[2,64,64]{2,1,0:T(8,128)S(1)} %pad_maximum_fusion.2), channel_id=1, source_target_pairs={{0,1},{1,0},{2,3},{3,2},{4,5},{5,4},{6,7},{7,6},{8,9},{9,8},{10,11... | collective-permute-start | bytes 98312 | tf_op jit(solution)/shard_map/ppermute | solution.py:327
  43.5 18.8 %collective-permute-start.3 = (f32[2,64,64]{2,1,0:T(8,128)S(1)}, f32[2,64,64]{2,1,0:T(8,128)S(1)}, u32[]{:S(2)}, u32[]{:S(2)}) collective-permute-start(f32[2,64,64]{2,1,0:T(8,128)S(1)} %fusion.15), channel_id=1, source_target_pairs={{0,2},{1,3},{2,0},{3,1},{4,6},{5,7},{6,4},{7,5},{8,10},{9,11},{10,... | collective-permute-start | bytes 98312 | tf_op jit(solution)/shard_map/ppermute | solution.py:327
  62.3 25.7 %collective-permute-start.4 = (f32[2,64,64]{2,1,0:T(8,128)S(1)}, f32[2,64,64]{2,1,0:T(8,128)S(1)}, u32[]{:S(2)}, u32[]{:S(2)}) collective-permute-start(f32[2,64,64]{2,1,0:T(8,128)S(1)} %fusion.18), channel_id=1, source_target_pairs={{0,4},{1,5},{2,6},{3,7},{4,0},{5,1},{6,2},{7,3},{8,12},{9,13},{10,... | collective-permute-start | bytes 98312 | tf_op jit(solution)/shard_map/ppermute | solution.py:327
  88.0 25.1 %collective-permute-start.5 = (f32[2,64,64]{2,1,0:T(8,128)S(1)}, f32[2,64,64]{2,1,0:T(8,128)S(1)}, u32[]{:S(2)}, u32[]{:S(2)}) collective-permute-start(f32[2,64,64]{2,1,0:T(8,128)S(1)} %add.20), channel_id=1, source_target_pairs={{0,8},{1,9},{2,10},{3,11},{4,12},{5,13},{6,14},{7,15},{8,0},{9,1},... | collective-permute-start | bytes 98312 | tf_op jit(solution)/shard_map/ppermute | solution.py:327

commit v7 on v5

--- a/solution.py
+++ b/solution.py
@@ -166,7 +166,7 @@
     frame_count, tile_count, lane_width = image_plane.shape
     slots, reads, links = plane_map.shape[1], plane_map.shape[2], plane_map.shape[3]
     coils = plane_maps.shape[0]
-    fb = 16 if frame_count % 16 == 0 else frame_count
+    fb = 32 if frame_count % 32 == 0 else frame_count
     nblocks = frame_count // fb
     half = lane_width // 2
     maps_t = jnp.swapaxes(plane_maps, 0, 1)

time: 139 us -> 135 us (0.971)
  Pallas kernels: 58.5 us -> 54.6 us
    pallas_call x1, Pallas kernels: 38.5 us -> 34.6 us  [fresh_image_of(): pl.pallas_call(kernel, out_shape=jax.ShapeDtypeStruct(image_plane.shape,...]
where the time goes in v7:
time: 135 us
  Pallas kernels  54.6 us (40%)
  waiting for transfers between devices  43.1 us (32%)
  local copies, waits for them, and re-layouts  12.1 us (9%)
  other arithmetic  10.1 us (7%)
  starting transfers between devices  8.58 us (6%)
  matrix products  4.84 us (4%)
  between operations  1.59 us (1%)
    pallas_call x1, Pallas kernels, fresh_image_of(): pl.pallas_call(kernel, out_shape=jax.ShapeDtypeStruct(image_plane.shape,...  34.6 us
    ppermute x1, waiting for transfers between devices, local(): fresh_before = lax.ppermute(flat, 'dom', forward)  30.4 us
    pallas_call x1, Pallas kernels, post_of(): pl.pallas_call(functools.partial(post_kernel, cut=SOFT_CUT), out_shape=ja...  13 us
    ppermute x4, waiting for transfers between devices, tree_sum(): value = value + lax.ppermute(value, axis, pairs)  9.71 us
    unnamed x17, local copies, waits for them, and re-layouts  8.08 us
    pallas_call x1, Pallas kernels, shrink_of(): pl.pallas_call(functools.partial(solve_kernel, steps=12), out_shape=jax.S...  6.94 us
    ppermute x1, starting transfers between devices, local(): fresh_before = lax.ppermute(flat, 'dom', forward)  5.49 us
    neg x2, other arithmetic, rotate(): -field_values[..., half_width:]  4.27 us
  transfers between devices with their start and end apart: 6, of which 6 were waited for; matrix products, arithmetic and copies ran while one was open for 4% of the time, Pallas kernels for 5%

profile of v7, /device:TPU:19, one launch (start us, length us, event | category | flops | bytes accessed | tf_op | source)
XLA Modules:
  0.0 135.0 jit_solution(10433585228858000636)
XLA Ops:
  0.0 1.0 slice_negate_fusion.1
  1.1 0.9 copy.31.btr_ref
  2.0 1.5 %copy.19 = s32[1,64,6,5,2]{4,3,2,1,0:T(8,128)S(1)} copy(s32[1,64,6,5,2]{1,4,3,2,0:T(2,128)} %param.12) | data formatting | bytes 30720 | tf_op args[4]
  3.6 0.9 reshape_squeeze.6.idx_ref
  4.5 1.1 copy.49
  5.6 0.9 copy.30.bt_ref
  7.1 0.7 reduce.3
  7.9 0.5 broadcast_minimum_fusion.nsl_ref
  8.5 34.6 %shard_map.82 = bf16[64,128,128]{2,1,0:T(8,128)(2,1)} custom-call(s32[3840]{0:T(1024)} %reshape_squeeze.6.idx_ref, s32[64]{0:T(128)} %bitcast.51, s32[2]{0:T(128)} %broadcast_minimum_fusion.nsl_ref, bf16[64,128,128]{2,1,0:T(8,128)(2,1)} %bitcast.49, bf16[64,128,128]{2,1,0:T(8,128)(2,1)} %bitcast.50, bf16[128,16,128]{2,1,0:T(8,128)(2,1)} %bitcast.46, ...), custom_call_target="tpu_custom_call" | custom-call | flops 6039797760 | bytes 6815744 | tf_op jit(solution)/shard_map/pallas_call | solution.py:186
  43.1 3.2 %slice_negate_fusion = (bf16[64,128,64]{2,1,0:T(8,128)(2,1)S(1)}, bf16[64,128,64]{2,1,0:T(8,128)(2,1)S(1)}) fusion(bf16[64,128,128]{2,1,0:T(8,128)(2,1)} %shard_map.82), kind=kLoop, calls=%fused_computation.1 | loop fusion | flops 524288 | bytes 4194304 | tf_op jit(solution)/shard_map/neg | solution.py:28
  46.3 2.4 %fusion.5 = f32[1,64,64]{2,1,0:T(8,128)S(1)} fusion(bf16[64,128,128]{2,1,0:T(8,128)(2,1)S(1)} %copy-done), kind=kOutput, calls=%fused_computation.8 | convolution fusion | flops 134217728 | bytes 2113536 | tf_op jit(solution)/shard_map/fn,gn->fg/dot_general | solution.py:349
  48.8 1.2 pad_maximum_fusion
  50.0 2.4 %fusion.8 = f32[1,64,64]{2,1,0:T(8,128)S(1)} fusion(bf16[64,128,128]{2,1,0:T(8,128)(2,1)S(1)} %copy-done, bf16[64,128,128]{2,1,0:T(8,128)(2,1)S(1)} %pad_maximum_fusion), kind=kOutput, calls=%fused_computation.9 | convolution fusion | flops 134217728 | bytes 4210688 | tf_op jit(solution)/shard_map/fn,gn->fg/dot_general | solution.py:350
  52.4 0.7 collective-permute-start
  53.1 0.9 collective-permute-done
  54.1 3.1 %collective-permute-done.1 = f32[2,64,64]{2,1,0:T(8,128)S(1)} collective-permute-done((f32[2,64,64]{2,1,0:T(8,128)S(1)}, f32[2,64,64]{2,1,0:T(8,128)S(1)}, u32[]{:S(2)}, u32[]{:S(2)}) %collective-permute-start.1) | collective-permute-done | bytes 32800 | tf_op jit(solution)/shard_map/ppermute | solution.py:327
  57.3 3.1 %collective-permute-done.2 = f32[2,64,64]{2,1,0:T(8,128)S(1)} collective-permute-done((f32[2,64,64]{2,1,0:T(8,128)S(1)}, f32[2,64,64]{2,1,0:T(8,128)S(1)}, u32[]{:S(2)}, u32[]{:S(2)}) %collective-permute-start.2) | collective-permute-done | bytes 32800 | tf_op jit(solution)/shard_map/ppermute | solution.py:327
  60.6 1.4 %copy.48 = bf16[8,8,128,128]{3,1,2,0:T(8,128)(2,1)S(1)} copy(bf16[8,8,128,128]{3,2,1,0:T(8,128)(2,1)S(1)} %bitcast.37) | data formatting | bytes 4194304
  61.9 2.6 %collective-permute-done.3 = f32[2,64,64]{2,1,0:T(8,128)S(1)} collective-permute-done((f32[2,64,64]{2,1,0:T(8,128)S(1)}, f32[2,64,64]{2,1,0:T(8,128)S(1)}, u32[]{:S(2)}, u32[]{:S(2)}) %collective-permute-start.3) | collective-permute-done | bytes 32800 | tf_op jit(solution)/shard_map/ppermute | solution.py:327
  64.6 5.5 %collective-permute-start.4 = (bf16[64,16384]{1,0:T(8,128)(2,1)S(1)}, bf16[64,16384]{1,0:T(8,128)(2,1)}, u32[]{:S(2)}, u32[]{:S(2)}) collective-permute-start(bf16[64,16384]{1,0:T(8,128)(2,1)S(1)} %bitcast.38), channel_id=1, source_target_pairs={{0,1},{1,2},{2,3},{3,4},{4,5},{5,6},{6,7},{7,8},{8,9},{9,10},{10,1... | collective-permute-start | bytes 6291464 | tf_op jit(solution)/shard_map/ppermute | solution.py:353
  70.1 2.1 %collective-permute-start.5 = (bf16[64,16384]{1,0:T(8,128)(2,1)S(1)}, bf16[64,16384]{1,0:T(8,128)(2,1)}, u32[]{:S(2)}, u32[]{:S(2)}) collective-permute-start(bf16[64,16384]{1,0:T(8,128)(2,1)S(1)} %bitcast.39), channel_id=1, source_target_pairs={{1,0},{2,1},{3,2},{4,3},{5,4},{6,5},{7,6},{8,7},{9,8},{10,9},{11,1... | collective-permute-start | bytes 6291464 | tf_op jit(solution)/shard_map/ppermute | solution.py:354
  73.1 0.6 maximum_bitcast_fusion.wz_ref
  73.7 0.7 select_reduce_fusion
  75.1 0.6 fusion.13.x0_ref
  75.8 0.7 select_add_fusion
  76.5 6.9 %shard_map.83 = f32[128,128]{1,0:T(8,128)} custom-call(f32[128,128]{1,0:T(8,128)} %get-tuple-element.11.a_ref, f32[128,128]{1,0:T(8,128)} %fusion.13.x0_ref, f32[128,128]{1,0:T(8,128)} %get-tuple-element.12.s_ref), custom_call_target="tpu_custom_call" | custom-call | tf_op jit(solution)/shard_map/pallas_call | solution.py:296
  83.4 0.9 copy.27
  84.5 0.6 maximum_bitcast_fusion.1.wl_ref
  85.1 30.4 %collective-permute-done.4.xb_ref = bf16[64,16384]{1,0:T(8,128)(2,1)} collective-permute-done((bf16[64,16384]{1,0:T(8,128)(2,1)S(1)}, bf16[64,16384]{1,0:T(8,128)(2,1)}, u32[]{:S(2)}, u32[]{:S(2)}) %collective-permute-start.4) | collective-permute-done | bytes 2097184 | tf_op jit(solution)/shard_map/ppermute | solution.py:353
  115.5 3.0 %collective-permute-done.5.xa_ref = bf16[64,16384]{1,0:T(8,128)(2,1)} collective-permute-done((bf16[64,16384]{1,0:T(8,128)(2,1)S(1)}, bf16[64,16384]{1,0:T(8,128)(2,1)}, u32[]{:S(2)}, u32[]{:S(2)}) %collective-permute-start.5) | collective-permute-done | bytes 2097184 | tf_op jit(solution)/shard_map/ppermute | solution.py:354
  118.5 13.0 %shard_map.84 = bf16[64,16384]{1,0:T(8,128)(2,1)} custom-call(bf16[64,16384]{1,0:T(8,128)(2,1)} %bitcast.40, bf16[64,16384]{1,0:T(8,128)(2,1)} %collective-permute-done.4.xb_ref, bf16[64,16384]{1,0:T(8,128)(2,1)} %collective-permute-done.5.xa_ref, bf16[128,64]{1,0:T(8,128)(2,1)} %maximum_bitcast_fusion.1.wl_ref, bf16[128,192]{1,0:T(8,128)(2,1)} %maximum_bitcast_fusion.wz_ref), custom_call_target="tpu_custom_call" | custom-call | flops 1610612736 | bytes 8388608 | tf_op jit(solution)/shard_map/pallas_call | solution.py:258
  131.5 3.5 %copy.33 = bf16[8,8,128,128]{3,2,1,0:T(8,128)(2,1)} copy(bf16[8,8,128,128]{3,1,2,0:T(8,128)(2,1)} %bitcast.41) | data formatting | bytes 4194304
  (30 shorter events, 1.3 us)
Async XLA Ops:
  1.0 3.5 %copy-start.3 = (bf16[1,16,128,128]{3,2,1,0:T(8,128)(2,1)S(1)}, bf16[1,16,128,128]{3,2,1,0:T(8,128)(2,1)}, u32[]{:S(2)}) copy-start(bf16[1,16,128,128]{3,2,1,0:T(8,128)(2,1)} %param.10) | copy-start | bytes 1572868
  2.0 3.6 %copy-start.2 = (bf16[5,2,128,128]{3,2,1,0:T(8,128)(2,1)S(1)}, bf16[5,2,128,128]{3,2,1,0:T(8,128)(2,1)}, u32[]{:S(2)}) copy-start(bf16[5,2,128,128]{3,2,1,0:T(8,128)(2,1)} %param.13) | copy-start | bytes 983044
  2.0 5.1 %copy-start.5 = (s32[1,64]{1,0:T(1,128)S(1)}, s32[1,64]{1,0:T(1,128)}, u32[]{:S(2)}) copy-start(s32[1,64]{1,0:T(1,128)} %param.11) | copy-start | bytes 772
  43.1 3.2 %copy-start = (bf16[64,128,128]{2,1,0:T(8,128)(2,1)S(1)}, bf16[64,128,128]{2,1,0:T(8,128)(2,1)}, u32[]{:S(2)}) copy-start(bf16[64,128,128]{2,1,0:T(8,128)(2,1)} %shard_map.82) | copy-start | bytes 6291460
  52.4 1.6 %collective-permute-start = (f32[2,64,64]{2,1,0:T(8,128)S(1)}, f32[2,64,64]{2,1,0:T(8,128)S(1)}, u32[]{:S(2)}, u32[]{:S(2)}) collective-permute-start(f32[2,64,64]{2,1,0:T(8,128)S(1)} %pad_maximum_fusion.2), channel_id=1, source_target_pairs={{0,1},{1,0},{2,3},{3,2},{4,5},{5,4},{6,7},{7,6},{8,9},{9,8},{10,11... | collective-permute-start | bytes 98312 | tf_op jit(solution)/shard_map/ppermute | solution.py:327
  54.1 3.2 %collective-permute-start.1 = (f32[2,64,64]{2,1,0:T(8,128)S(1)}, f32[2,64,64]{2,1,0:T(8,128)S(1)}, u32[]{:S(2)}, u32[]{:S(2)}) collective-permute-start(f32[2,64,64]{2,1,0:T(8,128)S(1)} %fusion.14), channel_id=1, source_target_pairs={{0,2},{1,3},{2,0},{3,1},{4,6},{5,7},{6,4},{7,5},{8,10},{9,11},{10,... | collective-permute-start | bytes 98312 | tf_op jit(solution)/shard_map/ppermute | solution.py:327
  57.3 3.2 %collective-permute-start.2 = (f32[2,64,64]{2,1,0:T(8,128)S(1)}, f32[2,64,64]{2,1,0:T(8,128)S(1)}, u32[]{:S(2)}, u32[]{:S(2)}) collective-permute-start(f32[2,64,64]{2,1,0:T(8,128)S(1)} %fusion.17), channel_id=1, source_target_pairs={{0,4},{1,5},{2,6},{3,7},{4,0},{5,1},{6,2},{7,3},{8,12},{9,13},{10,... | collective-permute-start | bytes 98312 | tf_op jit(solution)/shard_map/ppermute | solution.py:327
  60.5 4.1 %collective-permute-start.3 = (f32[2,64,64]{2,1,0:T(8,128)S(1)}, f32[2,64,64]{2,1,0:T(8,128)S(1)}, u32[]{:S(2)}, u32[]{:S(2)}) collective-permute-start(f32[2,64,64]{2,1,0:T(8,128)S(1)} %add.20), channel_id=1, source_target_pairs={{0,8},{1,9},{2,10},{3,11},{4,12},{5,13},{6,14},{7,15},{8,0},{9,1},... | collective-permute-start | bytes 98312 | tf_op jit(solution)/shard_map/ppermute | solution.py:327
  60.5 12.3 %copy-start.4 = (bf16[3,2,64,64]{3,2,1,0:T(8,128)(2,1)S(1)}, bf16[3,2,64,64]{3,2,1,0:T(8,128)(2,1)}, u32[]{:S(2)}) copy-start(bf16[3,2,64,64]{3,2,1,0:T(8,128)(2,1)} %param.14) | copy-start | bytes 147460
  61.9 56.6 %copy-start.1 = (bf16[8,8,128,128]{3,1,2,0:T(8,128)(2,1)}, bf16[8,8,128,128]{3,1,2,0:T(8,128)(2,1)S(1)}, u32[]{:S(2)}) copy-start(bf16[8,8,128,128]{3,1,2,0:T(8,128)(2,1)S(1)} %copy.48) | copy-start | bytes 6291460
  64.6 50.9 %collective-permute-start.4 = (bf16[64,16384]{1,0:T(8,128)(2,1)S(1)}, bf16[64,16384]{1,0:T(8,128)(2,1)}, u32[]{:S(2)}, u32[]{:S(2)}) collective-permute-start(bf16[64,16384]{1,0:T(8,128)(2,1)S(1)} %bitcast.38), channel_id=1, source_target_pairs={{0,1},{1,2},{2,3},{3,4},{4,5},{5,6},{6,7},{7,8},{8,9},{9,10},{10,1... | collective-permute-start | bytes 6291464 | tf_op jit(solution)/shard_map/ppermute | solution.py:353
  70.1 48.4 %collective-permute-start.5 = (bf16[64,16384]{1,0:T(8,128)(2,1)S(1)}, bf16[64,16384]{1,0:T(8,128)(2,1)}, u32[]{:S(2)}, u32[]{:S(2)}) collective-permute-start(bf16[64,16384]{1,0:T(8,128)(2,1)S(1)} %bitcast.39), channel_id=1, source_target_pairs={{1,0},{2,1},{3,2},{4,3},{5,4},{6,5},{7,6},{8,7},{9,8},{10,9},{11,1... | collective-permute-start | bytes 6291464 | tf_op jit(solution)/shard_map/ppermute | solution.py:354

commit v8 on v7

--- a/solution.py
+++ b/solution.py
@@ -345,9 +345,12 @@
     backward = [(target, source) for source, target in forward]
     flat = fresh.reshape(frame_count, -1)
     rows_real = flat
-    rows_turned = rotate(fresh).reshape(frame_count, -1)
+    half = fresh.shape[-1] // 2
     gram_real = jnp.einsum("fn,gn->fg", rows_real, rows_real, preferred_element_type=jnp.float32)
-    gram_imag = jnp.einsum("fn,gn->fg", rows_turned, rows_real, preferred_element_type=jnp.float32)
+    cross = jnp.einsum(
+        "ftw,gtw->fg", fresh[..., :half], fresh[..., half:], preferred_element_type=jnp.float32
+    )
+    gram_imag = cross - cross.T
     gram_real, gram_imag = tree_sum(jnp.stack([gram_real, gram_imag]), "dom")
     flat, gram_real, gram_imag = lax.optimization_barrier((flat, gram_real, gram_imag))
     fresh_before = lax.ppermute(flat, "dom", forward)

time: 135 us -> 142 us (1.052)
  local copies, waits for them, and re-layouts: 12.1 us -> 25 us
  other arithmetic: 10.1 us -> 5.74 us
    slice x0 -> x3, local copies, waits for them, and re-layouts: none -> 11.4 us  [the longest x2 8.61 us: local(): fresh[..., half:]]
    neg x2 -> x1, other arithmetic: 4.27 us -> 1.03 us  [rotate(): -field_values[..., half_width:]]
  transfers between devices with their start and end apart: 6 -> 6, of which waited for: 6 -> 6; matrix products, arithmetic and copies ran while one was open for 4% -> 5% of each run, Pallas kernels for 5% -> 5%
where the time goes in v8:
time: 142 us; the launch traced here: 141 us
  Pallas kernels  54.5 us (38%)
  waiting for transfers between devices  41.8 us (29%)
  local copies, waits for them, and re-layouts  25 us (18%)
  starting transfers between devices  8.79 us (6%)
  other arithmetic  5.74 us (4%)
  matrix products  4.05 us (3%)
  between operations  1.57 us (1%)
    pallas_call x1, Pallas kernels, fresh_image_of(): pl.pallas_call(kernel, out_shape=jax.ShapeDtypeStruct(image_plane.shape,...  34.6 us
    ppermute x1, waiting for transfers between devices, local(): fresh_before = lax.ppermute(flat, 'dom', forward)  30.5 us
    pallas_call x1, Pallas kernels, post_of(): pl.pallas_call(functools.partial(post_kernel, cut=SOFT_CUT), out_shape=ja...  13 us
    unnamed x17, local copies, waits for them, and re-layouts  9.46 us
    slice x2, local copies, waits for them, and re-layouts, local(): fresh[..., half:]  8.61 us
    ppermute x4, waiting for transfers between devices, tree_sum(): value = value + lax.ppermute(value, axis, pairs)  8.35 us
    pallas_call x1, Pallas kernels, shrink_of(): pl.pallas_call(functools.partial(solve_kernel, steps=12), out_shape=jax.S...  6.94 us
    ppermute x1, starting transfers between devices, local(): fresh_before = lax.ppermute(flat, 'dom', forward)  5.49 us
  transfers between devices with their start and end apart: 6, of which 6 were waited for; matrix products, arithmetic and copies ran while one was open for 5% of the time, Pallas kernels for 5%

profile of v8, /device:TPU:19, one launch (start us, length us, event | category | flops | bytes accessed | tf_op | source)
XLA Modules:
  0.0 141.4 jit_solution(10005694747505973300)
XLA Ops:
  0.0 1.0 slice_negate_fusion
  1.1 0.9 copy.33.btr_ref
  2.0 1.5 %copy.20 = s32[1,64,6,5,2]{4,3,2,1,0:T(8,128)S(1)} copy(s32[1,64,6,5,2]{1,4,3,2,0:T(2,128)} %param.12) | data formatting | bytes 30720 | tf_op args[4]
  3.6 0.9 reshape_squeeze.6.idx_ref
  4.5 1.1 copy.43
  5.6 0.9 copy.32.bt_ref
  7.1 0.7 reduce.3
  8.5 34.6 %shard_map.82 = bf16[64,128,128]{2,1,0:T(8,128)(2,1)} custom-call(s32[3840]{0:T(1024)} %reshape_squeeze.6.idx_ref, s32[64]{0:T(128)} %bitcast.55, s32[2]{0:T(128)} %broadcast_minimum_fusion.nsl_ref, bf16[64,128,128]{2,1,0:T(8,128)(2,1)} %bitcast.53, bf16[64,128,128]{2,1,0:T(8,128)(2,1)} %bitcast.54, bf16[128,16,128]{2,1,0:T(8,128)(2,1)} %bitcast.50, ...), custom_call_target="tpu_custom_call" | custom-call | flops 6039797760 | bytes 6815744 | tf_op jit(solution)/shard_map/pallas_call | solution.py:186
  43.0 5.2 %fusion.8 = (bf16[64,128,64]{2,1,0:T(8,128)(2,1)}, bf16[64,128,64]{2,1,0:T(8,128)(2,1)}) fusion(bf16[64,128,128]{2,1,0:T(8,128)(2,1)} %shard_map.82), kind=kLoop, calls=%fused_computation.23 | loop fusion | bytes 4194304 | tf_op jit(solution)/shard_map/slice | solution.py:351
  48.2 2.4 %fusion.2 = f32[1,64,64]{2,1,0:T(8,128)S(1)} fusion(bf16[64,128,128]{2,1,0:T(8,128)(2,1)S(1)} %copy-done), kind=kOutput, calls=%fused_computation.3 | convolution fusion | flops 134217728 | bytes 2113536 | tf_op jit(solution)/shard_map/fn,gn->fg/dot_general | solution.py:349
  50.7 2.8 %copy.26 = bf16[64,128,64]{1,0,2:T(8,128)(2,1)S(1)} copy(bf16[64,128,64]{2,1,0:T(8,128)(2,1)} %get-tuple-element.14) | data formatting | bytes 2097152 | tf_op jit(solution)/shard_map/slice | solution.py:351
  53.4 3.4 %copy.27 = bf16[64,128,64]{1,0,2:T(8,128)(2,1)} copy(bf16[64,128,64]{2,1,0:T(8,128)(2,1)} %get-tuple-element.13) | data formatting | bytes 2097152 | tf_op jit(solution)/shard_map/slice | solution.py:351
  56.9 1.6 %convolution_bitcast_fusion = f32[64,64]{1,0:T(8,128)S(1)} fusion(bf16[64,128,64]{1,0,2:T(8,128)(2,1)S(1)} %copy.26, bf16[64,128,64]{1,0,2:T(8,128)(2,1)} %copy.27), kind=kOutput, calls=%fused_computation.4 | convolution fusion | flops 67108864 | bytes 2113536 | tf_op jit(solution)/shard_map/ftw,gtw->fg/dot_general | solution.py:350
  58.6 0.8 collective-permute-start
  59.4 0.9 collective-permute-done
  60.4 3.1 %collective-permute-done.1 = f32[2,64,64]{2,1,0:T(8,128)S(1)} collective-permute-done((f32[2,64,64]{2,1,0:T(8,128)S(1)}, f32[2,64,64]{2,1,0:T(8,128)S(1)}, u32[]{:S(2)}, u32[]{:S(2)}) %collective-permute-start.1) | collective-permute-done | bytes 32800 | tf_op jit(solution)/shard_map/ppermute | solution.py:327
  63.6 3.1 %collective-permute-done.2 = f32[2,64,64]{2,1,0:T(8,128)S(1)} collective-permute-done((f32[2,64,64]{2,1,0:T(8,128)S(1)}, f32[2,64,64]{2,1,0:T(8,128)S(1)}, u32[]{:S(2)}, u32[]{:S(2)}) %collective-permute-start.2) | collective-permute-done | bytes 32800 | tf_op jit(solution)/shard_map/ppermute | solution.py:327
  66.8 2.8 %copy.42 = bf16[8,8,128,128]{3,1,2,0:T(8,128)(2,1)} copy(bf16[8,8,128,128]{3,2,1,0:T(8,128)(2,1)S(1)} %bitcast.44) | data formatting | bytes 4194304
  69.5 1.2 collective-permute-done.3
  70.8 5.5 %collective-permute-start.4 = (bf16[64,16384]{1,0:T(8,128)(2,1)}, bf16[64,16384]{1,0:T(8,128)(2,1)S(1)}, u32[]{:S(2)}, u32[]{:S(2)}) collective-permute-start(bf16[64,16384]{1,0:T(8,128)(2,1)} %bitcast.42.x_ref), channel_id=1, source_target_pairs={{0,1},{1,2},{2,3},{3,4},{4,5},{5,6},{6,7},{7,8},{8,9},{9,10},{10,1... | collective-permute-start | bytes 6291464 | tf_op jit(solution)/shard_map/ppermute | solution.py:356
  76.3 2.3 %collective-permute-start.5 = (bf16[64,16384]{1,0:T(8,128)(2,1)}, bf16[64,16384]{1,0:T(8,128)(2,1)}, u32[]{:S(2)}, u32[]{:S(2)}) collective-permute-start(bf16[64,16384]{1,0:T(8,128)(2,1)} %bitcast.42.x_ref), channel_id=1, source_target_pairs={{1,0},{2,1},{3,2},{4,3},{5,4},{6,5},{7,6},{8,7},{9,8},{10,9},{11,1... | collective-permute-start | bytes 6291464 | tf_op jit(solution)/shard_map/ppermute | solution.py:357
  79.5 0.6 maximum_bitcast_fusion.wz_ref
  80.1 0.7 select_reduce_fusion
  81.5 0.6 fusion.5.x0_ref
  82.2 0.8 select_add_fusion
  82.9 6.9 %shard_map.83 = f32[128,128]{1,0:T(8,128)} custom-call(f32[128,128]{1,0:T(8,128)} %get-tuple-element.11.a_ref, f32[128,128]{1,0:T(8,128)} %fusion.5.x0_ref, f32[128,128]{1,0:T(8,128)} %get-tuple-element.12.s_ref), custom_call_target="tpu_custom_call" | custom-call | tf_op jit(solution)/shard_map/pallas_call | solution.py:296
  89.9 0.9 copy.29
  90.9 0.6 maximum_bitcast_fusion.1.wl_ref
  91.5 30.5 %collective-permute-done.4.xb_ref = bf16[64,16384]{1,0:T(8,128)(2,1)S(1)} collective-permute-done((bf16[64,16384]{1,0:T(8,128)(2,1)}, bf16[64,16384]{1,0:T(8,128)(2,1)S(1)}, u32[]{:S(2)}, u32[]{:S(2)}) %collective-permute-start.4) | collective-permute-done | bytes 2097184 | tf_op jit(solution)/shard_map/ppermute | solution.py:356
  122.0 2.9 %collective-permute-done.5.xa_ref = bf16[64,16384]{1,0:T(8,128)(2,1)} collective-permute-done((bf16[64,16384]{1,0:T(8,128)(2,1)}, bf16[64,16384]{1,0:T(8,128)(2,1)}, u32[]{:S(2)}, u32[]{:S(2)}) %collective-permute-start.5) | collective-permute-done | bytes 2097184 | tf_op jit(solution)/shard_map/ppermute | solution.py:357
  124.9 13.0 %shard_map.84 = bf16[64,16384]{1,0:T(8,128)(2,1)} custom-call(bf16[64,16384]{1,0:T(8,128)(2,1)} %bitcast.42.x_ref, bf16[64,16384]{1,0:T(8,128)(2,1)} %copy-done.1, bf16[64,16384]{1,0:T(8,128)(2,1)} %collective-permute-done.5.xa_ref, bf16[128,64]{1,0:T(8,128)(2,1)} %maximum_bitcast_fusion.1.wl_ref, bf16[128,192]{1,0:T(8,128)(2,1)} %maximum_bitcast_fusion.wz_ref), custom_call_target="tpu_custom_call" | custom-call | flops 1610612736 | bytes 8388608 | tf_op jit(solution)/shard_map/pallas_call | solution.py:258
  138.0 3.5 %copy.35 = bf16[8,8,128,128]{3,2,1,0:T(8,128)(2,1)} copy(bf16[8,8,128,128]{3,1,2,0:T(8,128)(2,1)} %bitcast.45) | data formatting | bytes 4194304
  (33 shorter events, 1.9 us)
Async XLA Ops:
  1.0 3.5 %copy-start.3 = (bf16[1,16,128,128]{3,2,1,0:T(8,128)(2,1)S(1)}, bf16[1,16,128,128]{3,2,1,0:T(8,128)(2,1)}, u32[]{:S(2)}) copy-start(bf16[1,16,128,128]{3,2,1,0:T(8,128)(2,1)} %param.10) | copy-start | bytes 1572868
  2.0 3.6 %copy-start.2 = (bf16[5,2,128,128]{3,2,1,0:T(8,128)(2,1)S(1)}, bf16[5,2,128,128]{3,2,1,0:T(8,128)(2,1)}, u32[]{:S(2)}) copy-start(bf16[5,2,128,128]{3,2,1,0:T(8,128)(2,1)} %param.13) | copy-start | bytes 983044
  2.0 5.1 %copy-start.5 = (s32[1,64]{1,0:T(1,128)S(1)}, s32[1,64]{1,0:T(1,128)}, u32[]{:S(2)}) copy-start(s32[1,64]{1,0:T(1,128)} %param.11) | copy-start | bytes 772
  43.0 5.2 %copy-start = (bf16[64,128,128]{2,1,0:T(8,128)(2,1)S(1)}, bf16[64,128,128]{2,1,0:T(8,128)(2,1)}, u32[]{:S(2)}) copy-start(bf16[64,128,128]{2,1,0:T(8,128)(2,1)} %shard_map.82) | copy-start | bytes 6291460
  58.6 1.7 %collective-permute-start = (f32[2,64,64]{2,1,0:T(8,128)S(1)}, f32[2,64,64]{2,1,0:T(8,128)S(1)}, u32[]{:S(2)}, u32[]{:S(2)}) collective-permute-start(f32[2,64,64]{2,1,0:T(8,128)S(1)} %pad_maximum_fusion.1), channel_id=1, source_target_pairs={{0,1},{1,0},{2,3},{3,2},{4,5},{5,4},{6,7},{7,6},{8,9},{9,8},{10,11... | collective-permute-start | bytes 98312 | tf_op jit(solution)/shard_map/ppermute | solution.py:327
  60.3 3.2 %collective-permute-start.1 = (f32[2,64,64]{2,1,0:T(8,128)S(1)}, f32[2,64,64]{2,1,0:T(8,128)S(1)}, u32[]{:S(2)}, u32[]{:S(2)}) collective-permute-start(f32[2,64,64]{2,1,0:T(8,128)S(1)} %fusion.7), channel_id=1, source_target_pairs={{0,2},{1,3},{2,0},{3,1},{4,6},{5,7},{6,4},{7,5},{8,10},{9,11},{10,... | collective-permute-start | bytes 98312 | tf_op jit(solution)/shard_map/ppermute | solution.py:327
  63.5 3.2 %collective-permute-start.2 = (f32[2,64,64]{2,1,0:T(8,128)S(1)}, f32[2,64,64]{2,1,0:T(8,128)S(1)}, u32[]{:S(2)}, u32[]{:S(2)}) collective-permute-start(f32[2,64,64]{2,1,0:T(8,128)S(1)} %fusion.13), channel_id=1, source_target_pairs={{0,4},{1,5},{2,6},{3,7},{4,0},{5,1},{6,2},{7,3},{8,12},{9,13},{10,... | collective-permute-start | bytes 98312 | tf_op jit(solution)/shard_map/ppermute | solution.py:327
  66.7 4.1 %collective-permute-start.3 = (f32[2,64,64]{2,1,0:T(8,128)S(1)}, f32[2,64,64]{2,1,0:T(8,128)S(1)}, u32[]{:S(2)}, u32[]{:S(2)}) collective-permute-start(f32[2,64,64]{2,1,0:T(8,128)S(1)} %add.20), channel_id=1, source_target_pairs={{0,8},{1,9},{2,10},{3,11},{4,12},{5,13},{6,14},{7,15},{8,0},{9,1},... | collective-permute-start | bytes 98312 | tf_op jit(solution)/shard_map/ppermute | solution.py:327
  66.8 12.5 %copy-start.4 = (bf16[3,2,64,64]{3,2,1,0:T(8,128)(2,1)S(1)}, bf16[3,2,64,64]{3,2,1,0:T(8,128)(2,1)}, u32[]{:S(2)}) copy-start(bf16[3,2,64,64]{3,2,1,0:T(8,128)(2,1)} %param.14) | copy-start | bytes 147460
  70.8 51.2 %collective-permute-start.4 = (bf16[64,16384]{1,0:T(8,128)(2,1)}, bf16[64,16384]{1,0:T(8,128)(2,1)S(1)}, u32[]{:S(2)}, u32[]{:S(2)}) collective-permute-start(bf16[64,16384]{1,0:T(8,128)(2,1)} %bitcast.42.x_ref), channel_id=1, source_target_pairs={{0,1},{1,2},{2,3},{3,4},{4,5},{5,6},{6,7},{7,8},{8,9},{9,10},{10,1... | collective-permute-start | bytes 6291464 | tf_op jit(solution)/shard_map/ppermute | solution.py:356
  76.3 48.7 %collective-permute-start.5 = (bf16[64,16384]{1,0:T(8,128)(2,1)}, bf16[64,16384]{1,0:T(8,128)(2,1)}, u32[]{:S(2)}, u32[]{:S(2)}) collective-permute-start(bf16[64,16384]{1,0:T(8,128)(2,1)} %bitcast.42.x_ref), channel_id=1, source_target_pairs={{1,0},{2,1},{3,2},{4,3},{5,4},{6,5},{7,6},{8,7},{9,8},{10,9},{11,1... | collective-permute-start | bytes 6291464 | tf_op jit(solution)/shard_map/ppermute | solution.py:357
  122.0 2.9 %copy-start.1 = (bf16[64,16384]{1,0:T(8,128)(2,1)}, bf16[64,16384]{1,0:T(8,128)(2,1)S(1)}, u32[]{:S(2)}) copy-start(bf16[64,16384]{1,0:T(8,128)(2,1)S(1)} %collective-permute-done.4.xb_ref) | copy-start | bytes 6291460

commit v9 on v7

--- a/solution.py
+++ b/solution.py
@@ -252,7 +252,7 @@
 
 def post_of(plane, before, after, low_t, filter_t):
     frames, width = plane.shape
-    nb = 2048 if width % 2048 == 0 else width
+    nb = 4096 if width % 4096 == 0 else width
     lane_spec = pl.BlockSpec((frames, nb), lambda i: (0, i))
     whole2 = lambda shape: pl.BlockSpec(shape, lambda i: (0, 0))
     return pl.pallas_call(
@@ -294,7 +294,7 @@
     start = unit_matrix * (2.0 / (threshold_sq * (2.0 + rank_value)))
     whole = pl.BlockSpec(memory_space=pltpu.VMEM)
     return pl.pallas_call(
-        functools.partial(solve_kernel, steps=12),
+        functools.partial(solve_kernel, steps=10),
         out_shape=jax.ShapeDtypeStruct((size, size), jnp.float32),
         in_specs=[whole, whole, whole],
         out_specs=whole,

time: 135 us -> 134 us (level)
  Pallas kernels: 54.6 us -> 51.9 us
    pallas_call x1, Pallas kernels: 13 us -> 11.3 us  [post_of(): pl.pallas_call(functools.partial(post_kernel, cut=SOFT_CUT), out_shape=ja...]
where the time goes in v9:
time: 134 us; the launch traced here: 133 us
  Pallas kernels  51.9 us (39%)
  waiting for transfers between devices  44 us (33%)
  local copies, waits for them, and re-layouts  12.1 us (9%)
  other arithmetic  10.1 us (8%)
  starting transfers between devices  8.66 us (6%)
  matrix products  4.84 us (4%)
  between operations  1.59 us (1%)
    pallas_call x1, Pallas kernels, fresh_image_of(): pl.pallas_call(kernel, out_shape=jax.ShapeDtypeStruct(image_plane.shape,...  34.5 us
    ppermute x1, waiting for transfers between devices, local(): fresh_before = lax.ppermute(flat, 'dom', forward)  31.3 us
    pallas_call x1, Pallas kernels, post_of(): pl.pallas_call(functools.partial(post_kernel, cut=SOFT_CUT), out_shape=ja...  11.3 us
    ppermute x4, waiting for transfers between devices, tree_sum(): value = value + lax.ppermute(value, axis, pairs)  9.71 us
    unnamed x17, local copies, waits for them, and re-layouts  8.08 us
    pallas_call x1, Pallas kernels, shrink_of(): pl.pallas_call(functools.partial(solve_kernel, steps=10), out_shape=jax.S...  6.07 us
    ppermute x1, starting transfers between devices, local(): fresh_before = lax.ppermute(flat, 'dom', forward)  5.49 us
    neg x2, other arithmetic, rotate(): -field_values[..., half_width:]  4.27 us
  transfers between devices with their start and end apart: 6, of which 6 were waited for; matrix products, arithmetic and copies ran while one was open for 4% of the time, Pallas kernels for 5%

profile of v9, /device:TPU:19, one launch (start us, length us, event | category | flops | bytes accessed | tf_op | source)
XLA Modules:
  0.0 133.3 jit_solution(11427238042284839262)
XLA Ops:
  0.0 1.0 slice_negate_fusion.1
  1.1 0.9 copy.31.btr_ref
  2.0 1.5 %copy.19 = s32[1,64,6,5,2]{4,3,2,1,0:T(8,128)S(1)} copy(s32[1,64,6,5,2]{1,4,3,2,0:T(2,128)} %param.12) | data formatting | bytes 30720 | tf_op args[4]
  3.6 0.9 reshape_squeeze.6.idx_ref
  4.5 1.1 copy.49
  5.6 0.9 copy.30.bt_ref
  7.1 0.7 reduce.3
  7.9 0.5 broadcast_minimum_fusion.nsl_ref
  8.5 34.5 %shard_map.82 = bf16[64,128,128]{2,1,0:T(8,128)(2,1)} custom-call(s32[3840]{0:T(1024)} %reshape_squeeze.6.idx_ref, s32[64]{0:T(128)} %bitcast.51, s32[2]{0:T(128)} %broadcast_minimum_fusion.nsl_ref, bf16[64,128,128]{2,1,0:T(8,128)(2,1)} %bitcast.49, bf16[64,128,128]{2,1,0:T(8,128)(2,1)} %bitcast.50, bf16[128,16,128]{2,1,0:T(8,128)(2,1)} %bitcast.46, ...), custom_call_target="tpu_custom_call" | custom-call | flops 6039797760 | bytes 6815744 | tf_op jit(solution)/shard_map/pallas_call | solution.py:186
  43.0 3.2 %slice_negate_fusion = (bf16[64,128,64]{2,1,0:T(8,128)(2,1)S(1)}, bf16[64,128,64]{2,1,0:T(8,128)(2,1)S(1)}) fusion(bf16[64,128,128]{2,1,0:T(8,128)(2,1)} %shard_map.82), kind=kLoop, calls=%fused_computation.1 | loop fusion | flops 524288 | bytes 4194304 | tf_op jit(solution)/shard_map/neg | solution.py:28
  46.2 2.4 %fusion.5 = f32[1,64,64]{2,1,0:T(8,128)S(1)} fusion(bf16[64,128,128]{2,1,0:T(8,128)(2,1)S(1)} %copy-done), kind=kOutput, calls=%fused_computation.8 | convolution fusion | flops 134217728 | bytes 2113536 | tf_op jit(solution)/shard_map/fn,gn->fg/dot_general | solution.py:349
  48.7 1.2 pad_maximum_fusion
  49.9 2.4 %fusion.8 = f32[1,64,64]{2,1,0:T(8,128)S(1)} fusion(bf16[64,128,128]{2,1,0:T(8,128)(2,1)S(1)} %copy-done, bf16[64,128,128]{2,1,0:T(8,128)(2,1)S(1)} %pad_maximum_fusion), kind=kOutput, calls=%fused_computation.9 | convolution fusion | flops 134217728 | bytes 4210688 | tf_op jit(solution)/shard_map/fn,gn->fg/dot_general | solution.py:350
  52.3 0.8 collective-permute-start
  53.1 0.9 collective-permute-done
  54.1 3.1 %collective-permute-done.1 = f32[2,64,64]{2,1,0:T(8,128)S(1)} collective-permute-done((f32[2,64,64]{2,1,0:T(8,128)S(1)}, f32[2,64,64]{2,1,0:T(8,128)S(1)}, u32[]{:S(2)}, u32[]{:S(2)}) %collective-permute-start.1) | collective-permute-done | bytes 32800 | tf_op jit(solution)/shard_map/ppermute | solution.py:327
  57.3 3.1 %collective-permute-done.2 = f32[2,64,64]{2,1,0:T(8,128)S(1)} collective-permute-done((f32[2,64,64]{2,1,0:T(8,128)S(1)}, f32[2,64,64]{2,1,0:T(8,128)S(1)}, u32[]{:S(2)}, u32[]{:S(2)}) %collective-permute-start.2) | collective-permute-done | bytes 32800 | tf_op jit(solution)/shard_map/ppermute | solution.py:327
  60.5 1.4 %copy.48 = bf16[8,8,128,128]{3,1,2,0:T(8,128)(2,1)S(1)} copy(bf16[8,8,128,128]{3,2,1,0:T(8,128)(2,1)S(1)} %bitcast.37) | data formatting | bytes 4194304
  61.9 2.6 %collective-permute-done.3 = f32[2,64,64]{2,1,0:T(8,128)S(1)} collective-permute-done((f32[2,64,64]{2,1,0:T(8,128)S(1)}, f32[2,64,64]{2,1,0:T(8,128)S(1)}, u32[]{:S(2)}, u32[]{:S(2)}) %collective-permute-start.3) | collective-permute-done | bytes 32800 | tf_op jit(solution)/shard_map/ppermute | solution.py:327
  64.6 5.5 %collective-permute-start.4 = (bf16[64,16384]{1,0:T(8,128)(2,1)S(1)}, bf16[64,16384]{1,0:T(8,128)(2,1)}, u32[]{:S(2)}, u32[]{:S(2)}) collective-permute-start(bf16[64,16384]{1,0:T(8,128)(2,1)S(1)} %bitcast.38), channel_id=1, source_target_pairs={{0,1},{1,2},{2,3},{3,4},{4,5},{5,6},{6,7},{7,8},{8,9},{9,10},{10,1... | collective-permute-start | bytes 6291464 | tf_op jit(solution)/shard_map/ppermute | solution.py:353
  70.1 2.1 %collective-permute-start.5 = (bf16[64,16384]{1,0:T(8,128)(2,1)S(1)}, bf16[64,16384]{1,0:T(8,128)(2,1)}, u32[]{:S(2)}, u32[]{:S(2)}) collective-permute-start(bf16[64,16384]{1,0:T(8,128)(2,1)S(1)} %bitcast.39), channel_id=1, source_target_pairs={{1,0},{2,1},{3,2},{4,3},{5,4},{6,5},{7,6},{8,7},{9,8},{10,9},{11,1... | collective-permute-start | bytes 6291464 | tf_op jit(solution)/shard_map/ppermute | solution.py:354
  73.1 0.6 maximum_bitcast_fusion.wz_ref
  73.7 0.7 select_reduce_fusion
  75.1 0.6 fusion.13.x0_ref
  75.7 0.7 select_add_fusion
  76.5 6.1 %shard_map.83 = f32[128,128]{1,0:T(8,128)} custom-call(f32[128,128]{1,0:T(8,128)} %get-tuple-element.11.a_ref, f32[128,128]{1,0:T(8,128)} %fusion.13.x0_ref, f32[128,128]{1,0:T(8,128)} %get-tuple-element.12.s_ref), custom_call_target="tpu_custom_call" | custom-call | tf_op jit(solution)/shard_map/pallas_call | solution.py:296
  82.5 0.9 copy.27
  83.6 0.6 maximum_bitcast_fusion.1.wl_ref
  84.2 31.3 %collective-permute-done.4.xb_ref = bf16[64,16384]{1,0:T(8,128)(2,1)} collective-permute-done((bf16[64,16384]{1,0:T(8,128)(2,1)S(1)}, bf16[64,16384]{1,0:T(8,128)(2,1)}, u32[]{:S(2)}, u32[]{:S(2)}) %collective-permute-start.4) | collective-permute-done | bytes 2097184 | tf_op jit(solution)/shard_map/ppermute | solution.py:353
  115.5 3.0 %collective-permute-done.5.xa_ref = bf16[64,16384]{1,0:T(8,128)(2,1)} collective-permute-done((bf16[64,16384]{1,0:T(8,128)(2,1)S(1)}, bf16[64,16384]{1,0:T(8,128)(2,1)}, u32[]{:S(2)}, u32[]{:S(2)}) %collective-permute-start.5) | collective-permute-done | bytes 2097184 | tf_op jit(solution)/shard_map/ppermute | solution.py:354
  118.5 11.3 %shard_map.84 = bf16[64,16384]{1,0:T(8,128)(2,1)} custom-call(bf16[64,16384]{1,0:T(8,128)(2,1)} %bitcast.40, bf16[64,16384]{1,0:T(8,128)(2,1)} %collective-permute-done.4.xb_ref, bf16[64,16384]{1,0:T(8,128)(2,1)} %collective-permute-done.5.xa_ref, bf16[128,64]{1,0:T(8,128)(2,1)} %maximum_bitcast_fusion.1.wl_ref, bf16[128,192]{1,0:T(8,128)(2,1)} %maximum_bitcast_fusion.wz_ref), custom_call_target="tpu_custom_call" | custom-call | flops 1610612736 | bytes 8388608 | tf_op jit(solution)/shard_map/pallas_call | solution.py:258
  129.8 3.5 %copy.33 = bf16[8,8,128,128]{3,2,1,0:T(8,128)(2,1)} copy(bf16[8,8,128,128]{3,1,2,0:T(8,128)(2,1)} %bitcast.41) | data formatting | bytes 4194304
  (30 shorter events, 1.3 us)
Async XLA Ops:
  1.0 3.5 %copy-start.3 = (bf16[1,16,128,128]{3,2,1,0:T(8,128)(2,1)S(1)}, bf16[1,16,128,128]{3,2,1,0:T(8,128)(2,1)}, u32[]{:S(2)}) copy-start(bf16[1,16,128,128]{3,2,1,0:T(8,128)(2,1)} %param.10) | copy-start | bytes 1572868
  2.0 3.6 %copy-start.2 = (bf16[5,2,128,128]{3,2,1,0:T(8,128)(2,1)S(1)}, bf16[5,2,128,128]{3,2,1,0:T(8,128)(2,1)}, u32[]{:S(2)}) copy-start(bf16[5,2,128,128]{3,2,1,0:T(8,128)(2,1)} %param.13) | copy-start | bytes 983044
  2.0 5.1 %copy-start.5 = (s32[1,64]{1,0:T(1,128)S(1)}, s32[1,64]{1,0:T(1,128)}, u32[]{:S(2)}) copy-start(s32[1,64]{1,0:T(1,128)} %param.11) | copy-start | bytes 772
  43.0 3.2 %copy-start = (bf16[64,128,128]{2,1,0:T(8,128)(2,1)S(1)}, bf16[64,128,128]{2,1,0:T(8,128)(2,1)}, u32[]{:S(2)}) copy-start(bf16[64,128,128]{2,1,0:T(8,128)(2,1)} %shard_map.82) | copy-start | bytes 6291460
  52.3 1.7 %collective-permute-start = (f32[2,64,64]{2,1,0:T(8,128)S(1)}, f32[2,64,64]{2,1,0:T(8,128)S(1)}, u32[]{:S(2)}, u32[]{:S(2)}) collective-permute-start(f32[2,64,64]{2,1,0:T(8,128)S(1)} %pad_maximum_fusion.2), channel_id=1, source_target_pairs={{0,1},{1,0},{2,3},{3,2},{4,5},{5,4},{6,7},{7,6},{8,9},{9,8},{10,11... | collective-permute-start | bytes 98312 | tf_op jit(solution)/shard_map/ppermute | solution.py:327
  54.1 3.2 %collective-permute-start.1 = (f32[2,64,64]{2,1,0:T(8,128)S(1)}, f32[2,64,64]{2,1,0:T(8,128)S(1)}, u32[]{:S(2)}, u32[]{:S(2)}) collective-permute-start(f32[2,64,64]{2,1,0:T(8,128)S(1)} %fusion.14), channel_id=1, source_target_pairs={{0,2},{1,3},{2,0},{3,1},{4,6},{5,7},{6,4},{7,5},{8,10},{9,11},{10,... | collective-permute-start | bytes 98312 | tf_op jit(solution)/shard_map/ppermute | solution.py:327
  57.3 3.2 %collective-permute-start.2 = (f32[2,64,64]{2,1,0:T(8,128)S(1)}, f32[2,64,64]{2,1,0:T(8,128)S(1)}, u32[]{:S(2)}, u32[]{:S(2)}) collective-permute-start(f32[2,64,64]{2,1,0:T(8,128)S(1)} %fusion.17), channel_id=1, source_target_pairs={{0,4},{1,5},{2,6},{3,7},{4,0},{5,1},{6,2},{7,3},{8,12},{9,13},{10,... | collective-permute-start | bytes 98312 | tf_op jit(solution)/shard_map/ppermute | solution.py:327
  60.5 4.1 %collective-permute-start.3 = (f32[2,64,64]{2,1,0:T(8,128)S(1)}, f32[2,64,64]{2,1,0:T(8,128)S(1)}, u32[]{:S(2)}, u32[]{:S(2)}) collective-permute-start(f32[2,64,64]{2,1,0:T(8,128)S(1)} %add.20), channel_id=1, source_target_pairs={{0,8},{1,9},{2,10},{3,11},{4,12},{5,13},{6,14},{7,15},{8,0},{9,1},... | collective-permute-start | bytes 98312 | tf_op jit(solution)/shard_map/ppermute | solution.py:327
  60.5 12.3 %copy-start.4 = (bf16[3,2,64,64]{3,2,1,0:T(8,128)(2,1)S(1)}, bf16[3,2,64,64]{3,2,1,0:T(8,128)(2,1)}, u32[]{:S(2)}) copy-start(bf16[3,2,64,64]{3,2,1,0:T(8,128)(2,1)} %param.14) | copy-start | bytes 147460
  61.9 56.6 %copy-start.1 = (bf16[8,8,128,128]{3,1,2,0:T(8,128)(2,1)}, bf16[8,8,128,128]{3,1,2,0:T(8,128)(2,1)S(1)}, u32[]{:S(2)}) copy-start(bf16[8,8,128,128]{3,1,2,0:T(8,128)(2,1)S(1)} %copy.48) | copy-start | bytes 6291460
  64.6 50.9 %collective-permute-start.4 = (bf16[64,16384]{1,0:T(8,128)(2,1)S(1)}, bf16[64,16384]{1,0:T(8,128)(2,1)}, u32[]{:S(2)}, u32[]{:S(2)}) collective-permute-start(bf16[64,16384]{1,0:T(8,128)(2,1)S(1)} %bitcast.38), channel_id=1, source_target_pairs={{0,1},{1,2},{2,3},{3,4},{4,5},{5,6},{6,7},{7,8},{8,9},{9,10},{10,1... | collective-permute-start | bytes 6291464 | tf_op jit(solution)/shard_map/ppermute | solution.py:353
  70.1 48.4 %collective-permute-start.5 = (bf16[64,16384]{1,0:T(8,128)(2,1)S(1)}, bf16[64,16384]{1,0:T(8,128)(2,1)}, u32[]{:S(2)}, u32[]{:S(2)}) collective-permute-start(bf16[64,16384]{1,0:T(8,128)(2,1)S(1)} %bitcast.39), channel_id=1, source_target_pairs={{1,0},{2,1},{3,2},{4,3},{5,4},{6,5},{7,6},{8,7},{9,8},{10,9},{11,1... | collective-permute-start | bytes 6291464 | tf_op jit(solution)/shard_map/ppermute | solution.py:354

commit v10 on v9

--- a/solution.py
+++ b/solution.py
@@ -220,8 +220,7 @@
     )(idx, cnt, nsl, image_plane, adjoint_plane, maps_t, bf, bt, btr)
 
 
-def post_kernel(x_ref, xb_ref, xa_ref, wl_ref, wz_ref, out_ref, *, cut):
-    frames, width = x_ref.shape
+def lane_tools(frames, width):
     lane = lax.broadcasted_iota(jnp.int32, (frames, width), 1) % 128
     low_lane = lane < 64
 
@@ -231,23 +230,40 @@
     def pair(v):
         return jnp.where(low_lane, pltpu.roll(v, width - 64, 1), pltpu.roll(v, 64, 1))
 
-    def low_of(plane):
-        mixed = jnp.dot(wl_ref[...], plane, preferred_element_type=jnp.float32)
-        return mixed[:frames] + turn(mixed[frames:])
+    return turn, pair
+
+
+def low_of(wl_ref, plane, turn):
+    frames = plane.shape[0]
+    mixed = jnp.dot(wl_ref[...], plane, preferred_element_type=jnp.float32)
+    return mixed[:frames] + turn(mixed[frames:])
+
+
+def own_kernel(x_ref, wl_ref, low_ref, rem_ref):
+    frames, width = x_ref.shape
+    turn, _ = lane_tools(frames, width)
+    x = x_ref[...]
+    low = low_of(wl_ref, x, turn)
+    low_ref[...] = low
+    rem_ref[...] = (x.astype(jnp.float32) - low).astype(jnp.bfloat16)
+
+
+def post_kernel(low_ref, rem_ref, xb_ref, xa_ref, wl_ref, wz_ref, out_ref, *, cut):
+    frames, width = rem_ref.shape
+    turn, pair = lane_tools(frames, width)
 
     def remainder_of(plane):
-        return (plane.astype(jnp.float32) - low_of(plane)).astype(jnp.bfloat16)
-
-    x = x_ref[...]
-    low = low_of(x)
-    rem = (x.astype(jnp.float32) - low).astype(jnp.bfloat16)
-    planes = jnp.concatenate([remainder_of(xb_ref[...]), rem, remainder_of(xa_ref[...])], axis=0)
+        return (plane.astype(jnp.float32) - low_of(wl_ref, plane, turn)).astype(jnp.bfloat16)
+
+    planes = jnp.concatenate(
+        [remainder_of(xb_ref[...]), rem_ref[...], remainder_of(xa_ref[...])], axis=0
+    )
     mixed = jnp.dot(wz_ref[...], planes, preferred_element_type=jnp.float32)
     filtered = mixed[:frames] + turn(mixed[frames:])
     square = filtered * filtered
     magnitude = jnp.sqrt(square + pair(square))
     scale = jnp.maximum(magnitude - cut, 0.0) / jnp.maximum(magnitude, cut)
-    out_ref[...] = (low + filtered * scale).astype(out_ref.dtype)
+    out_ref[...] = (low_ref[...] + filtered * scale).astype(out_ref.dtype)
 
 
 def post_of(plane, before, after, low_t, filter_t):
@@ -255,18 +271,34 @@
     nb = 4096 if width % 4096 == 0 else width
     lane_spec = pl.BlockSpec((frames, nb), lambda i: (0, i))
     whole2 = lambda shape: pl.BlockSpec(shape, lambda i: (0, 0))
+    params = pltpu.CompilerParams(dimension_semantics=("arbitrary",))
+    low, rem = pl.pallas_call(
+        own_kernel,
+        out_shape=(
+            jax.ShapeDtypeStruct(plane.shape, jnp.float32),
+            jax.ShapeDtypeStruct(plane.shape, jnp.bfloat16),
+        ),
+        grid=(width // nb,),
+        in_specs=[lane_spec, whole2(low_t.shape)],
+        out_specs=(lane_spec, lane_spec),
+        compiler_params=params,
+        cost_estimate=pl.CostEstimate(
+            flops=2 * width * frames * (2 * frames), transcendentals=0,
+            bytes_accessed=plane.size * 8,
+        ),
+    )(plane, low_t)
     return pl.pallas_call(
         functools.partial(post_kernel, cut=SOFT_CUT),
         out_shape=jax.ShapeDtypeStruct(plane.shape, jnp.bfloat16),
         grid=(width // nb,),
-        in_specs=[lane_spec, lane_spec, lane_spec, whole2(low_t.shape), whole2(filter_t.shape)],
+        in_specs=[lane_spec] * 4 + [whole2(low_t.shape), whole2(filter_t.shape)],
         out_specs=lane_spec,
-        compiler_params=pltpu.CompilerParams(dimension_semantics=("arbitrary",)),
+        compiler_params=params,
         cost_estimate=pl.CostEstimate(
-            flops=2 * width * frames * (2 * frames) * 6, transcendentals=width * frames,
-            bytes_accessed=plane.size * 8,
-        ),
-    )(plane, before, after, low_t, filter_t)
+            flops=2 * width * frames * (2 * frames) * 5, transcendentals=width * frames,
+            bytes_accessed=plane.size * 12,
+        ),
+    )(low, rem, before, after, low_t, filter_t)
 
 
 def solve_kernel(a_ref, x0_ref, s_ref, out_ref, *, steps):

time: 134 us -> 133 us (level)
  waiting for transfers between devices: 44 us -> 38.4 us
  Pallas kernels: 51.9 us -> 56.5 us
    pallas_call x0 -> x1, Pallas kernels: none -> 5.6 us  [post_of(): pl.pallas_call(own_kernel, out_shape=(jax.ShapeDtypeStruct(plane.shape, j...]
    ppermute x1, waiting for transfers between devices: 31.3 us -> 25.7 us  [local(): fresh_before = lax.ppermute(flat, 'dom', forward)]
  transfers between devices with their start and end apart: 6 -> 6, of which waited for: 6 -> 6; matrix products, arithmetic and copies ran while one was open for 4% -> 4% of each run, Pallas kernels for 5% -> 9%
where the time goes in v10:
time: 133 us; the launch traced here: 132 us
  Pallas kernels  56.5 us (42%)
  waiting for transfers between devices  38.4 us (29%)
  local copies, waits for them, and re-layouts  12.2 us (9%)
  other arithmetic  10.2 us (8%)
  starting transfers between devices  8.61 us (6%)
  matrix products  4.84 us (4%)
  between operations  1.54 us (1%)
    pallas_call x1, Pallas kernels, fresh_image_of(): pl.pallas_call(kernel, out_shape=jax.ShapeDtypeStruct(image_plane.shape,...  34.6 us
    ppermute x1, waiting for transfers between devices, local(): fresh_before = lax.ppermute(flat, 'dom', forward)  25.7 us
    pallas_call x1, Pallas kernels, post_of(): pl.pallas_call(functools.partial(post_kernel, cut=SOFT_CUT), out_shape=ja...  10.2 us
    ppermute x4, waiting for transfers between devices, tree_sum(): value = value + lax.ppermute(value, axis, pairs)  9.71 us
    unnamed x17, local copies, waits for them, and re-layouts  8.07 us
    pallas_call x1, Pallas kernels, shrink_of(): pl.pallas_call(functools.partial(solve_kernel, steps=10), out_shape=jax.S...  6.08 us
    pallas_call x1, Pallas kernels, post_of(): pl.pallas_call(own_kernel, out_shape=(jax.ShapeDtypeStruct(plane.shape, j...  5.6 us
    ppermute x1, starting transfers between devices, local(): fresh_before = lax.ppermute(flat, 'dom', forward)  5.49 us
  transfers between devices with their start and end apart: 6, of which 6 were waited for; matrix products, arithmetic and copies ran while one was open for 4% of the time, Pallas kernels for 9%

profile of v10, /device:TPU:19, one launch (start us, length us, event | category | flops | bytes accessed | tf_op | source)
XLA Modules:
  0.0 132.3 jit_solution(1294157067878109731)
XLA Ops:
  0.0 1.0 slice_negate_fusion.1
  1.1 0.9 copy.31.btr_ref
  2.0 1.5 %copy.19 = s32[1,64,6,5,2]{4,3,2,1,0:T(8,128)S(1)} copy(s32[1,64,6,5,2]{1,4,3,2,0:T(2,128)} %param.12) | data formatting | bytes 30720 | tf_op args[4]
  3.6 0.9 reshape_squeeze.6.idx_ref
  4.5 1.1 copy.49
  5.6 0.9 copy.30.bt_ref
  7.1 0.7 reduce.3
  8.5 34.6 %shard_map.82 = bf16[64,128,128]{2,1,0:T(8,128)(2,1)} custom-call(s32[3840]{0:T(1024)} %reshape_squeeze.6.idx_ref, s32[64]{0:T(128)} %bitcast.51, s32[2]{0:T(128)} %broadcast_minimum_fusion.nsl_ref, bf16[64,128,128]{2,1,0:T(8,128)(2,1)} %bitcast.49, bf16[64,128,128]{2,1,0:T(8,128)(2,1)} %bitcast.50, bf16[128,16,128]{2,1,0:T(8,128)(2,1)} %bitcast.46, ...), custom_call_target="tpu_custom_call" | custom-call | flops 6039797760 | bytes 6815744 | tf_op jit(solution)/shard_map/pallas_call | solution.py:186
  43.1 3.2 %slice_negate_fusion = (bf16[64,128,64]{2,1,0:T(8,128)(2,1)S(1)}, bf16[64,128,64]{2,1,0:T(8,128)(2,1)S(1)}) fusion(bf16[64,128,128]{2,1,0:T(8,128)(2,1)} %shard_map.82), kind=kLoop, calls=%fused_computation.1 | loop fusion | flops 524288 | bytes 4194304 | tf_op jit(solution)/shard_map/neg | solution.py:28
  46.3 2.4 %fusion.5 = f32[1,64,64]{2,1,0:T(8,128)S(1)} fusion(bf16[64,128,128]{2,1,0:T(8,128)(2,1)S(1)} %copy-done), kind=kOutput, calls=%fused_computation.8 | convolution fusion | flops 134217728 | bytes 2113536 | tf_op jit(solution)/shard_map/fn,gn->fg/dot_general | solution.py:381
  48.8 1.2 pad_maximum_fusion
  50.0 2.4 %fusion.8 = f32[1,64,64]{2,1,0:T(8,128)S(1)} fusion(bf16[64,128,128]{2,1,0:T(8,128)(2,1)S(1)} %copy-done, bf16[64,128,128]{2,1,0:T(8,128)(2,1)S(1)} %pad_maximum_fusion), kind=kOutput, calls=%fused_computation.9 | convolution fusion | flops 134217728 | bytes 4210688 | tf_op jit(solution)/shard_map/fn,gn->fg/dot_general | solution.py:382
  52.4 0.8 collective-permute-start
  53.2 0.9 collective-permute-done
  54.2 3.1 %collective-permute-done.1 = f32[2,64,64]{2,1,0:T(8,128)S(1)} collective-permute-done((f32[2,64,64]{2,1,0:T(8,128)S(1)}, f32[2,64,64]{2,1,0:T(8,128)S(1)}, u32[]{:S(2)}, u32[]{:S(2)}) %collective-permute-start.1) | collective-permute-done | bytes 32800 | tf_op jit(solution)/shard_map/ppermute | solution.py:359
  57.4 3.1 %collective-permute-done.2 = f32[2,64,64]{2,1,0:T(8,128)S(1)} collective-permute-done((f32[2,64,64]{2,1,0:T(8,128)S(1)}, f32[2,64,64]{2,1,0:T(8,128)S(1)}, u32[]{:S(2)}, u32[]{:S(2)}) %collective-permute-start.2) | collective-permute-done | bytes 32800 | tf_op jit(solution)/shard_map/ppermute | solution.py:359
  60.6 1.4 %copy.48 = bf16[8,8,128,128]{3,1,2,0:T(8,128)(2,1)S(1)} copy(bf16[8,8,128,128]{3,2,1,0:T(8,128)(2,1)S(1)} %bitcast.37) | data formatting | bytes 4194304
  62.0 2.6 %collective-permute-done.3 = f32[2,64,64]{2,1,0:T(8,128)S(1)} collective-permute-done((f32[2,64,64]{2,1,0:T(8,128)S(1)}, f32[2,64,64]{2,1,0:T(8,128)S(1)}, u32[]{:S(2)}, u32[]{:S(2)}) %collective-permute-start.3) | collective-permute-done | bytes 32800 | tf_op jit(solution)/shard_map/ppermute | solution.py:359
  64.6 5.5 %collective-permute-start.4 = (bf16[64,16384]{1,0:T(8,128)(2,1)S(1)}, bf16[64,16384]{1,0:T(8,128)(2,1)}, u32[]{:S(2)}, u32[]{:S(2)}) collective-permute-start(bf16[64,16384]{1,0:T(8,128)(2,1)S(1)} %bitcast.38), channel_id=1, source_target_pairs={{0,1},{1,2},{2,3},{3,4},{4,5},{5,6},{6,7},{7,8},{8,9},{9,10},{10,1... | collective-permute-start | bytes 6291464 | tf_op jit(solution)/shard_map/ppermute | solution.py:385
  70.1 2.1 %collective-permute-start.5 = (bf16[64,16384]{1,0:T(8,128)(2,1)S(1)}, bf16[64,16384]{1,0:T(8,128)(2,1)}, u32[]{:S(2)}, u32[]{:S(2)}) collective-permute-start(bf16[64,16384]{1,0:T(8,128)(2,1)S(1)} %bitcast.39), channel_id=1, source_target_pairs={{1,0},{2,1},{3,2},{4,3},{5,4},{6,5},{7,6},{8,7},{9,8},{10,9},{11,1... | collective-permute-start | bytes 6291464 | tf_op jit(solution)/shard_map/ppermute | solution.py:386
  73.1 0.6 maximum_bitcast_fusion.wz_ref
  73.8 0.7 select_reduce_fusion
  75.1 0.6 fusion.13.x0_ref
  75.8 0.7 select_add_fusion
  76.5 6.1 %shard_map.83 = f32[128,128]{1,0:T(8,128)} custom-call(f32[128,128]{1,0:T(8,128)} %get-tuple-element.15.a_ref, f32[128,128]{1,0:T(8,128)} %fusion.13.x0_ref, f32[128,128]{1,0:T(8,128)} %get-tuple-element.16.s_ref), custom_call_target="tpu_custom_call" | custom-call | tf_op jit(solution)/shard_map/pallas_call | solution.py:328
  82.6 0.9 copy.27
  83.6 0.6 maximum_bitcast_fusion.1.wl_ref
  84.2 5.6 %shard_map.84 = (f32[64,16384]{1,0:T(8,128)}, bf16[64,16384]{1,0:T(8,128)(2,1)}) custom-call(bf16[64,16384]{1,0:T(8,128)(2,1)} %bitcast.40, bf16[128,64]{1,0:T(8,128)(2,1)} %maximum_bitcast_fusion.1.wl_ref), custom_call_target="tpu_custom_call" | custom-call | flops 268435456 | bytes 8388608 | tf_op jit(solution)/shard_map/pallas_call | solution.py:275
  89.8 25.7 %collective-permute-done.4.xb_ref = bf16[64,16384]{1,0:T(8,128)(2,1)} collective-permute-done((bf16[64,16384]{1,0:T(8,128)(2,1)S(1)}, bf16[64,16384]{1,0:T(8,128)(2,1)}, u32[]{:S(2)}, u32[]{:S(2)}) %collective-permute-start.4) | collective-permute-done | bytes 2097184 | tf_op jit(solution)/shard_map/ppermute | solution.py:385
  115.5 3.0 %collective-permute-done.5.xa_ref = bf16[64,16384]{1,0:T(8,128)(2,1)} collective-permute-done((bf16[64,16384]{1,0:T(8,128)(2,1)S(1)}, bf16[64,16384]{1,0:T(8,128)(2,1)}, u32[]{:S(2)}, u32[]{:S(2)}) %collective-permute-start.5) | collective-permute-done | bytes 2097184 | tf_op jit(solution)/shard_map/ppermute | solution.py:386
  118.6 10.2 %shard_map.85 = bf16[64,16384]{1,0:T(8,128)(2,1)} custom-call(f32[64,16384]{1,0:T(8,128)} %get-tuple-element.13.low_ref, bf16[64,16384]{1,0:T(8,128)(2,1)} %get-tuple-element.14.rem_ref, bf16[64,16384]{1,0:T(8,128)(2,1)} %collective-permute-done.4.xb_ref, bf16[64,16384]{1,0:T(8,128)(2,1)} %collective-permute-done.5.xa_ref, ...), custom_call_target="tpu_custom_call" | custom-call | flops 1342177280 | bytes 12582912 | tf_op jit(solution)/shard_map/pallas_call | solution.py:290
  128.8 3.5 %copy.33 = bf16[8,8,128,128]{3,2,1,0:T(8,128)(2,1)} copy(bf16[8,8,128,128]{3,1,2,0:T(8,128)(2,1)} %bitcast.41) | data formatting | bytes 4194304
  (31 shorter events, 1.9 us)
Async XLA Ops:
  1.0 3.5 %copy-start.3 = (bf16[1,16,128,128]{3,2,1,0:T(8,128)(2,1)S(1)}, bf16[1,16,128,128]{3,2,1,0:T(8,128)(2,1)}, u32[]{:S(2)}) copy-start(bf16[1,16,128,128]{3,2,1,0:T(8,128)(2,1)} %param.10) | copy-start | bytes 1572868
  2.0 3.6 %copy-start.2 = (bf16[5,2,128,128]{3,2,1,0:T(8,128)(2,1)S(1)}, bf16[5,2,128,128]{3,2,1,0:T(8,128)(2,1)}, u32[]{:S(2)}) copy-start(bf16[5,2,128,128]{3,2,1,0:T(8,128)(2,1)} %param.13) | copy-start | bytes 983044
  2.0 5.1 %copy-start.5 = (s32[1,64]{1,0:T(1,128)S(1)}, s32[1,64]{1,0:T(1,128)}, u32[]{:S(2)}) copy-start(s32[1,64]{1,0:T(1,128)} %param.11) | copy-start | bytes 772
  43.1 3.2 %copy-start = (bf16[64,128,128]{2,1,0:T(8,128)(2,1)S(1)}, bf16[64,128,128]{2,1,0:T(8,128)(2,1)}, u32[]{:S(2)}) copy-start(bf16[64,128,128]{2,1,0:T(8,128)(2,1)} %shard_map.82) | copy-start | bytes 6291460
  52.4 1.7 %collective-permute-start = (f32[2,64,64]{2,1,0:T(8,128)S(1)}, f32[2,64,64]{2,1,0:T(8,128)S(1)}, u32[]{:S(2)}, u32[]{:S(2)}) collective-permute-start(f32[2,64,64]{2,1,0:T(8,128)S(1)} %pad_maximum_fusion.2), channel_id=1, source_target_pairs={{0,1},{1,0},{2,3},{3,2},{4,5},{5,4},{6,7},{7,6},{8,9},{9,8},{10,11... | collective-permute-start | bytes 98312 | tf_op jit(solution)/shard_map/ppermute | solution.py:359
  54.1 3.2 %collective-permute-start.1 = (f32[2,64,64]{2,1,0:T(8,128)S(1)}, f32[2,64,64]{2,1,0:T(8,128)S(1)}, u32[]{:S(2)}, u32[]{:S(2)}) collective-permute-start(f32[2,64,64]{2,1,0:T(8,128)S(1)} %fusion.14), channel_id=1, source_target_pairs={{0,2},{1,3},{2,0},{3,1},{4,6},{5,7},{6,4},{7,5},{8,10},{9,11},{10,... | collective-permute-start | bytes 98312 | tf_op jit(solution)/shard_map/ppermute | solution.py:359
  57.3 3.2 %collective-permute-start.2 = (f32[2,64,64]{2,1,0:T(8,128)S(1)}, f32[2,64,64]{2,1,0:T(8,128)S(1)}, u32[]{:S(2)}, u32[]{:S(2)}) collective-permute-start(f32[2,64,64]{2,1,0:T(8,128)S(1)} %fusion.17), channel_id=1, source_target_pairs={{0,4},{1,5},{2,6},{3,7},{4,0},{5,1},{6,2},{7,3},{8,12},{9,13},{10,... | collective-permute-start | bytes 98312 | tf_op jit(solution)/shard_map/ppermute | solution.py:359
  60.5 4.1 %collective-permute-start.3 = (f32[2,64,64]{2,1,0:T(8,128)S(1)}, f32[2,64,64]{2,1,0:T(8,128)S(1)}, u32[]{:S(2)}, u32[]{:S(2)}) collective-permute-start(f32[2,64,64]{2,1,0:T(8,128)S(1)} %add.20), channel_id=1, source_target_pairs={{0,8},{1,9},{2,10},{3,11},{4,12},{5,13},{6,14},{7,15},{8,0},{9,1},... | collective-permute-start | bytes 98312 | tf_op jit(solution)/shard_map/ppermute | solution.py:359
  60.6 12.3 %copy-start.4 = (bf16[3,2,64,64]{3,2,1,0:T(8,128)(2,1)S(1)}, bf16[3,2,64,64]{3,2,1,0:T(8,128)(2,1)}, u32[]{:S(2)}) copy-start(bf16[3,2,64,64]{3,2,1,0:T(8,128)(2,1)} %param.14) | copy-start | bytes 147460
  62.0 22.3 %copy-start.1 = (bf16[8,8,128,128]{3,1,2,0:T(8,128)(2,1)}, bf16[8,8,128,128]{3,1,2,0:T(8,128)(2,1)S(1)}, u32[]{:S(2)}) copy-start(bf16[8,8,128,128]{3,1,2,0:T(8,128)(2,1)S(1)} %copy.48) | copy-start | bytes 6291460
  64.6 50.9 %collective-permute-start.4 = (bf16[64,16384]{1,0:T(8,128)(2,1)S(1)}, bf16[64,16384]{1,0:T(8,128)(2,1)}, u32[]{:S(2)}, u32[]{:S(2)}) collective-permute-start(bf16[64,16384]{1,0:T(8,128)(2,1)S(1)} %bitcast.38), channel_id=1, source_target_pairs={{0,1},{1,2},{2,3},{3,4},{4,5},{5,6},{6,7},{7,8},{8,9},{9,10},{10,1... | collective-permute-start | bytes 6291464 | tf_op jit(solution)/shard_map/ppermute | solution.py:385
  70.1 48.4 %collective-permute-start.5 = (bf16[64,16384]{1,0:T(8,128)(2,1)S(1)}, bf16[64,16384]{1,0:T(8,128)(2,1)}, u32[]{:S(2)}, u32[]{:S(2)}) collective-permute-start(bf16[64,16384]{1,0:T(8,128)(2,1)S(1)} %bitcast.39), channel_id=1, source_target_pairs={{1,0},{2,1},{3,2},{4,3},{5,4},{6,5},{7,6},{8,7},{9,8},{10,9},{11,1... | collective-permute-start | bytes 6291464 | tf_op jit(solution)/shard_map/ppermute | solution.py:386

commit v11 on v10

--- a/solution.py
+++ b/solution.py
@@ -263,7 +263,8 @@
     square = filtered * filtered
     magnitude = jnp.sqrt(square + pair(square))
     scale = jnp.maximum(magnitude - cut, 0.0) / jnp.maximum(magnitude, cut)
-    out_ref[...] = (low_ref[...] + filtered * scale).astype(out_ref.dtype)
+    result = low_ref[...] + filtered * scale
+    out_ref[...] = result.reshape(out_ref.shape).astype(out_ref.dtype)
 
 
 def post_of(plane, before, after, low_t, filter_t):
@@ -287,12 +288,13 @@
             bytes_accessed=plane.size * 8,
         ),
     )(plane, low_t)
+    tile_spec = pl.BlockSpec((frames, nb // 128, 128), lambda i: (0, i, 0))
     return pl.pallas_call(
         functools.partial(post_kernel, cut=SOFT_CUT),
-        out_shape=jax.ShapeDtypeStruct(plane.shape, jnp.bfloat16),
+        out_shape=jax.ShapeDtypeStruct((frames, width // 128, 128), jnp.bfloat16),
         grid=(width // nb,),
         in_specs=[lane_spec] * 4 + [whole2(low_t.shape), whole2(filter_t.shape)],
-        out_specs=lane_spec,
+        out_specs=tile_spec,
         compiler_params=params,
         cost_estimate=pl.CostEstimate(
             flops=2 * width * frames * (2 * frames) * 5, transcendentals=width * frames,

time: 133 us -> 130 us (0.977)
  local copies, waits for them, and re-layouts: 12.2 us -> 8.66 us
    unnamed x17 -> x16, local copies, waits for them, and re-layouts: 8.07 us -> 4.58 us
where the time goes in v11:
time: 130 us; the launch traced here: 129 us
  Pallas kernels  57.2 us (44%)
  waiting for transfers between devices  38.5 us (30%)
  other arithmetic  10.1 us (8%)
  local copies, waits for them, and re-layouts  8.66 us (7%)
  starting transfers between devices  8.58 us (7%)
  matrix products  4.84 us (4%)
  between operations  1.49 us (1%)
    pallas_call x1, Pallas kernels, fresh_image_of(): pl.pallas_call(kernel, out_shape=jax.ShapeDtypeStruct(image_plane.shape,...  34.6 us
    ppermute x1, waiting for transfers between devices, local(): fresh_before = lax.ppermute(flat, 'dom', forward)  25.8 us
    pallas_call x1, Pallas kernels, post_of(): pl.pallas_call(functools.partial(post_kernel, cut=SOFT_CUT), out_shape=ja...  10.9 us
    ppermute x4, waiting for transfers between devices, tree_sum(): value = value + lax.ppermute(value, axis, pairs)  9.71 us
    pallas_call x1, Pallas kernels, shrink_of(): pl.pallas_call(functools.partial(solve_kernel, steps=10), out_shape=jax.S...  6.08 us
    pallas_call x1, Pallas kernels, post_of(): pl.pallas_call(own_kernel, out_shape=(jax.ShapeDtypeStruct(plane.shape, j...  5.6 us
    ppermute x1, starting transfers between devices, local(): fresh_before = lax.ppermute(flat, 'dom', forward)  5.49 us
    unnamed x16, local copies, waits for them, and re-layouts  4.58 us
  transfers between devices with their start and end apart: 6, of which 6 were waited for; matrix products, arithmetic and copies ran while one was open for 4% of the time, Pallas kernels for 9%

profile of v11, /device:TPU:19, one launch (start us, length us, event | category | flops | bytes accessed | tf_op | source)
XLA Modules:
  0.0 129.5 jit_solution(406641499869701358)
XLA Ops:
  0.0 1.0 slice_negate_fusion.1
  1.1 0.9 copy.31.btr_ref
  2.0 1.5 %copy.19 = s32[1,64,6,5,2]{4,3,2,1,0:T(8,128)S(1)} copy(s32[1,64,6,5,2]{1,4,3,2,0:T(2,128)} %param.12) | data formatting | bytes 30720 | tf_op args[4]
  3.6 0.9 reshape_squeeze.6.idx_ref
  4.5 1.1 copy.48
  5.6 0.9 copy.30.bt_ref
  7.1 0.7 reduce.3
  7.9 0.5 broadcast_minimum_fusion.nsl_ref
  8.5 34.6 %shard_map.82 = bf16[64,128,128]{2,1,0:T(8,128)(2,1)} custom-call(s32[3840]{0:T(1024)} %reshape_squeeze.6.idx_ref, s32[64]{0:T(128)} %bitcast.48, s32[2]{0:T(128)} %broadcast_minimum_fusion.nsl_ref, bf16[64,128,128]{2,1,0:T(8,128)(2,1)} %bitcast.46, bf16[64,128,128]{2,1,0:T(8,128)(2,1)} %bitcast.47, bf16[128,16,128]{2,1,0:T(8,128)(2,1)} %bitcast.43, ...), custom_call_target="tpu_custom_call" | custom-call | flops 6039797760 | bytes 6815744 | tf_op jit(solution)/shard_map/pallas_call | solution.py:186
  43.1 3.2 %slice_negate_fusion = (bf16[64,128,64]{2,1,0:T(8,128)(2,1)S(1)}, bf16[64,128,64]{2,1,0:T(8,128)(2,1)S(1)}) fusion(bf16[64,128,128]{2,1,0:T(8,128)(2,1)} %shard_map.82), kind=kLoop, calls=%fused_computation.1 | loop fusion | flops 524288 | bytes 4194304 | tf_op jit(solution)/shard_map/neg | solution.py:28
  46.3 2.4 %fusion.5 = f32[1,64,64]{2,1,0:T(8,128)S(1)} fusion(bf16[64,128,128]{2,1,0:T(8,128)(2,1)S(1)} %copy-done), kind=kOutput, calls=%fused_computation.8 | convolution fusion | flops 134217728 | bytes 2113536 | tf_op jit(solution)/shard_map/fn,gn->fg/dot_general | solution.py:383
  48.7 1.2 pad_maximum_fusion
  50.0 2.4 %fusion.8 = f32[1,64,64]{2,1,0:T(8,128)S(1)} fusion(bf16[64,128,128]{2,1,0:T(8,128)(2,1)S(1)} %copy-done, bf16[64,128,128]{2,1,0:T(8,128)(2,1)S(1)} %pad_maximum_fusion), kind=kOutput, calls=%fused_computation.9 | convolution fusion | flops 134217728 | bytes 4210688 | tf_op jit(solution)/shard_map/fn,gn->fg/dot_general | solution.py:384
  52.4 0.7 collective-permute-start
  53.1 0.9 collective-permute-done
  54.1 3.1 %collective-permute-done.1 = f32[2,64,64]{2,1,0:T(8,128)S(1)} collective-permute-done((f32[2,64,64]{2,1,0:T(8,128)S(1)}, f32[2,64,64]{2,1,0:T(8,128)S(1)}, u32[]{:S(2)}, u32[]{:S(2)}) %collective-permute-start.1) | collective-permute-done | bytes 32800 | tf_op jit(solution)/shard_map/ppermute | solution.py:361
  57.3 3.1 %collective-permute-done.2 = f32[2,64,64]{2,1,0:T(8,128)S(1)} collective-permute-done((f32[2,64,64]{2,1,0:T(8,128)S(1)}, f32[2,64,64]{2,1,0:T(8,128)S(1)}, u32[]{:S(2)}, u32[]{:S(2)}) %collective-permute-start.2) | collective-permute-done | bytes 32800 | tf_op jit(solution)/shard_map/ppermute | solution.py:361
  60.5 1.4 %copy.47 = bf16[8,8,128,128]{3,1,2,0:T(8,128)(2,1)S(1)} copy(bf16[8,8,128,128]{3,2,1,0:T(8,128)(2,1)S(1)} %bitcast.35) | data formatting | bytes 4194304
  61.9 2.6 %collective-permute-done.3 = f32[2,64,64]{2,1,0:T(8,128)S(1)} collective-permute-done((f32[2,64,64]{2,1,0:T(8,128)S(1)}, f32[2,64,64]{2,1,0:T(8,128)S(1)}, u32[]{:S(2)}, u32[]{:S(2)}) %collective-permute-start.3) | collective-permute-done | bytes 32800 | tf_op jit(solution)/shard_map/ppermute | solution.py:361
  64.6 5.5 %collective-permute-start.4 = (bf16[64,16384]{1,0:T(8,128)(2,1)S(1)}, bf16[64,16384]{1,0:T(8,128)(2,1)}, u32[]{:S(2)}, u32[]{:S(2)}) collective-permute-start(bf16[64,16384]{1,0:T(8,128)(2,1)S(1)} %bitcast.36), channel_id=1, source_target_pairs={{0,1},{1,2},{2,3},{3,4},{4,5},{5,6},{6,7},{7,8},{8,9},{9,10},{10,1... | collective-permute-start | bytes 6291464 | tf_op jit(solution)/shard_map/ppermute | solution.py:387
  70.1 2.1 %collective-permute-start.5 = (bf16[64,16384]{1,0:T(8,128)(2,1)S(1)}, bf16[64,16384]{1,0:T(8,128)(2,1)}, u32[]{:S(2)}, u32[]{:S(2)}) collective-permute-start(bf16[64,16384]{1,0:T(8,128)(2,1)S(1)} %bitcast.37), channel_id=1, source_target_pairs={{1,0},{2,1},{3,2},{4,3},{5,4},{6,5},{7,6},{8,7},{9,8},{10,9},{11,1... | collective-permute-start | bytes 6291464 | tf_op jit(solution)/shard_map/ppermute | solution.py:388
  73.1 0.6 maximum_bitcast_fusion.wz_ref
  73.7 0.6 select_reduce_fusion
  75.0 0.6 fusion.13.x0_ref
  75.6 0.7 select_add_fusion
  76.3 6.1 %shard_map.83 = f32[128,128]{1,0:T(8,128)} custom-call(f32[128,128]{1,0:T(8,128)} %get-tuple-element.15.a_ref, f32[128,128]{1,0:T(8,128)} %fusion.13.x0_ref, f32[128,128]{1,0:T(8,128)} %get-tuple-element.16.s_ref), custom_call_target="tpu_custom_call" | custom-call | tf_op jit(solution)/shard_map/pallas_call | solution.py:330
  82.4 0.9 copy.27
  83.4 0.6 maximum_bitcast_fusion.1.wl_ref
  84.1 5.6 %shard_map.84 = (f32[64,16384]{1,0:T(8,128)}, bf16[64,16384]{1,0:T(8,128)(2,1)}) custom-call(bf16[64,16384]{1,0:T(8,128)(2,1)} %bitcast.38, bf16[128,64]{1,0:T(8,128)(2,1)} %maximum_bitcast_fusion.1.wl_ref), custom_call_target="tpu_custom_call" | custom-call | flops 268435456 | bytes 8388608 | tf_op jit(solution)/shard_map/pallas_call | solution.py:276
  89.7 25.8 %collective-permute-done.4.xb_ref = bf16[64,16384]{1,0:T(8,128)(2,1)} collective-permute-done((bf16[64,16384]{1,0:T(8,128)(2,1)S(1)}, bf16[64,16384]{1,0:T(8,128)(2,1)}, u32[]{:S(2)}, u32[]{:S(2)}) %collective-permute-start.4) | collective-permute-done | bytes 2097184 | tf_op jit(solution)/shard_map/ppermute | solution.py:387
  115.5 3.0 %collective-permute-done.5.xa_ref = bf16[64,16384]{1,0:T(8,128)(2,1)} collective-permute-done((bf16[64,16384]{1,0:T(8,128)(2,1)S(1)}, bf16[64,16384]{1,0:T(8,128)(2,1)}, u32[]{:S(2)}, u32[]{:S(2)}) %collective-permute-start.5) | collective-permute-done | bytes 2097184 | tf_op jit(solution)/shard_map/ppermute | solution.py:388
  118.5 10.9 %shard_map.85 = bf16[64,128,128]{2,1,0:T(8,128)(2,1)} custom-call(f32[64,16384]{1,0:T(8,128)} %get-tuple-element.13.low_ref, bf16[64,16384]{1,0:T(8,128)(2,1)} %get-tuple-element.14.rem_ref, bf16[64,16384]{1,0:T(8,128)(2,1)} %collective-permute-done.4.xb_ref, bf16[64,16384]{1,0:T(8,128)(2,1)} %collective-permute-done.5.xa_ref, ...), custom_call_target="tpu_custom_call" | custom-call | flops 1342177280 | bytes 12582912 | tf_op jit(solution)/shard_map/pallas_call | solution.py:292
  (30 shorter events, 1.3 us)
Async XLA Ops:
  1.0 3.5 %copy-start.3 = (bf16[1,16,128,128]{3,2,1,0:T(8,128)(2,1)S(1)}, bf16[1,16,128,128]{3,2,1,0:T(8,128)(2,1)}, u32[]{:S(2)}) copy-start(bf16[1,16,128,128]{3,2,1,0:T(8,128)(2,1)} %param.10) | copy-start | bytes 1572868
  2.0 3.6 %copy-start.2 = (bf16[5,2,128,128]{3,2,1,0:T(8,128)(2,1)S(1)}, bf16[5,2,128,128]{3,2,1,0:T(8,128)(2,1)}, u32[]{:S(2)}) copy-start(bf16[5,2,128,128]{3,2,1,0:T(8,128)(2,1)} %param.13) | copy-start | bytes 983044
  2.0 5.1 %copy-start.5 = (s32[1,64]{1,0:T(1,128)S(1)}, s32[1,64]{1,0:T(1,128)}, u32[]{:S(2)}) copy-start(s32[1,64]{1,0:T(1,128)} %param.11) | copy-start | bytes 772
  43.1 3.2 %copy-start = (bf16[64,128,128]{2,1,0:T(8,128)(2,1)S(1)}, bf16[64,128,128]{2,1,0:T(8,128)(2,1)}, u32[]{:S(2)}) copy-start(bf16[64,128,128]{2,1,0:T(8,128)(2,1)} %shard_map.82) | copy-start | bytes 6291460
  52.4 1.6 %collective-permute-start = (f32[2,64,64]{2,1,0:T(8,128)S(1)}, f32[2,64,64]{2,1,0:T(8,128)S(1)}, u32[]{:S(2)}, u32[]{:S(2)}) collective-permute-start(f32[2,64,64]{2,1,0:T(8,128)S(1)} %pad_maximum_fusion.2), channel_id=1, source_target_pairs={{0,1},{1,0},{2,3},{3,2},{4,5},{5,4},{6,7},{7,6},{8,9},{9,8},{10,11... | collective-permute-start | bytes 98312 | tf_op jit(solution)/shard_map/ppermute | solution.py:361
  54.1 3.2 %collective-permute-start.1 = (f32[2,64,64]{2,1,0:T(8,128)S(1)}, f32[2,64,64]{2,1,0:T(8,128)S(1)}, u32[]{:S(2)}, u32[]{:S(2)}) collective-permute-start(f32[2,64,64]{2,1,0:T(8,128)S(1)} %fusion.14), channel_id=1, source_target_pairs={{0,2},{1,3},{2,0},{3,1},{4,6},{5,7},{6,4},{7,5},{8,10},{9,11},{10,... | collective-permute-start | bytes 98312 | tf_op jit(solution)/shard_map/ppermute | solution.py:361
  57.3 3.2 %collective-permute-start.2 = (f32[2,64,64]{2,1,0:T(8,128)S(1)}, f32[2,64,64]{2,1,0:T(8,128)S(1)}, u32[]{:S(2)}, u32[]{:S(2)}) collective-permute-start(f32[2,64,64]{2,1,0:T(8,128)S(1)} %fusion.17), channel_id=1, source_target_pairs={{0,4},{1,5},{2,6},{3,7},{4,0},{5,1},{6,2},{7,3},{8,12},{9,13},{10,... | collective-permute-start | bytes 98312 | tf_op jit(solution)/shard_map/ppermute | solution.py:361
  60.5 4.1 %collective-permute-start.3 = (f32[2,64,64]{2,1,0:T(8,128)S(1)}, f32[2,64,64]{2,1,0:T(8,128)S(1)}, u32[]{:S(2)}, u32[]{:S(2)}) collective-permute-start(f32[2,64,64]{2,1,0:T(8,128)S(1)} %add.20), channel_id=1, source_target_pairs={{0,8},{1,9},{2,10},{3,11},{4,12},{5,13},{6,14},{7,15},{8,0},{9,1},... | collective-permute-start | bytes 98312 | tf_op jit(solution)/shard_map/ppermute | solution.py:361
  60.5 12.3 %copy-start.4 = (bf16[3,2,64,64]{3,2,1,0:T(8,128)(2,1)S(1)}, bf16[3,2,64,64]{3,2,1,0:T(8,128)(2,1)}, u32[]{:S(2)}) copy-start(bf16[3,2,64,64]{3,2,1,0:T(8,128)(2,1)} %param.14) | copy-start | bytes 147460
  61.9 22.2 %copy-start.1 = (bf16[8,8,128,128]{3,1,2,0:T(8,128)(2,1)}, bf16[8,8,128,128]{3,1,2,0:T(8,128)(2,1)S(1)}, u32[]{:S(2)}) copy-start(bf16[8,8,128,128]{3,1,2,0:T(8,128)(2,1)S(1)} %copy.47) | copy-start | bytes 6291460
  64.6 50.9 %collective-permute-start.4 = (bf16[64,16384]{1,0:T(8,128)(2,1)S(1)}, bf16[64,16384]{1,0:T(8,128)(2,1)}, u32[]{:S(2)}, u32[]{:S(2)}) collective-permute-start(bf16[64,16384]{1,0:T(8,128)(2,1)S(1)} %bitcast.36), channel_id=1, source_target_pairs={{0,1},{1,2},{2,3},{3,4},{4,5},{5,6},{6,7},{7,8},{8,9},{9,10},{10,1... | collective-permute-start | bytes 6291464 | tf_op jit(solution)/shard_map/ppermute | solution.py:387
  70.1 48.4 %collective-permute-start.5 = (bf16[64,16384]{1,0:T(8,128)(2,1)S(1)}, bf16[64,16384]{1,0:T(8,128)(2,1)}, u32[]{:S(2)}, u32[]{:S(2)}) collective-permute-start(bf16[64,16384]{1,0:T(8,128)(2,1)S(1)} %bitcast.37), channel_id=1, source_target_pairs={{1,0},{2,1},{3,2},{4,3},{5,4},{6,5},{7,6},{8,7},{9,8},{10,9},{11,1... | collective-permute-start | bytes 6291464 | tf_op jit(solution)/shard_map/ppermute | solution.py:388

commit v12 on v11

--- a/solution.py
+++ b/solution.py
@@ -90,7 +90,7 @@
 
 
 def gradient_kernel(idx_ref, cnt_ref, nsl_ref, img_ref, adj_ref, maps_ref,
-                    bf_ref, bt_ref, btr_ref, out_ref, x_scr, rx_scr, g_scr, g2_scr,
+                    bf_ref, out_ref, x_scr, rx_scr, g_scr, g2_scr,
                     lhs_a, y_a, ry_a, lhs_b, y_b, ry_b, mrr_ref, mii_ref, *, fb, slots, links,
                     coils):
     b = pl.program_id(0)
@@ -134,8 +134,14 @@
             lax.fori_loop(0, fb, gather_t, 0, unroll=True)
             samples = jnp.dot(lhs_scr[...], bf_ref[q], preferred_element_type=jnp.float32)
             samples = samples.astype(jnp.bfloat16)
-            y_scr[...] = jnp.dot(samples, bt_ref[q], preferred_element_type=jnp.float32)
-            ry_scr[...] = jnp.dot(samples, btr_ref[q], preferred_element_type=jnp.float32)
+            pairs = (((1,), (1,)), ((), ()))
+            for j in range(2):
+                block = bf_ref[q, pl.ds(j * 128, 128), :]
+                turned = jnp.concatenate([-block[64:], block[:64]], axis=0)
+                y_scr[:, pl.ds(j * 128, 128)] = lax.dot_general(
+                    samples, block, pairs, preferred_element_type=jnp.float32)
+                ry_scr[:, pl.ds(j * 128, 128)] = lax.dot_general(
+                    samples, turned, pairs, preferred_element_type=jnp.float32)
 
             def scatter_t(t, c):
                 frame = b * fb + t
@@ -171,9 +177,6 @@
     half = lane_width // 2
     maps_t = jnp.swapaxes(plane_maps, 0, 1)
     bf = blocks.reshape(reads, links * lane_width, lane_width)
-    bt4 = jnp.transpose(blocks, (0, 3, 1, 2))
-    bt = bt4.reshape(reads, lane_width, links * lane_width)
-    btr = rotate(bt4).reshape(reads, lane_width, links * lane_width)
     idx = plane_map.reshape(-1).astype(jnp.int32)
     cnt = counts.astype(jnp.int32)
     nsl = jnp.minimum(jnp.max(cnt.reshape(nblocks, fb), axis=1), slots).astype(jnp.int32)
@@ -194,8 +197,6 @@
                 plane_spec,
                 whole3(maps_t.shape),
                 whole3(bf.shape),
-                whole3(bt.shape),
-                whole3(btr.shape),
             ],
             out_specs=plane_spec,
             scratch_shapes=[
@@ -217,7 +218,7 @@
         cost_estimate=pl.CostEstimate(
             flops=flops, transcendentals=0, bytes_accessed=image_plane.size * 6 + maps_t.size * 2
         ),
-    )(idx, cnt, nsl, image_plane, adjoint_plane, maps_t, bf, bt, btr)
+    )(idx, cnt, nsl, image_plane, adjoint_plane, maps_t, bf)
 
 
 def lane_tools(frames, width):

time: 130 us -> 129 us (level)
  Pallas kernels: 57.2 us -> 59.3 us
  local copies, waits for them, and re-layouts: 8.66 us -> 6.83 us
    pallas_call x1, Pallas kernels: 34.6 us -> 36.7 us  [fresh_image_of(): pl.pallas_call(kernel, out_shape=jax.ShapeDtypeStruct(image_plane.shape,...]
    reshape x2 -> x0, local copies, waits for them, and re-layouts: 1.85 us -> none  [the longest x1 0.93 us: fresh_image_of(): bt = bt4.reshape(reads, lane_width, links * lane_width)]
    neg x2 -> x1, other arithmetic: 4.27 us -> 3.24 us  [rotate(): -field_values[..., half_width:]]
    unnamed x16 -> x14, local copies, waits for them, and re-layouts: 4.58 us -> 4.6 us
  transfers between devices with their start and end apart: 6 -> 6, of which waited for: 6 -> 6; matrix products, arithmetic and copies ran while one was open for 4% -> 5% of each run, Pallas kernels for 9% -> 9%
where the time goes in v12:
time: 129 us
  Pallas kernels  59.3 us (46%)
  waiting for transfers between devices  38.4 us (30%)
  other arithmetic  9.17 us (7%)
  starting transfers between devices  8.64 us (7%)
  local copies, waits for them, and re-layouts  6.83 us (5%)
  matrix products  4.84 us (4%)
  between operations  1.58 us (1%)
    pallas_call x1, Pallas kernels, fresh_image_of(): pl.pallas_call(kernel, out_shape=jax.ShapeDtypeStruct(image_plane.shape,...  36.7 us
    ppermute x1, waiting for transfers between devices, local(): fresh_before = lax.ppermute(flat, 'dom', forward)  25.7 us
    pallas_call x1, Pallas kernels, post_of(): pl.pallas_call(functools.partial(post_kernel, cut=SOFT_CUT), out_shape=ja...  11 us
    ppermute x4, waiting for transfers between devices, tree_sum(): value = value + lax.ppermute(value, axis, pairs)  9.71 us
    pallas_call x1, Pallas kernels, shrink_of(): pl.pallas_call(functools.partial(solve_kernel, steps=10), out_shape=jax.S...  6.07 us
    pallas_call x1, Pallas kernels, post_of(): pl.pallas_call(own_kernel, out_shape=(jax.ShapeDtypeStruct(plane.shape, j...  5.55 us
    ppermute x1, starting transfers between devices, local(): fresh_before = lax.ppermute(flat, 'dom', forward)  5.49 us
    unnamed x14, local copies, waits for them, and re-layouts  4.6 us
  transfers between devices with their start and end apart: 6, of which 6 were waited for; matrix products, arithmetic and copies ran while one was open for 5% of the time, Pallas kernels for 9%

profile of v12, /device:TPU:19, one launch (start us, length us, event | category | flops | bytes accessed | tf_op | source)
XLA Modules:
  0.0 128.8 jit_solution(7463364245700827152)
XLA Ops:
  0.0 1.6 %copy.17 = s32[1,64,6,5,2]{4,3,2,1,0:T(8,128)S(1)} copy(s32[1,64,6,5,2]{1,4,3,2,0:T(2,128)} %param.12) | data formatting | bytes 30720 | tf_op args[4]
  1.6 0.9 reshape_squeeze.6.idx_ref
  2.5 1.1 copy.42
  3.6 0.5 broadcast.15
  4.2 0.7 reduce.3
  4.9 0.1 reduce_max.9
  5.0 0.5 broadcast_minimum_fusion.nsl_ref
  5.6 36.7 %shard_map.82 = bf16[64,128,128]{2,1,0:T(8,128)(2,1)} custom-call(s32[3840]{0:T(1024)} %reshape_squeeze.6.idx_ref, s32[64]{0:T(128)} %bitcast.41, s32[2]{0:T(128)} %broadcast_minimum_fusion.nsl_ref, bf16[64,128,128]{2,1,0:T(8,128)(2,1)} %bitcast.38, bf16[64,128,128]{2,1,0:T(8,128)(2,1)} %bitcast.39, bf16[128,16,128]{2,1,0:T(8,128)(2,1)} %bitcast.35, ...), custom_call_target="tpu_custom_call" | custom-call | flops 6039797760 | bytes 6815744 | tf_op jit(solution)/shard_map/pallas_call | solution.py:189
  42.3 3.2 %slice_negate_fusion = (bf16[64,128,64]{2,1,0:T(8,128)(2,1)S(1)}, bf16[64,128,64]{2,1,0:T(8,128)(2,1)S(1)}) fusion(bf16[64,128,128]{2,1,0:T(8,128)(2,1)} %shard_map.82), kind=kLoop, calls=%fused_computation.1 | loop fusion | flops 524288 | bytes 4194304 | tf_op jit(solution)/shard_map/neg | solution.py:28
  45.6 2.4 %fusion.5 = f32[1,64,64]{2,1,0:T(8,128)S(1)} fusion(bf16[64,128,128]{2,1,0:T(8,128)(2,1)S(1)} %copy-done), kind=kOutput, calls=%fused_computation.8 | convolution fusion | flops 134217728 | bytes 2113536 | tf_op jit(solution)/shard_map/fn,gn->fg/dot_general | solution.py:384
  48.0 1.2 pad_maximum_fusion
  49.2 2.4 %fusion.8 = f32[1,64,64]{2,1,0:T(8,128)S(1)} fusion(bf16[64,128,128]{2,1,0:T(8,128)(2,1)S(1)} %copy-done, bf16[64,128,128]{2,1,0:T(8,128)(2,1)S(1)} %pad_maximum_fusion), kind=kOutput, calls=%fused_computation.9 | convolution fusion | flops 134217728 | bytes 4210688 | tf_op jit(solution)/shard_map/fn,gn->fg/dot_general | solution.py:385
  51.6 0.8 collective-permute-start
  52.4 0.9 collective-permute-done
  53.4 3.1 %collective-permute-done.1 = f32[2,64,64]{2,1,0:T(8,128)S(1)} collective-permute-done((f32[2,64,64]{2,1,0:T(8,128)S(1)}, f32[2,64,64]{2,1,0:T(8,128)S(1)}, u32[]{:S(2)}, u32[]{:S(2)}) %collective-permute-start.1) | collective-permute-done | bytes 32800 | tf_op jit(solution)/shard_map/ppermute | solution.py:362
  56.6 3.1 %collective-permute-done.2 = f32[2,64,64]{2,1,0:T(8,128)S(1)} collective-permute-done((f32[2,64,64]{2,1,0:T(8,128)S(1)}, f32[2,64,64]{2,1,0:T(8,128)S(1)}, u32[]{:S(2)}, u32[]{:S(2)}) %collective-permute-start.2) | collective-permute-done | bytes 32800 | tf_op jit(solution)/shard_map/ppermute | solution.py:362
  59.8 1.4 %copy.41 = bf16[8,8,128,128]{3,1,2,0:T(8,128)(2,1)S(1)} copy(bf16[8,8,128,128]{3,2,1,0:T(8,128)(2,1)S(1)} %bitcast.31) | data formatting | bytes 4194304
  61.2 2.6 %collective-permute-done.3 = f32[2,64,64]{2,1,0:T(8,128)S(1)} collective-permute-done((f32[2,64,64]{2,1,0:T(8,128)S(1)}, f32[2,64,64]{2,1,0:T(8,128)S(1)}, u32[]{:S(2)}, u32[]{:S(2)}) %collective-permute-start.3) | collective-permute-done | bytes 32800 | tf_op jit(solution)/shard_map/ppermute | solution.py:362
  63.9 5.5 %collective-permute-start.4 = (bf16[64,16384]{1,0:T(8,128)(2,1)S(1)}, bf16[64,16384]{1,0:T(8,128)(2,1)}, u32[]{:S(2)}, u32[]{:S(2)}) collective-permute-start(bf16[64,16384]{1,0:T(8,128)(2,1)S(1)} %bitcast.32), channel_id=1, source_target_pairs={{0,1},{1,2},{2,3},{3,4},{4,5},{5,6},{6,7},{7,8},{8,9},{9,10},{10,1... | collective-permute-start | bytes 6291464 | tf_op jit(solution)/shard_map/ppermute | solution.py:388
  69.4 2.1 %collective-permute-start.5 = (bf16[64,16384]{1,0:T(8,128)(2,1)S(1)}, bf16[64,16384]{1,0:T(8,128)(2,1)}, u32[]{:S(2)}, u32[]{:S(2)}) collective-permute-start(bf16[64,16384]{1,0:T(8,128)(2,1)S(1)} %bitcast.33), channel_id=1, source_target_pairs={{1,0},{2,1},{3,2},{4,3},{5,4},{6,5},{7,6},{8,7},{9,8},{10,9},{11,1... | collective-permute-start | bytes 6291464 | tf_op jit(solution)/shard_map/ppermute | solution.py:389
  72.2 0.1 copy.24
  72.4 0.6 maximum_bitcast_fusion.wz_ref
  73.0 0.7 select_reduce_fusion
  74.4 0.6 fusion.13.x0_ref
  75.1 0.8 select_add_fusion
  75.8 6.1 %shard_map.83 = f32[128,128]{1,0:T(8,128)} custom-call(f32[128,128]{1,0:T(8,128)} %get-tuple-element.15.a_ref, f32[128,128]{1,0:T(8,128)} %fusion.13.x0_ref, f32[128,128]{1,0:T(8,128)} %get-tuple-element.16.s_ref), custom_call_target="tpu_custom_call" | custom-call | tf_op jit(solution)/shard_map/pallas_call | solution.py:331
  81.9 0.9 copy.23
  82.9 0.6 maximum_bitcast_fusion.1.wl_ref
  83.6 5.6 %shard_map.84 = (f32[64,16384]{1,0:T(8,128)}, bf16[64,16384]{1,0:T(8,128)(2,1)}) custom-call(bf16[64,16384]{1,0:T(8,128)(2,1)} %bitcast.34, bf16[128,64]{1,0:T(8,128)(2,1)} %maximum_bitcast_fusion.1.wl_ref), custom_call_target="tpu_custom_call" | custom-call | flops 268435456 | bytes 8388608 | tf_op jit(solution)/shard_map/pallas_call | solution.py:277
  89.1 25.7 %collective-permute-done.4.xb_ref = bf16[64,16384]{1,0:T(8,128)(2,1)} collective-permute-done((bf16[64,16384]{1,0:T(8,128)(2,1)S(1)}, bf16[64,16384]{1,0:T(8,128)(2,1)}, u32[]{:S(2)}, u32[]{:S(2)}) %collective-permute-start.4) | collective-permute-done | bytes 2097184 | tf_op jit(solution)/shard_map/ppermute | solution.py:388
  114.8 3.0 %collective-permute-done.5.xa_ref = bf16[64,16384]{1,0:T(8,128)(2,1)} collective-permute-done((bf16[64,16384]{1,0:T(8,128)(2,1)S(1)}, bf16[64,16384]{1,0:T(8,128)(2,1)}, u32[]{:S(2)}, u32[]{:S(2)}) %collective-permute-start.5) | collective-permute-done | bytes 2097184 | tf_op jit(solution)/shard_map/ppermute | solution.py:389
  117.8 11.0 %shard_map.85 = bf16[64,128,128]{2,1,0:T(8,128)(2,1)} custom-call(f32[64,16384]{1,0:T(8,128)} %get-tuple-element.13.low_ref, bf16[64,16384]{1,0:T(8,128)(2,1)} %get-tuple-element.14.rem_ref, bf16[64,16384]{1,0:T(8,128)(2,1)} %collective-permute-done.4.xb_ref, bf16[64,16384]{1,0:T(8,128)(2,1)} %collective-permute-done.5.xa_ref, ...), custom_call_target="tpu_custom_call" | custom-call | flops 1342177280 | bytes 12582912 | tf_op jit(solution)/shard_map/pallas_call | solution.py:293
  (24 shorter events, 0.6 us)
Async XLA Ops:
  0.0 2.5 %copy-start.2 = (bf16[1,16,128,128]{3,2,1,0:T(8,128)(2,1)S(1)}, bf16[1,16,128,128]{3,2,1,0:T(8,128)(2,1)}, u32[]{:S(2)}) copy-start(bf16[1,16,128,128]{3,2,1,0:T(8,128)(2,1)} %param.10) | copy-start | bytes 1572868
  0.0 4.2 %copy-start.4 = (s32[1,64]{1,0:T(1,128)S(1)}, s32[1,64]{1,0:T(1,128)}, u32[]{:S(2)}) copy-start(s32[1,64]{1,0:T(1,128)} %param.11) | copy-start | bytes 772
  42.3 3.2 %copy-start = (bf16[64,128,128]{2,1,0:T(8,128)(2,1)S(1)}, bf16[64,128,128]{2,1,0:T(8,128)(2,1)}, u32[]{:S(2)}) copy-start(bf16[64,128,128]{2,1,0:T(8,128)(2,1)} %shard_map.82) | copy-start | bytes 6291460
  51.6 1.7 %collective-permute-start = (f32[2,64,64]{2,1,0:T(8,128)S(1)}, f32[2,64,64]{2,1,0:T(8,128)S(1)}, u32[]{:S(2)}, u32[]{:S(2)}) collective-permute-start(f32[2,64,64]{2,1,0:T(8,128)S(1)} %pad_maximum_fusion.1), channel_id=1, source_target_pairs={{0,1},{1,0},{2,3},{3,2},{4,5},{5,4},{6,7},{7,6},{8,9},{9,8},{10,11... | collective-permute-start | bytes 98312 | tf_op jit(solution)/shard_map/ppermute | solution.py:362
  53.4 3.2 %collective-permute-start.1 = (f32[2,64,64]{2,1,0:T(8,128)S(1)}, f32[2,64,64]{2,1,0:T(8,128)S(1)}, u32[]{:S(2)}, u32[]{:S(2)}) collective-permute-start(f32[2,64,64]{2,1,0:T(8,128)S(1)} %fusion.14), channel_id=1, source_target_pairs={{0,2},{1,3},{2,0},{3,1},{4,6},{5,7},{6,4},{7,5},{8,10},{9,11},{10,... | collective-permute-start | bytes 98312 | tf_op jit(solution)/shard_map/ppermute | solution.py:362
  56.6 3.2 %collective-permute-start.2 = (f32[2,64,64]{2,1,0:T(8,128)S(1)}, f32[2,64,64]{2,1,0:T(8,128)S(1)}, u32[]{:S(2)}, u32[]{:S(2)}) collective-permute-start(f32[2,64,64]{2,1,0:T(8,128)S(1)} %fusion.17), channel_id=1, source_target_pairs={{0,4},{1,5},{2,6},{3,7},{4,0},{5,1},{6,2},{7,3},{8,12},{9,13},{10,... | collective-permute-start | bytes 98312 | tf_op jit(solution)/shard_map/ppermute | solution.py:362
  59.8 4.1 %collective-permute-start.3 = (f32[2,64,64]{2,1,0:T(8,128)S(1)}, f32[2,64,64]{2,1,0:T(8,128)S(1)}, u32[]{:S(2)}, u32[]{:S(2)}) collective-permute-start(f32[2,64,64]{2,1,0:T(8,128)S(1)} %add.20), channel_id=1, source_target_pairs={{0,8},{1,9},{2,10},{3,11},{4,12},{5,13},{6,14},{7,15},{8,0},{9,1},... | collective-permute-start | bytes 98312 | tf_op jit(solution)/shard_map/ppermute | solution.py:362
  59.8 12.3 %copy-start.3 = (bf16[3,2,64,64]{3,2,1,0:T(8,128)(2,1)S(1)}, bf16[3,2,64,64]{3,2,1,0:T(8,128)(2,1)}, u32[]{:S(2)}) copy-start(bf16[3,2,64,64]{3,2,1,0:T(8,128)(2,1)} %param.14) | copy-start | bytes 147460
  61.2 22.3 %copy-start.1 = (bf16[8,8,128,128]{3,1,2,0:T(8,128)(2,1)}, bf16[8,8,128,128]{3,1,2,0:T(8,128)(2,1)S(1)}, u32[]{:S(2)}) copy-start(bf16[8,8,128,128]{3,1,2,0:T(8,128)(2,1)S(1)} %copy.41) | copy-start | bytes 6291460
  63.9 50.9 %collective-permute-start.4 = (bf16[64,16384]{1,0:T(8,128)(2,1)S(1)}, bf16[64,16384]{1,0:T(8,128)(2,1)}, u32[]{:S(2)}, u32[]{:S(2)}) collective-permute-start(bf16[64,16384]{1,0:T(8,128)(2,1)S(1)} %bitcast.32), channel_id=1, source_target_pairs={{0,1},{1,2},{2,3},{3,4},{4,5},{5,6},{6,7},{7,8},{8,9},{9,10},{10,1... | collective-permute-start | bytes 6291464 | tf_op jit(solution)/shard_map/ppermute | solution.py:388
  69.4 48.4 %collective-permute-start.5 = (bf16[64,16384]{1,0:T(8,128)(2,1)S(1)}, bf16[64,16384]{1,0:T(8,128)(2,1)}, u32[]{:S(2)}, u32[]{:S(2)}) collective-permute-start(bf16[64,16384]{1,0:T(8,128)(2,1)S(1)} %bitcast.33), channel_id=1, source_target_pairs={{1,0},{2,1},{3,2},{4,3},{5,4},{6,5},{7,6},{8,7},{9,8},{10,9},{11,1... | collective-permute-start | bytes 6291464 | tf_op jit(solution)/shard_map/ppermute | solution.py:389

commit v13 on v12

--- a/solution.py
+++ b/solution.py
@@ -172,7 +172,7 @@
     frame_count, tile_count, lane_width = image_plane.shape
     slots, reads, links = plane_map.shape[1], plane_map.shape[2], plane_map.shape[3]
     coils = plane_maps.shape[0]
-    fb = 32 if frame_count % 32 == 0 else frame_count
+    fb = 64 if frame_count % 64 == 0 else frame_count
     nblocks = frame_count // fb
     half = lane_width // 2
     maps_t = jnp.swapaxes(plane_maps, 0, 1)
@@ -329,7 +329,7 @@
     start = unit_matrix * (2.0 / (threshold_sq * (2.0 + rank_value)))
     whole = pl.BlockSpec(memory_space=pltpu.VMEM)
     return pl.pallas_call(
-        functools.partial(solve_kernel, steps=10),
+        functools.partial(solve_kernel, steps=9),
         out_shape=jax.ShapeDtypeStruct((size, size), jnp.float32),
         in_specs=[whole, whole, whole],
         out_specs=whole,

time: 129 us -> 127 us (0.984)
  Pallas kernels: 59.3 us -> 57.2 us
    pallas_call x1, Pallas kernels: 36.7 us -> 35 us  [fresh_image_of(): pl.pallas_call(kernel, out_shape=jax.ShapeDtypeStruct(image_plane.shape,...]
    unnamed x14 -> x13, local copies, waits for them, and re-layouts: 4.6 us -> 4.07 us
where the time goes in v13:
time: 127 us; the launch traced here: 126 us
  Pallas kernels  57.2 us (45%)
  waiting for transfers between devices  38.6 us (30%)
  starting transfers between devices  8.82 us (7%)
  other arithmetic  8.44 us (7%)
  local copies, waits for them, and re-layouts  6.21 us (5%)
  matrix products  4.84 us (4%)
  between operations  2.24 us (2%)
    pallas_call x1, Pallas kernels, fresh_image_of(): pl.pallas_call(kernel, out_shape=jax.ShapeDtypeStruct(image_plane.shape,...  35 us
    ppermute x1, waiting for transfers between devices, local(): fresh_before = lax.ppermute(flat, 'dom', forward)  25.9 us
    pallas_call x1, Pallas kernels, post_of(): pl.pallas_call(functools.partial(post_kernel, cut=SOFT_CUT), out_shape=ja...  10.9 us
    ppermute x4, waiting for transfers between devices, tree_sum(): value = value + lax.ppermute(value, axis, pairs)  9.71 us
    pallas_call x1, Pallas kernels, shrink_of(): pl.pallas_call(functools.partial(solve_kernel, steps=9), out_shape=jax.Sh...  5.64 us
    pallas_call x1, Pallas kernels, post_of(): pl.pallas_call(own_kernel, out_shape=(jax.ShapeDtypeStruct(plane.shape, j...  5.57 us
    ppermute x1, starting transfers between devices, local(): fresh_before = lax.ppermute(flat, 'dom', forward)  5.49 us
    unnamed x13, local copies, waits for them, and re-layouts  4.07 us
  transfers between devices with their start and end apart: 6, of which 6 were waited for; matrix products, arithmetic and copies ran while one was open for 5% of the time, Pallas kernels for 9%

profile of v13, /device:TPU:19, one launch (start us, length us, event | category | flops | bytes accessed | tf_op | source)
XLA Modules:
  0.0 126.4 jit_solution(10240693048343654258)
XLA Ops:
  0.0 1.6 %copy.17 = s32[1,64,6,5,2]{4,3,2,1,0:T(8,128)S(1)} copy(s32[1,64,6,5,2]{1,4,3,2,0:T(2,128)} %param.12) | data formatting | bytes 30720 | tf_op args[4]
  1.6 0.9 reshape_squeeze.3.idx_ref
  2.5 1.1 copy.42
  3.6 0.6 reduce_max.9
  4.9 35.0 %shard_map.82 = bf16[64,128,128]{2,1,0:T(8,128)(2,1)} custom-call(s32[3840]{0:T(1024)} %reshape_squeeze.3.idx_ref, s32[64]{0:T(128)} %bitcast.42, s32[1]{0:T(128)} %bitcast.1.nsl_ref, bf16[64,128,128]{2,1,0:T(8,128)(2,1)} %bitcast.39, bf16[64,128,128]{2,1,0:T(8,128)(2,1)} %bitcast.40, bf16[128,16,128]{2,1,0:T(8,128)(2,1)} %bitcast.36, ...), custom_call_target="tpu_custom_call" | custom-call | flops 6039797760 | bytes 6815744 | tf_op jit(solution)/shard_map/pallas_call | solution.py:189
  40.0 3.2 %slice_negate_fusion = (bf16[64,128,64]{2,1,0:T(8,128)(2,1)S(1)}, bf16[64,128,64]{2,1,0:T(8,128)(2,1)S(1)}) fusion(bf16[64,128,128]{2,1,0:T(8,128)(2,1)} %shard_map.82), kind=kLoop, calls=%fused_computation.1 | loop fusion | flops 524288 | bytes 4194304 | tf_op jit(solution)/shard_map/neg | solution.py:28
  43.2 2.4 %fusion.5 = f32[1,64,64]{2,1,0:T(8,128)S(1)} fusion(bf16[64,128,128]{2,1,0:T(8,128)(2,1)S(1)} %copy-done), kind=kOutput, calls=%fused_computation.8 | convolution fusion | flops 134217728 | bytes 2113536 | tf_op jit(solution)/shard_map/fn,gn->fg/dot_general | solution.py:384
  45.6 1.2 pad_maximum_fusion
  46.9 2.4 %fusion.8 = f32[1,64,64]{2,1,0:T(8,128)S(1)} fusion(bf16[64,128,128]{2,1,0:T(8,128)(2,1)S(1)} %copy-done, bf16[64,128,128]{2,1,0:T(8,128)(2,1)S(1)} %pad_maximum_fusion), kind=kOutput, calls=%fused_computation.9 | convolution fusion | flops 134217728 | bytes 4210688 | tf_op jit(solution)/shard_map/fn,gn->fg/dot_general | solution.py:385
  49.3 0.8 collective-permute-start
  50.1 0.9 collective-permute-done
  51.0 0.1 collective-permute-start.1
  51.1 3.1 %collective-permute-done.1 = f32[2,64,64]{2,1,0:T(8,128)S(1)} collective-permute-done((f32[2,64,64]{2,1,0:T(8,128)S(1)}, f32[2,64,64]{2,1,0:T(8,128)S(1)}, u32[]{:S(2)}, u32[]{:S(2)}) %collective-permute-start.1) | collective-permute-done | bytes 32800 | tf_op jit(solution)/shard_map/ppermute | solution.py:362
  54.3 3.1 %collective-permute-done.2 = f32[2,64,64]{2,1,0:T(8,128)S(1)} collective-permute-done((f32[2,64,64]{2,1,0:T(8,128)S(1)}, f32[2,64,64]{2,1,0:T(8,128)S(1)}, u32[]{:S(2)}, u32[]{:S(2)}) %collective-permute-start.2) | collective-permute-done | bytes 32800 | tf_op jit(solution)/shard_map/ppermute | solution.py:362
  57.5 1.4 %copy.41 = bf16[8,8,128,128]{3,1,2,0:T(8,128)(2,1)S(1)} copy(bf16[8,8,128,128]{3,2,1,0:T(8,128)(2,1)S(1)} %bitcast.32) | data formatting | bytes 4194304
  58.9 2.6 %collective-permute-done.3 = f32[2,64,64]{2,1,0:T(8,128)S(1)} collective-permute-done((f32[2,64,64]{2,1,0:T(8,128)S(1)}, f32[2,64,64]{2,1,0:T(8,128)S(1)}, u32[]{:S(2)}, u32[]{:S(2)}) %collective-permute-start.3) | collective-permute-done | bytes 32800 | tf_op jit(solution)/shard_map/ppermute | solution.py:362
  61.5 5.5 %collective-permute-start.4 = (bf16[64,16384]{1,0:T(8,128)(2,1)S(1)}, bf16[64,16384]{1,0:T(8,128)(2,1)}, u32[]{:S(2)}, u32[]{:S(2)}) collective-permute-start(bf16[64,16384]{1,0:T(8,128)(2,1)S(1)} %bitcast.33), channel_id=1, source_target_pairs={{0,1},{1,2},{2,3},{3,4},{4,5},{5,6},{6,7},{7,8},{8,9},{9,10},{10,1... | collective-permute-start | bytes 6291464 | tf_op jit(solution)/shard_map/ppermute | solution.py:388
  67.0 2.4 %collective-permute-start.5 = (bf16[64,16384]{1,0:T(8,128)(2,1)S(1)}, bf16[64,16384]{1,0:T(8,128)(2,1)}, u32[]{:S(2)}, u32[]{:S(2)}) collective-permute-start(bf16[64,16384]{1,0:T(8,128)(2,1)S(1)} %bitcast.34), channel_id=1, source_target_pairs={{1,0},{2,1},{3,2},{4,3},{5,4},{6,5},{7,6},{8,7},{9,8},{10,9},{11,1... | collective-permute-start | bytes 6291464 | tf_op jit(solution)/shard_map/ppermute | solution.py:389
  70.0 0.1 copy.24
  70.1 0.1 copy.25
  70.2 0.6 maximum_bitcast_fusion.wz_ref
  70.9 0.7 select_reduce_fusion
  72.3 0.6 fusion.13.x0_ref
  72.9 0.7 select_add_fusion
  73.7 5.6 %shard_map.83 = f32[128,128]{1,0:T(8,128)} custom-call(f32[128,128]{1,0:T(8,128)} %get-tuple-element.15.a_ref, f32[128,128]{1,0:T(8,128)} %fusion.13.x0_ref, f32[128,128]{1,0:T(8,128)} %get-tuple-element.16.s_ref), custom_call_target="tpu_custom_call" | custom-call | tf_op jit(solution)/shard_map/pallas_call | solution.py:331
  79.3 0.9 copy.23
  80.2 0.1 fusion.16
  80.3 0.6 maximum_bitcast_fusion.1.wl_ref
  80.9 5.6 %shard_map.84 = (f32[64,16384]{1,0:T(8,128)}, bf16[64,16384]{1,0:T(8,128)(2,1)}) custom-call(bf16[64,16384]{1,0:T(8,128)(2,1)} %bitcast.35, bf16[128,64]{1,0:T(8,128)(2,1)} %maximum_bitcast_fusion.1.wl_ref), custom_call_target="tpu_custom_call" | custom-call | flops 268435456 | bytes 8388608 | tf_op jit(solution)/shard_map/pallas_call | solution.py:277
  86.5 25.9 %collective-permute-done.4.xb_ref = bf16[64,16384]{1,0:T(8,128)(2,1)} collective-permute-done((bf16[64,16384]{1,0:T(8,128)(2,1)S(1)}, bf16[64,16384]{1,0:T(8,128)(2,1)}, u32[]{:S(2)}, u32[]{:S(2)}) %collective-permute-start.4) | collective-permute-done | bytes 2097184 | tf_op jit(solution)/shard_map/ppermute | solution.py:388
  112.4 3.0 %collective-permute-done.5.xa_ref = bf16[64,16384]{1,0:T(8,128)(2,1)} collective-permute-done((bf16[64,16384]{1,0:T(8,128)(2,1)S(1)}, bf16[64,16384]{1,0:T(8,128)(2,1)}, u32[]{:S(2)}, u32[]{:S(2)}) %collective-permute-start.5) | collective-permute-done | bytes 2097184 | tf_op jit(solution)/shard_map/ppermute | solution.py:389
  115.4 10.9 %shard_map.85 = bf16[64,128,128]{2,1,0:T(8,128)(2,1)} custom-call(f32[64,16384]{1,0:T(8,128)} %get-tuple-element.13.low_ref, bf16[64,16384]{1,0:T(8,128)(2,1)} %get-tuple-element.14.rem_ref, bf16[64,16384]{1,0:T(8,128)(2,1)} %collective-permute-done.4.xb_ref, bf16[64,16384]{1,0:T(8,128)(2,1)} %collective-permute-done.5.xa_ref, ...), custom_call_target="tpu_custom_call" | custom-call | flops 1342177280 | bytes 12582912 | tf_op jit(solution)/shard_map/pallas_call | solution.py:293
  (20 shorter events, 0.2 us)
Async XLA Ops:
  0.0 2.5 %copy-start.2 = (bf16[1,16,128,128]{3,2,1,0:T(8,128)(2,1)S(1)}, bf16[1,16,128,128]{3,2,1,0:T(8,128)(2,1)}, u32[]{:S(2)}) copy-start(bf16[1,16,128,128]{3,2,1,0:T(8,128)(2,1)} %param.10) | copy-start | bytes 1572868
  0.0 3.6 %copy-start.4 = (s32[1,64]{1,0:T(1,128)S(1)}, s32[1,64]{1,0:T(1,128)}, u32[]{:S(2)}) copy-start(s32[1,64]{1,0:T(1,128)} %param.11) | copy-start | bytes 772
  40.0 3.2 %copy-start = (bf16[64,128,128]{2,1,0:T(8,128)(2,1)S(1)}, bf16[64,128,128]{2,1,0:T(8,128)(2,1)}, u32[]{:S(2)}) copy-start(bf16[64,128,128]{2,1,0:T(8,128)(2,1)} %shard_map.82) | copy-start | bytes 6291460
  49.3 1.7 %collective-permute-start = (f32[2,64,64]{2,1,0:T(8,128)S(1)}, f32[2,64,64]{2,1,0:T(8,128)S(1)}, u32[]{:S(2)}, u32[]{:S(2)}) collective-permute-start(f32[2,64,64]{2,1,0:T(8,128)S(1)} %pad_maximum_fusion.1), channel_id=1, source_target_pairs={{0,1},{1,0},{2,3},{3,2},{4,5},{5,4},{6,7},{7,6},{8,9},{9,8},{10,11... | collective-permute-start | bytes 98312 | tf_op jit(solution)/shard_map/ppermute | solution.py:362
  51.0 3.2 %collective-permute-start.1 = (f32[2,64,64]{2,1,0:T(8,128)S(1)}, f32[2,64,64]{2,1,0:T(8,128)S(1)}, u32[]{:S(2)}, u32[]{:S(2)}) collective-permute-start(f32[2,64,64]{2,1,0:T(8,128)S(1)} %fusion.14), channel_id=1, source_target_pairs={{0,2},{1,3},{2,0},{3,1},{4,6},{5,7},{6,4},{7,5},{8,10},{9,11},{10,... | collective-permute-start | bytes 98312 | tf_op jit(solution)/shard_map/ppermute | solution.py:362
  54.2 3.2 %collective-permute-start.2 = (f32[2,64,64]{2,1,0:T(8,128)S(1)}, f32[2,64,64]{2,1,0:T(8,128)S(1)}, u32[]{:S(2)}, u32[]{:S(2)}) collective-permute-start(f32[2,64,64]{2,1,0:T(8,128)S(1)} %fusion.17), channel_id=1, source_target_pairs={{0,4},{1,5},{2,6},{3,7},{4,0},{5,1},{6,2},{7,3},{8,12},{9,13},{10,... | collective-permute-start | bytes 98312 | tf_op jit(solution)/shard_map/ppermute | solution.py:362
  57.4 4.1 %collective-permute-start.3 = (f32[2,64,64]{2,1,0:T(8,128)S(1)}, f32[2,64,64]{2,1,0:T(8,128)S(1)}, u32[]{:S(2)}, u32[]{:S(2)}) collective-permute-start(f32[2,64,64]{2,1,0:T(8,128)S(1)} %add.20), channel_id=1, source_target_pairs={{0,8},{1,9},{2,10},{3,11},{4,12},{5,13},{6,14},{7,15},{8,0},{9,1},... | collective-permute-start | bytes 98312 | tf_op jit(solution)/shard_map/ppermute | solution.py:362
  57.5 12.5 %copy-start.3 = (bf16[3,2,64,64]{3,2,1,0:T(8,128)(2,1)S(1)}, bf16[3,2,64,64]{3,2,1,0:T(8,128)(2,1)}, u32[]{:S(2)}) copy-start(bf16[3,2,64,64]{3,2,1,0:T(8,128)(2,1)} %param.14) | copy-start | bytes 147460
  58.8 22.1 %copy-start.1 = (bf16[8,8,128,128]{3,1,2,0:T(8,128)(2,1)}, bf16[8,8,128,128]{3,1,2,0:T(8,128)(2,1)S(1)}, u32[]{:S(2)}) copy-start(bf16[8,8,128,128]{3,1,2,0:T(8,128)(2,1)S(1)} %copy.41) | copy-start | bytes 6291460
  61.5 50.9 %collective-permute-start.4 = (bf16[64,16384]{1,0:T(8,128)(2,1)S(1)}, bf16[64,16384]{1,0:T(8,128)(2,1)}, u32[]{:S(2)}, u32[]{:S(2)}) collective-permute-start(bf16[64,16384]{1,0:T(8,128)(2,1)S(1)} %bitcast.33), channel_id=1, source_target_pairs={{0,1},{1,2},{2,3},{3,4},{4,5},{5,6},{6,7},{7,8},{8,9},{9,10},{10,1... | collective-permute-start | bytes 6291464 | tf_op jit(solution)/shard_map/ppermute | solution.py:388
  67.0 48.4 %collective-permute-start.5 = (bf16[64,16384]{1,0:T(8,128)(2,1)S(1)}, bf16[64,16384]{1,0:T(8,128)(2,1)}, u32[]{:S(2)}, u32[]{:S(2)}) collective-permute-start(bf16[64,16384]{1,0:T(8,128)(2,1)S(1)} %bitcast.34), channel_id=1, source_target_pairs={{1,0},{2,1},{3,2},{4,3},{5,4},{6,5},{7,6},{8,7},{9,8},{10,9},{11,1... | collective-permute-start | bytes 6291464 | tf_op jit(solution)/shard_map/ppermute | solution.py:389
